TPU v7x, 128 devices: a whole 4x4x4 slice. The times are simulated.
128 devices in a mesh: row: 8 (over x, core), col: 4 (over z), depth: 4 (over y).
Axes of the slice: x: 4, y: 4, z: 4, core: 2. Of those that a mesh axis runs over, the one named last changes fastest.
Arguments:
- tokens: bfloat16 [1024, 8192], P(('col', 'depth'), 'row'), may hold values from -6 to 6
- gate_weight: bfloat16 [8192, 14336], P('row', ('col', 'depth')), may hold values from -0.109375 to 0.109375
- up_weight: bfloat16 [8192, 14336], P('row', ('col', 'depth')), may hold values from -0.109375 to 0.109375
- down_weight: bfloat16 [14336, 8192], P(('col', 'depth'), 'row'), may hold values from -0.078125 to 0.078125
- gate_mask: int32 [64, 112], P('row', ('col', 'depth')), may hold values 0 or 1
- up_mask: int32 [64, 112], P('row', ('col', 'depth')), may hold values 0 or 1
- down_mask: int32 [112, 64], P(('col', 'depth'), 'row'), may hold values 0 or 1
- grad_out: bfloat16 [1024, 8192], P(('col', 'depth'), 'row'), may hold values from -1.5 to 1.5
Outputs:
- mixed: bfloat16 [1024, 8192], P(('col', 'depth'), 'row')
- grad_tokens: bfloat16 [1024, 8192], P(('col', 'depth'), 'row')
- grad_gate_weight: bfloat16 [8192, 14336], P('row', ('col', 'depth'))
- grad_up_weight: bfloat16 [8192, 14336], P('row', ('col', 'depth'))
- grad_down_weight: bfloat16 [14336, 8192], P(('col', 'depth'), 'row')
Inputs may be any that keep to these rules, and one draw needn't show every extreme that they name: `gate_mask`: 1 keeps the 128 x 128 block of the gate projection, 0 zeroes it. `up_mask`: 1 keeps the 128 x 128 block of the up projection, 0 zeroes it. `down_mask`: 1 keeps the 128 x 128 block of the down projection, 0 zeroes it.
All inputs are finite; a program needn't handle non-finite values.
Results may differ from a plain program's by a relative error of at most 0.015.
Values may be sent and summed in bfloat16 or wider, within the bound.
No kernel may reach another device: no remote copies, remote signals or barrier semaphores. Data moves between devices by JAX's collectives and lax.ppermute only.
A program may use at most 128 MiB of HBM per device.

v0:
```python
import jax
import jax.numpy as jnp
from jax import lax
from jax.sharding import PartitionSpec as P

BLK = 128


def expand(mask):
    return jnp.repeat(jnp.repeat(mask, BLK, axis=0), BLK, axis=1) > 0


def swiglu(sums):
    width = sums.shape[1] // 2
    gate = sums[:, :width]
    up = sums[:, width:]
    sig = jax.nn.sigmoid(gate)
    return (gate * sig * up).astype(jnp.bfloat16)


def swiglu_back(sums, grad_act):
    width = sums.shape[1] // 2
    gate = sums[:, :width]
    up = sums[:, width:]
    sig = jax.nn.sigmoid(gate)
    grad_gate = grad_act * up * sig * (1.0 + gate * (1.0 - sig))
    grad_up = grad_act * gate * sig
    return jnp.concatenate([grad_gate, grad_up], axis=1).astype(jnp.bfloat16)


def row_sums(term, rows):
    return lax.psum_scatter(
        term(jnp.int32(0), lax.axis_size("row") * rows), "row", scatter_dimension=0, tiled=True
    )


def row_gather(block):
    return lax.all_gather(block, "row", axis=0, tiled=True)


def group_sums(term, rows):
    return lax.psum_scatter(
        term(jnp.int32(0), rows * lax.axis_size(("col", "depth"))).astype(jnp.bfloat16),
        ("col", "depth"),
        scatter_dimension=0,
        tiled=True,
    ).astype(jnp.float32)


def local(tokens, gate_weight, up_weight, down_weight, gate_mask, up_mask, down_mask, grad_out):
    zero_value = jnp.zeros((), jnp.bfloat16)
    keep_gate = expand(gate_mask)
    keep_up = expand(up_mask)
    keep_down = expand(down_mask)
    w_both = jnp.concatenate(
        [jnp.where(keep_gate, gate_weight, zero_value), jnp.where(keep_up, up_weight, zero_value)],
        axis=1,
    )
    w_down = jnp.where(keep_down, down_weight, zero_value)
    x_all, grad_all = (
        lax.all_gather(tokens, ("col", "depth"), axis=0, tiled=True),
        lax.all_gather(grad_out, ("col", "depth"), axis=0, tiled=True),
    )
    total = x_all.shape[0]
    split_rows = total // lax.axis_size("row")
    own_rows = tokens.shape[0]
    inner = (((0,), (0,)), ((), ()))
    outer = (((1,), (1,)), ((), ()))

    def hidden_term(start, count):
        return jnp.dot(x_all, w_both, preferred_element_type=jnp.float32)

    def act_term(start, count):
        return lax.dot_general(grad_all, w_down, outer, preferred_element_type=jnp.float32)

    sums = row_sums(hidden_term, split_rows)
    act_all = row_gather(swiglu(sums))

    def out_term(start, count):
        return jnp.dot(act_all, w_down, preferred_element_type=jnp.float32)

    mixed = group_sums(out_term, own_rows).astype(jnp.bfloat16)
    grad_down = lax.dot_general(act_all, grad_all, inner, preferred_element_type=jnp.float32)
    grad_down_weight = jnp.where(keep_down, grad_down, jnp.float32(0.0)).astype(jnp.bfloat16)
    grad_act = row_sums(act_term, split_rows)
    grads_all = row_gather(swiglu_back(sums, grad_act))
    grad_both = lax.dot_general(x_all, grads_all, inner, preferred_element_type=jnp.float32)
    width = grad_both.shape[1] // 2
    grad_gate_weight = jnp.where(keep_gate, grad_both[:, :width], jnp.float32(0.0)).astype(
        jnp.bfloat16
    )
    grad_up_weight = jnp.where(keep_up, grad_both[:, width:], jnp.float32(0.0)).astype(jnp.bfloat16)

    def input_term(start, count):
        return lax.dot_general(grads_all, w_both, outer, preferred_element_type=jnp.float32)

    grad_tokens = group_sums(input_term, own_rows).astype(jnp.bfloat16)
    return (mixed, grad_tokens, grad_gate_weight, grad_up_weight, grad_down_weight)


def solution(mesh):
    return jax.shard_map(
        local,
        mesh=mesh,
        in_specs=(
            P(("col", "depth"), "row"),
            P("row", ("col", "depth")),
            P("row", ("col", "depth")),
            P(("col", "depth"), "row"),
            P("row", ("col", "depth")),
            P("row", ("col", "depth")),
            P(("col", "depth"), "row"),
            P(("col", "depth"), "row"),
        ),
        out_specs=(
            P(("col", "depth"), "row"),
            P(("col", "depth"), "row"),
            P("row", ("col", "depth")),
            P("row", ("col", "depth")),
            P(("col", "depth"), "row"),
        ),
        check_vma=False,
    )
```

profile of v0, /device:TPU:1, one launch (start us, length us, event | category | flops | bytes accessed | tf_op | source)
XLA Modules:
  0.0 420.3 jit_solution(67889986307446359)
XLA Ops:
  7.2 0.0 all-gather.9.cloned.1.call-start
  7.2 0.7 all-gather.9.cloned.1.call-update
  7.9 0.0 all-gather.5.cloned.1.call-start
  7.9 0.7 all-gather.5.cloned.1.call-update
  8.6 0.0 reduce-scatter.9.cloned.1.call-start
  8.7 0.7 broadcast_compare_fusion
  9.4 47.5 %all-gather.9.cloned.1.call-done = bf16[1024,1024]{1,0:T(8,128)(2,1)} async-done(((bf16[64,1024]{1,0:T(8,128)(2,1)}), bf16[1024,1024]{1,0:T(8,128)(2,1)}) %all-gather.9.cloned.1.call-update) | async-done | bytes 2097168 | tf_op jit(solution)/shard_map/all_gather | solution.py:62
  56.9 2.8 broadcast_in_dim.42
  59.7 6.2 %convolution_bitcast_fusion.2 = f32[1024,896]{0,1:T(8,128)} fusion(bf16[1024,1024]{1,0:T(8,128)(2,1)} %all-gather.9.cloned.1.call-done, bf16[896,1024]{1,0:T(8,128)(2,1)} %param.11, pred[112,8,8,128]{3,2,1,0:T(8,128)(4,1)S(1)} %bitcast.45), kind=kOutput, calls=%fused_computation.12 | convolution fusion | flops 1879965696 | bytes 8519680 | tf_op jit(solution)/shard_map/dot_general | solution.py:74
  65.9 0.0 reduce-scatter.9.cloned.1.call-update
  65.9 0.0 reduce-scatter.5.cloned.1.call-start
  65.9 0.6 copy-done.1
  66.6 0.1 copy.15
  66.7 0.1 broadcast_bitcast_fusion
  66.7 0.0 copy-done.2
  66.8 0.1 copy.13
  66.9 0.1 broadcast_bitcast_fusion.1
  67.0 2.9 copy.14
  69.9 3.8 copy.16
  73.7 3.6 bitcast_select_fusion.1
  77.3 26.0 %all-gather.5.cloned.1.call-done = bf16[1024,1024]{1,0:T(8,128)(2,1)} async-done(((bf16[64,1024]{1,0:T(8,128)(2,1)}), bf16[1024,1024]{1,0:T(8,128)(2,1)}) %all-gather.5.cloned.1.call-update) | async-done | bytes 2097168 | tf_op jit(solution)/shard_map/all_gather | solution.py:61
  103.3 9.7 %convolution_bitcast_fusion.1 = f32[1024,1792]{0,1:T(8,128)} fusion(bf16[1024,1024]{1,0:T(8,128)(2,1)} %all-gather.5.cloned.1.call-done, bf16[1024,896]{0,1:T(8,128)(2,1)} %get-tuple-element.15, bf16[1024,896]{0,1:T(8,128)(2,1)} %get-tuple-element.16), kind=kOutput, calls=%fused_computation.5 | convolution fusion | flops 3765436416 | bytes 13107200 | tf_op jit(solution)/shard_map/dot_general | solution.py:71
  113.0 0.0 reduce-scatter.5.cloned.1.call-update
  113.0 0.0 all-gather.7.cloned.1.call-start
  113.1 27.4 %reduce-scatter.9.cloned.1.call-done = f32[128,896]{0,1:T(8,128)} async-done(((f32[1024,896]{0,1:T(8,128)}), f32[128,896]{0,1:T(8,128)}) %reduce-scatter.9.cloned.1.call-update) | async-done | bytes 458768 | tf_op jit(solution)/shard_map/reduce_scatter | solution.py:32
  140.4 51.1 %reduce-scatter.5.cloned.1.call-done = f32[128,1792]{0,1:T(8,128)} async-done(((f32[1024,1792]{0,1:T(8,128)}), f32[128,1792]{0,1:T(8,128)}) %reduce-scatter.5.cloned.1.call-update) | async-done | bytes 917520 | tf_op jit(solution)/shard_map/reduce_scatter | solution.py:32
  191.5 2.3 multiply_convert_fusion.1
  193.8 0.0 all-gather.7.cloned.1.call-update
  193.8 0.0 all-gather.11.cloned.1.call-start
  193.8 0.8 pad_maximum_fusion.5
  194.6 0.0 all-gather.11.cloned.1.call-update
  194.7 0.0 reduce-scatter.7.cloned.1.call-start
  194.7 25.6 %all-gather.7.cloned.1.call-done = bf16[1024,896]{0,1:T(8,128)(2,1)} async-done(((bf16[128,896]{0,1:T(8,128)(2,1)}), bf16[1024,896]{0,1:T(8,128)(2,1)}) %all-gather.7.cloned.1.call-update) | async-done | bytes 1835024 | tf_op jit(solution)/shard_map/all_gather | solution.py:38
  220.3 5.8 %convolution_convert_fusion = bf16[1024,1024]{1,0:T(8,128)(2,1)} fusion(bf16[1024,896]{0,1:T(8,128)(2,1)} %all-gather.7.cloned.1.call-done, bf16[896,1024]{1,0:T(8,128)(2,1)} %param.11, pred[112,8,8,128]{3,2,1,0:T(8,128)(4,1)S(1)} %bitcast.46), kind=kOutput, calls=%fused_computation.14 | convolution fusion | flops 1881014272 | bytes 6684672 | tf_op jit(solution)/shard_map/dot_general | solution.py:80
  226.2 0.0 reduce-scatter.7.cloned.1.call-update
  226.2 0.2 reduce-scatter.11.cloned.1.call-start
  226.4 30.3 %all-gather.11.cloned.1.call-done = bf16[1024,1792]{0,1:T(8,128)(2,1)} async-done(((bf16[128,1792]{0,1:T(8,128)(2,1)}), bf16[1024,1792]{0,1:T(8,128)(2,1)}) %all-gather.11.cloned.1.call-update) | async-done | bytes 3670032 | tf_op jit(solution)/shard_map/all_gather | solution.py:38
  256.7 0.0 copy-done
  256.7 8.0 %fusion.3 = bf16[1024,1024]{1,0:T(8,128)(2,1)} fusion(bf16[1024,1792]{0,1:T(8,128)(2,1)} %all-gather.11.cloned.1.call-done, bf16[1024,896]{0,1:T(8,128)(2,1)S(1)} %copy-done, bf16[1024,896]{0,1:T(8,128)(2,1)} %get-tuple-element.16), kind=kOutput, calls=%fused_computation.13 | convolution fusion | flops 3766484992 | bytes 9437184 | tf_op jit(solution)/shard_map/dot_general | solution.py:95
  264.7 0.0 reduce-scatter.11.cloned.1.call-update
  264.7 1.5 copy-done.5
  266.2 5.0 %select_convert_fusion = bf16[896,1024]{1,0:T(8,128)(2,1)} fusion(pred[112,8,8,128]{3,2,1,0:T(8,128)(4,1)S(1)} %bitcast.47, bf16[1024,896]{0,1:T(8,128)(2,1)S(1)} %copy-done.5, bf16[1024,1024]{1,0:T(8,128)(2,1)} %all-gather.9.cloned.1.call-done), kind=kOutput, calls=%fused_computation.9 | convolution fusion | flops 1880883200 | bytes 6684672 | tf_op jit(solution)/shard_map/dot_general | solution.py:83
  271.2 4.1 convolution_bitcast_fusion
  275.4 2.3 fusion.1
  277.7 3.8 copy.17
  281.5 2.4 copy.18
  284.0 51.0 %reduce-scatter.7.cloned.1.call-done = bf16[64,1024]{1,0:T(8,128)(2,1)} async-done(((bf16[1024,1024]{1,0:T(8,128)(2,1)}), bf16[64,1024]{1,0:T(8,128)(2,1)}) %reduce-scatter.7.cloned.1.call-update) | async-done | bytes 131088 | tf_op jit(solution)/shard_map/reduce_scatter | solution.py:42
  334.9 78.5 %reduce-scatter.11.cloned.1.call-done = bf16[64,1024]{1,0:T(8,128)(2,1)} async-done(((bf16[1024,1024]{1,0:T(8,128)(2,1)}), bf16[64,1024]{1,0:T(8,128)(2,1)}) %reduce-scatter.11.cloned.1.call-update) | async-done | bytes 131088 | tf_op jit(solution)/shard_map/reduce_scatter | solution.py:42
  (13 shorter events, 0.1 us)
Async XLA Ops:
  7.2 49.7 %all-gather.9.cloned.1.call-start = ((), (), s32[]{:S(2)}) async-start(), calls=%async_computation.8 | async-start | bytes 2228224 | tf_op jit(solution)/shard_map/all_gather | solution.py:62
  7.9 95.4 %all-gather.5.cloned.1.call-start = ((), (), s32[]{:S(2)}) async-start(), calls=%async_computation.4 | async-start | bytes 2228224 | tf_op jit(solution)/shard_map/all_gather | solution.py:61
  8.6 131.8 %reduce-scatter.9.cloned.1.call-start = ((), (), s32[]{:S(2)}) async-start(), calls=%async_computation.9 | async-start | bytes 4128768 | tf_op jit(solution)/shard_map/reduce_scatter | solution.py:32
  65.9 0.7 copy-start.1
  65.9 0.9 copy-start.2
  65.9 125.6 %reduce-scatter.5.cloned.1.call-start = ((), (), s32[]{:S(2)}) async-start(), calls=%async_computation.5 | async-start | bytes 8257536 | tf_op jit(solution)/shard_map/reduce_scatter | solution.py:32
  113.0 107.3 %all-gather.7.cloned.1.call-start = ((), (), s32[]{:S(2)}) async-start(), calls=%async_computation.6 | async-start | bytes 2064384 | tf_op jit(solution)/shard_map/all_gather | solution.py:38
  193.8 62.9 %all-gather.11.cloned.1.call-start = ((), (), s32[]{:S(2)}) async-start(), calls=%async_computation.10 | async-start | bytes 4128768 | tf_op jit(solution)/shard_map/all_gather | solution.py:38
  194.7 140.3 %reduce-scatter.7.cloned.1.call-start = ((), (), s32[]{:S(2)}) async-start(), calls=%async_computation.7 | async-start | bytes 2228224 | tf_op jit(solution)/shard_map/reduce_scatter | solution.py:42
  226.2 30.6 %copy-start = (bf16[1024,896]{0,1:T(8,128)(2,1)S(1)}, bf16[1024,896]{0,1:T(8,128)(2,1)}, u32[]{:S(2)}) copy-start(bf16[1024,896]{0,1:T(8,128)(2,1)} %get-tuple-element.15) | copy-start | bytes 5505028
  226.2 187.2 %reduce-scatter.11.cloned.1.call-start = ((), (), s32[]{:S(2)}) async-start(), calls=%async_computation.11 | async-start | bytes 2228224 | tf_op jit(solution)/shard_map/reduce_scatter | solution.py:42
  264.7 1.5 copy-start.5
  266.2 5.1 %copy-start.3 = (bf16[1024,1792]{0,1:T(8,128)(2,1)S(1)}, bf16[1024,1792]{0,1:T(8,128)(2,1)}, u32[]{:S(2)}) copy-start(bf16[1024,1792]{0,1:T(8,128)(2,1)} %all-gather.11.cloned.1.call-done) | copy-start | bytes 11010052
  266.2 5.1 %copy-start.4 = (bf16[1024,1024]{1,0:T(8,128)(2,1)S(1)}, bf16[1024,1024]{1,0:T(8,128)(2,1)}, u32[]{:S(2)}) copy-start(bf16[1024,1024]{1,0:T(8,128)(2,1)} %all-gather.5.cloned.1.call-done) | copy-start | bytes 6291460
Sparse Core Ops, SparseCore 0:
  10.1 46.6 all-gather.8
  59.0 44.2 all-gather.4
  105.7 34.6 reduce-scatter.8
  142.7 48.7 reduce-scatter.4
  193.9 26.3 all-gather.6
  222.4 34.2 all-gather.10
  260.5 74.3 reduce-scatter.6
  338.8 74.5 reduce-scatter.10
where the time goes:
time: 422 us; the launch traced here: 420 us
  waiting for transfers between devices  339 us (80%)
  matrix products  38.8 us (9%)
  local copies, waits for them, and re-layouts  18.2 us (4%)
  between operations  14.2 us (3%)
  other arithmetic  9.71 us (2%)
    reduce_scatter x2, waiting for transfers between devices, group_sums(): lax.psum_scatter(term(jnp.int32(0), rows * lax.axis_size(('col', 'depth')...  129 us
    reduce_scatter x2, waiting for transfers between devices, row_sums(): lax.psum_scatter(term(jnp.int32(0), lax.axis_size('row') * rows), 'row',...  78.5 us
    all_gather x2, waiting for transfers between devices, row_gather(): return lax.all_gather(block, 'row', axis=0, tiled=True)  55.9 us
    all_gather x1, waiting for transfers between devices, local(): lax.all_gather(grad_out, ('col', 'depth'), axis=0, tiled=True)  47.5 us
    all_gather x1, waiting for transfers between devices, local(): lax.all_gather(tokens, ('col', 'depth'), axis=0, tiled=True)  26 us
    unnamed x20, local copies, waits for them, and re-layouts  15.2 us
    dot_general x1, matrix products, hidden_term(): return jnp.dot(x_all, w_both, preferred_element_type=jnp.float32)  9.67 us
  transfers between devices with their start and end apart: 8, of which 8 were waited for; matrix products, arithmetic and copies ran while one was open for 15% of the time, Pallas kernels for 0%

commit v1 on v0

--- a/solution.py
+++ b/solution.py
@@ -39,12 +39,17 @@
 
 
 def group_sums(term, rows):
-    return lax.psum_scatter(
-        term(jnp.int32(0), rows * lax.axis_size(("col", "depth"))).astype(jnp.bfloat16),
-        ("col", "depth"),
-        scatter_dimension=0,
-        tiled=True,
-    ).astype(jnp.float32)
+    parts = lax.axis_size(("col", "depth"))
+    full = term(jnp.int32(0), rows * parts).astype(jnp.bfloat16)
+    pieces = lax.all_to_all(full.reshape((parts, rows) + full.shape[1:]), ("col", "depth"), 0, 0)
+    return jnp.sum(pieces.astype(jnp.float32), axis=0)
+
+
+def group_gather(block):
+    parts = lax.axis_size(("col", "depth"))
+    copies = jnp.broadcast_to(block[None], (parts,) + block.shape)
+    pieces = lax.all_to_all(copies, ("col", "depth"), 0, 0)
+    return pieces.reshape((parts * block.shape[0],) + block.shape[1:])
 
 
 def local(tokens, gate_weight, up_weight, down_weight, gate_mask, up_mask, down_mask, grad_out):
@@ -57,10 +62,9 @@
         axis=1,
     )
     w_down = jnp.where(keep_down, down_weight, zero_value)
-    x_all, grad_all = (
-        lax.all_gather(tokens, ("col", "depth"), axis=0, tiled=True),
-        lax.all_gather(grad_out, ("col", "depth"), axis=0, tiled=True),
-    )
+    both_all = group_gather(jnp.concatenate([tokens, grad_out], axis=1))
+    x_all = both_all[:, : tokens.shape[1]]
+    grad_all = both_all[:, tokens.shape[1] :]
     total = x_all.shape[0]
     split_rows = total // lax.axis_size("row")
     own_rows = tokens.shape[0]

time: 422 us -> 295 us (0.70)
  waiting for transfers between devices: 339 us -> 180 us
  starting transfers between devices: 0.5 us -> 20.1 us
  local copies, waits for them, and re-layouts: 18.2 us -> 24 us
    reduce_scatter x2 -> x0, waiting for transfers between devices: 129 us -> none  [group_sums(): lax.psum_scatter(term(jnp.int32(0), rows * lax.axis_size(('col', 'depth')...]
    all_gather x2 -> x0, waiting for transfers between devices: 73.5 us -> none  [the longest x1 47.5 us: local(): lax.all_gather(grad_out, ('col', 'depth'), axis=0, tiled=True)]
    all_to_all x0 -> x3, waiting for transfers between devices: none -> 71.1 us  [the longest x1 62.4 us: group_gather(): pieces = lax.all_to_all(copies, ('col', 'depth'), 0, 0)]
    all_to_all x0 -> x3, starting transfers between devices: none -> 19.9 us  [the longest x2 11.1 us: group_sums(): lax.all_to_all(full.reshape((parts, rows) + full.shape[1:]), ('col', 'dep...]
    reduce_scatter x2, waiting for transfers between devices: 78.5 us -> 65.4 us  [row_sums(): lax.psum_scatter(term(jnp.int32(0), lax.axis_size('row') * rows), 'row',...]
    all_gather x2, waiting for transfers between devices: 55.9 us -> 43.8 us  [row_gather(): return lax.all_gather(block, 'row', axis=0, tiled=True)]
    gt x2 -> x4, local copies, waits for them, and re-layouts: 0.2 us -> 7.04 us  [expand(): return jnp.repeat(jnp.repeat(mask, BLK, axis=0), BLK, axis=1) > 0]
    unnamed x20, local copies, waits for them, and re-layouts: 15.2 us -> 9.3 us
  transfers between devices with their start and end apart: 8 -> 7, of which waited for: 8 -> 7; matrix products, arithmetic and copies ran while one was open for 15% -> 20% of each run, Pallas kernels for 0% -> 0%
where the time goes in v1:
time: 295 us; the launch traced here: 293 us
  waiting for transfers between devices  180 us (61%)
  matrix products  42.2 us (14%)
  local copies, waits for them, and re-layouts  24 us (8%)
  starting transfers between devices  20.1 us (7%)
  between operations  13.9 us (5%)
  other arithmetic  12.6 us (4%)
    reduce_scatter x2, waiting for transfers between devices, row_sums(): lax.psum_scatter(term(jnp.int32(0), lax.axis_size('row') * rows), 'row',...  65.4 us
    all_to_all x1, waiting for transfers between devices, group_gather(): pieces = lax.all_to_all(copies, ('col', 'depth'), 0, 0)  62.4 us
    all_gather x2, waiting for transfers between devices, row_gather(): return lax.all_gather(block, 'row', axis=0, tiled=True)  43.8 us
    all_to_all x2, starting transfers between devices, group_sums(): lax.all_to_all(full.reshape((parts, rows) + full.shape[1:]), ('col', 'dep...  11.1 us
    unnamed x20, local copies, waits for them, and re-layouts  9.3 us
    all_to_all x1, starting transfers between devices, group_gather(): pieces = lax.all_to_all(copies, ('col', 'depth'), 0, 0)  8.77 us
    all_to_all x2, waiting for transfers between devices, group_sums(): lax.all_to_all(full.reshape((parts, rows) + full.shape[1:]), ('col', 'dep...  8.68 us
    dot_general x1, matrix products, hidden_term(): return jnp.dot(x_all, w_both, preferred_element_type=jnp.float32)  8.54 us
  transfers between devices with their start and end apart: 7, of which 7 were waited for; matrix products, arithmetic and copies ran while one was open for 20% of the time, Pallas kernels for 0%

profile of v1, /device:TPU:1, one launch (start us, length us, event | category | flops | bytes accessed | tf_op | source)
XLA Modules:
  0.0 293.1 jit_solution(7494494642032948292)
XLA Ops:
  7.2 1.0 pad_maximum_fusion.6
  8.2 2.5 broadcast_in_dim.42
  10.7 8.8 %all-to-all-start = ((bf16[16,64,2048]{2,1,0:T(8,128)(2,1)}), bf16[16,64,2048]{2,1,0:T(8,128)(2,1)}, u32[]{:S(2)}, u32[]{:S(2)}) async-start(bf16[16,64,2048]{2,1,0:T(8,128)(2,1)} %broadcast_in_dim.42), calls=%async_computation | async-start | bytes 8388608 | tf_op jit(solution)/shard_map/all_to_all | solution.py:51
  19.4 0.0 reduce-scatter.5.cloned.1.call-start
  19.5 62.4 %all-to-all-done = bf16[16,64,2048]{2,1,0:T(8,128)(2,1)} async-done(((bf16[16,64,2048]{2,1,0:T(8,128)(2,1)}), bf16[16,64,2048]{2,1,0:T(8,128)(2,1)}, u32[]{:S(2)}, u32[]{:S(2)}) %all-to-all-start) | async-done | bytes 4194336 | tf_op jit(solution)/shard_map/all_to_all | solution.py:51
  81.9 2.8 broadcast_in_dim.49
  84.7 0.0 copy-start.3
  84.7 6.7 %fusion.7 = f32[1024,896]{1,0:T(8,128)} fusion(bf16[1024,2048]{1,0:T(8,128)(2,1)} %bitcast, bf16[896,1024]{1,0:T(8,128)(2,1)} %param.11, pred[112,8,8,128]{3,2,1,0:T(8,128)(4,1)S(1)} %bitcast.36), kind=kOutput, calls=%fused_computation.13 | convolution fusion | flops 1879965696 | bytes 8519680 | tf_op jit(solution)/shard_map/dot_general | solution.py:78
  91.5 0.0 reduce-scatter.5.cloned.1.call-update
  91.5 0.0 reduce-scatter.3.cloned.1.call-start
  91.6 0.6 copy-done.5
  92.2 0.1 copy.15
  92.3 0.1 broadcast_bitcast_fusion
  92.4 0.1 copy.13
  92.5 0.1 broadcast_bitcast_fusion.1
  92.6 2.9 copy.14
  95.5 3.8 %copy.16 = bf16[1024,896]{0,1:T(8,128)(2,1)} copy(bf16[1024,896]{1,0:T(8,128)(2,1)} %param.10) | data formatting | bytes 3670016 | tf_op args[2]
  99.3 1.8 bitcast_select_fusion.1
  101.1 0.0 copy-start.1
  101.1 1.2 copy-done.1
  102.3 0.6 copy-done.2
  102.9 8.5 %fusion.3 = f32[1024,1792]{1,0:T(8,128)} fusion(bf16[1024,896]{0,1:T(8,128)(2,1)S(1)} %get-tuple-element.10, bf16[1024,896]{0,1:T(8,128)(2,1)S(1)} %get-tuple-element.11, bf16[1024,2048]{1,0:T(8,128)(2,1)} %bitcast), kind=kOutput, calls=%fused_computation.8 | convolution fusion | flops 3765436416 | bytes 13107200 | tf_op jit(solution)/shard_map/dot_general | solution.py:75
  111.5 0.0 reduce-scatter.3.cloned.1.call-update
  111.5 0.0 all-gather.3.cloned.1.call-start
  111.5 14.1 %reduce-scatter.5.cloned.1.call-done = f32[128,896]{1,0:T(8,128)} async-done(((f32[1024,896]{1,0:T(8,128)}), f32[128,896]{1,0:T(8,128)}) %reduce-scatter.5.cloned.1.call-update) | async-done | bytes 458768 | tf_op jit(solution)/shard_map/reduce_scatter | solution.py:32
  125.7 51.2 %reduce-scatter.3.cloned.1.call-done = f32[128,1792]{1,0:T(8,128)} async-done(((f32[1024,1792]{1,0:T(8,128)}), f32[128,1792]{1,0:T(8,128)}) %reduce-scatter.3.cloned.1.call-update) | async-done | bytes 917520 | tf_op jit(solution)/shard_map/reduce_scatter | solution.py:32
  176.9 2.2 multiply_convert_fusion.1
  179.2 0.0 all-gather.3.cloned.1.call-update
  179.2 0.0 all-gather.5.cloned.1.call-start
  179.2 0.8 pad_maximum_fusion.5
  180.1 0.0 all-gather.5.cloned.1.call-update
  180.1 24.6 %all-gather.3.cloned.1.call-done = bf16[1024,896]{1,0:T(8,128)(2,1)} async-done(((bf16[128,896]{1,0:T(8,128)(2,1)}), bf16[1024,896]{1,0:T(8,128)(2,1)}) %all-gather.3.cloned.1.call-update) | async-done | bytes 1835024 | tf_op jit(solution)/shard_map/all_gather | solution.py:38
  204.7 5.9 %convolution_convert_fusion = bf16[1024,1024]{1,0:T(8,128)(2,1)} fusion(bf16[1024,896]{1,0:T(8,128)(2,1)} %all-gather.3.cloned.1.call-done, bf16[896,1024]{1,0:T(8,128)(2,1)} %param.11, pred[112,8,8,128]{3,2,1,0:T(8,128)(4,1)S(1)} %bitcast.37), kind=kOutput, calls=%fused_computation.10 | convolution fusion | flops 1881014272 | bytes 6684672 | tf_op jit(solution)/shard_map/dot_general | solution.py:84
  210.6 6.7 %all-to-all-start.1 = ((bf16[16,64,1024]{2,1,0:T(8,128)(2,1)}), bf16[16,64,1024]{2,1,0:T(8,128)(2,1)S(1)}, u32[]{:S(2)}, u32[]{:S(2)}) async-start(bf16[16,64,1024]{2,1,0:T(8,128)(2,1)} %bitcast.35), calls=%async_computation.2 | async-start | bytes 4194304 | tf_op jit(solution)/shard_map/all_to_all | solution.py:44
  217.3 19.1 %all-gather.5.cloned.1.call-done = bf16[1024,1792]{1,0:T(8,128)(2,1)} async-done(((bf16[128,1792]{1,0:T(8,128)(2,1)}), bf16[1024,1792]{1,0:T(8,128)(2,1)}) %all-gather.5.cloned.1.call-update) | async-done | bytes 3670032 | tf_op jit(solution)/shard_map/all_gather | solution.py:38
  236.4 8.4 %fusion.4 = bf16[1024,1024]{1,0:T(8,128)(2,1)} fusion(bf16[1024,1792]{1,0:T(8,128)(2,1)} %all-gather.5.cloned.1.call-done, bf16[1024,896]{0,1:T(8,128)(2,1)} %copy-done.1, bf16[1024,896]{0,1:T(8,128)(2,1)} %copy-done.2), kind=kOutput, calls=%fused_computation.9 | convolution fusion | flops 3766484992 | bytes 9437184 | tf_op jit(solution)/shard_map/dot_general | solution.py:99
  244.9 5.0 %all-to-all-done.1 = bf16[16,64,1024]{2,1,0:T(8,128)(2,1)S(1)} async-done(((bf16[16,64,1024]{2,1,0:T(8,128)(2,1)}), bf16[16,64,1024]{2,1,0:T(8,128)(2,1)S(1)}, u32[]{:S(2)}, u32[]{:S(2)}) %all-to-all-start.1) | async-done | bytes 2097184 | tf_op jit(solution)/shard_map/all_to_all | solution.py:44
  249.9 4.4 %all-to-all-start.2 = ((bf16[16,64,1024]{2,1,0:T(8,128)(2,1)}), bf16[16,64,1024]{2,1,0:T(8,128)(2,1)}, u32[]{:S(2)}, u32[]{:S(2)}) async-start(bf16[16,64,1024]{2,1,0:T(8,128)(2,1)} %bitcast.34), calls=%async_computation.4 | async-start | bytes 4194304 | tf_op jit(solution)/shard_map/all_to_all | solution.py:44
  254.3 1.2 broadcast_in_dim.44
  255.5 3.2 %copy.17 = pred[1024,896]{1,0:T(8,128)(4,1)S(1)} copy(pred[1024,896]{0,1:T(8,128)(4,1)} %bitcast.32) | data formatting | bytes 1835008 | tf_op jit(solution)/shard_map/gt | solution.py:10
  258.8 1.2 broadcast_in_dim.47
  259.9 3.6 %copy.18 = pred[1024,896]{1,0:T(8,128)(4,1)} copy(pred[1024,896]{0,1:T(8,128)(4,1)} %bitcast.33) | data formatting | bytes 1835008 | tf_op jit(solution)/shard_map/gt | solution.py:10
  263.5 5.8 %select_convert_fusion = bf16[896,1024]{1,0:T(8,128)(2,1)} fusion(pred[112,8,8,128]{3,2,1,0:T(8,128)(4,1)} %bitcast.38, bf16[1024,896]{1,0:T(8,128)(2,1)} %all-gather.3.cloned.1.call-done, bf16[1024,2048]{1,0:T(8,128)(2,1)} %bitcast), kind=kOutput, calls=%fused_computation.5 | convolution fusion | flops 1880883200 | bytes 6684672 | tf_op jit(solution)/shard_map/dot_general | solution.py:87
  269.4 1.1 reduce_sum.24
  270.4 6.8 %fusion.9 = bf16[1024,1792]{1,0:T(8,128)(2,1)S(1)} fusion(bf16[1024,1792]{1,0:T(8,128)(2,1)} %all-gather.5.cloned.1.call-done, bf16[1024,2048]{1,0:T(8,128)(2,1)} %bitcast), kind=kOutput, calls=%fused_computation.15 | convolution fusion | flops 3758096384 | bytes 9437184 | tf_op jit(solution)/shard_map/dot_general | solution.py:91
  277.2 3.0 %fusion = (bf16[1024,896]{1,0:T(8,128)(2,1)}, bf16[1024,896]{1,0:T(8,128)(2,1)}) fusion(pred[1024,896]{1,0:T(8,128)(4,1)S(1)} %copy-done, bf16[1024,1792]{1,0:T(8,128)(2,1)S(1)} %fusion.9, pred[1024,896]{1,0:T(8,128)(4,1)S(1)} %copy.17), kind=kLoop, calls=%fused_computation.1 | loop fusion | flops 1835008 | bytes 9175040 | tf_op jit(solution)/shard_map/convert_element_type | solution.py:96
  280.2 3.7 %all-to-all-done.2 = bf16[16,64,1024]{2,1,0:T(8,128)(2,1)} async-done(((bf16[16,64,1024]{2,1,0:T(8,128)(2,1)}), bf16[16,64,1024]{2,1,0:T(8,128)(2,1)}, u32[]{:S(2)}, u32[]{:S(2)}) %all-to-all-start.2) | async-done | bytes 2097184 | tf_op jit(solution)/shard_map/all_to_all | solution.py:44
  283.9 2.7 reduce_sum.25
  (15 shorter events, 0.1 us)
Async XLA Ops:
  10.6 8.8 %copy-start.4 = (s32[7,8]{1,0:T(8,128)S(1)}, s32[7,8]{1,0:T(8,128)}, u32[]{:S(2)}) copy-start(s32[7,8]{1,0:T(8,128)} %param.14) | copy-start | bytes 676
  10.7 71.2 %all-to-all-start = ((bf16[16,64,2048]{2,1,0:T(8,128)(2,1)}), bf16[16,64,2048]{2,1,0:T(8,128)(2,1)}, u32[]{:S(2)}, u32[]{:S(2)}) async-start(bf16[16,64,2048]{2,1,0:T(8,128)(2,1)} %broadcast_in_dim.42), calls=%async_computation | async-start | bytes 8388608 | tf_op jit(solution)/shard_map/all_to_all | solution.py:51
  19.4 106.3 %reduce-scatter.5.cloned.1.call-start = ((), (), s32[]{:S(2)}) async-start(), calls=%async_computation.7 | async-start | bytes 4128768 | tf_op jit(solution)/shard_map/reduce_scatter | solution.py:32
  84.7 120.0 %copy-start.3 = (pred[896,8,128]{2,1,0:T(8,128)(4,1)}, pred[896,8,128]{2,1,0:T(8,128)(4,1)S(1)}, u32[]{:S(2)}) copy-start(pred[896,8,128]{2,1,0:T(8,128)(4,1)S(1)} %broadcast_in_dim.49) | copy-start | bytes 2752516
  91.5 0.7 copy-start.5
  91.5 0.9 copy-start.6
  91.5 85.4 %reduce-scatter.3.cloned.1.call-start = ((), (), s32[]{:S(2)}) async-start(), calls=%async_computation.5 | async-start | bytes 8257536 | tf_op jit(solution)/shard_map/reduce_scatter | solution.py:32
  101.1 1.2 copy-start.1
  101.1 1.8 copy-start.2
  111.5 93.2 %all-gather.3.cloned.1.call-start = ((), (), s32[]{:S(2)}) async-start(), calls=%async_computation.6 | async-start | bytes 2064384 | tf_op jit(solution)/shard_map/all_gather | solution.py:38
  179.2 57.2 %all-gather.5.cloned.1.call-start = ((), (), s32[]{:S(2)}) async-start(), calls=%async_computation.8 | async-start | bytes 4128768 | tf_op jit(solution)/shard_map/all_gather | solution.py:38
  210.6 39.3 %all-to-all-start.1 = ((bf16[16,64,1024]{2,1,0:T(8,128)(2,1)}), bf16[16,64,1024]{2,1,0:T(8,128)(2,1)S(1)}, u32[]{:S(2)}, u32[]{:S(2)}) async-start(bf16[16,64,1024]{2,1,0:T(8,128)(2,1)} %bitcast.35), calls=%async_computation.2 | async-start | bytes 4194304 | tf_op jit(solution)/shard_map/all_to_all | solution.py:44
  249.9 34.0 %all-to-all-start.2 = ((bf16[16,64,1024]{2,1,0:T(8,128)(2,1)}), bf16[16,64,1024]{2,1,0:T(8,128)(2,1)}, u32[]{:S(2)}, u32[]{:S(2)}) async-start(bf16[16,64,1024]{2,1,0:T(8,128)(2,1)} %bitcast.34), calls=%async_computation.4 | async-start | bytes 4194304 | tf_op jit(solution)/shard_map/all_to_all | solution.py:44
  270.4 6.8 %copy-start = (pred[1024,896]{1,0:T(8,128)(4,1)S(1)}, pred[1024,896]{1,0:T(8,128)(4,1)}, u32[]{:S(2)}) copy-start(pred[1024,896]{1,0:T(8,128)(4,1)} %copy.18) | copy-start | bytes 2752516
Sparse Core Ops, SparseCore 0:
  91.6 33.9 reduce-scatter.4
  128.1 48.7 reduce-scatter.2
  179.3 25.3 all-gather.2
  206.3 30.1 all-gather.4

commit v2 on v1

--- a/solution.py
+++ b/solution.py
@@ -62,9 +62,8 @@
         axis=1,
     )
     w_down = jnp.where(keep_down, down_weight, zero_value)
-    both_all = group_gather(jnp.concatenate([tokens, grad_out], axis=1))
-    x_all = both_all[:, : tokens.shape[1]]
-    grad_all = both_all[:, tokens.shape[1] :]
+    grad_all = group_gather(grad_out)
+    x_all = group_gather(tokens)
     total = x_all.shape[0]
     split_rows = total // lax.axis_size("row")
     own_rows = tokens.shape[0]

time: 295 us -> 273 us (0.925)
  waiting for transfers between devices: 180 us -> 152 us
  starting transfers between devices: 20.1 us -> 26.7 us
    reduce_scatter x2, waiting for transfers between devices: 65.4 us -> 47.2 us  [row_sums(): lax.psum_scatter(term(jnp.int32(0), lax.axis_size('row') * rows), 'row',...]
    all_to_all x1 -> x2, waiting for transfers between devices: 62.4 us -> 48.2 us  [group_gather(): pieces = lax.all_to_all(copies, ('col', 'depth'), 0, 0)]
    unnamed x20, local copies, waits for them, and re-layouts: 9.3 us -> 16.7 us
    gt x4 -> x2, local copies, waits for them, and re-layouts: 7.04 us -> 0.19 us  [expand(): return jnp.repeat(jnp.repeat(mask, BLK, axis=0), BLK, axis=1) > 0]
    all_gather x2, waiting for transfers between devices: 43.8 us -> 49.5 us  [row_gather(): return lax.all_gather(block, 'row', axis=0, tiled=True)]
    all_to_all x1 -> x2, starting transfers between devices: 8.77 us -> 13.3 us  [group_gather(): pieces = lax.all_to_all(copies, ('col', 'depth'), 0, 0)]
  transfers between devices with their start and end apart: 7 -> 8, of which waited for: 7 -> 7; matrix products, arithmetic and copies ran while one was open for 20% -> 23% of each run, Pallas kernels for 0% -> 0%
where the time goes in v2:
time: 273 us; the launch traced here: 272 us
  waiting for transfers between devices  152 us (56%)
  matrix products  41.6 us (15%)
  starting transfers between devices  26.7 us (10%)
  local copies, waits for them, and re-layouts  23.9 us (9%)
  between operations  13.9 us (5%)
  other arithmetic  13.4 us (5%)
    all_gather x2, waiting for transfers between devices, row_gather(): return lax.all_gather(block, 'row', axis=0, tiled=True)  49.5 us
    all_to_all x2, waiting for transfers between devices, group_gather(): pieces = lax.all_to_all(copies, ('col', 'depth'), 0, 0)  48.2 us
    reduce_scatter x2, waiting for transfers between devices, row_sums(): lax.psum_scatter(term(jnp.int32(0), lax.axis_size('row') * rows), 'row',...  47.2 us
    unnamed x20, local copies, waits for them, and re-layouts  16.7 us
    all_to_all x2, starting transfers between devices, group_gather(): pieces = lax.all_to_all(copies, ('col', 'depth'), 0, 0)  13.3 us
    all_to_all x2, starting transfers between devices, group_sums(): lax.all_to_all(full.reshape((parts, rows) + full.shape[1:]), ('col', 'dep...  13.2 us
    dot_general x1, matrix products, hidden_term(): return jnp.dot(x_all, w_both, preferred_element_type=jnp.float32)  9.66 us
    dot_general x1, matrix products, input_term(): lax.dot_general(grads_all, w_both, outer, preferred_element_type=jnp.floa...  8.54 us
  transfers between devices with their start and end apart: 8, of which 7 were waited for; matrix products, arithmetic and copies ran while one was open for 23% of the time, Pallas kernels for 0%

profile of v2, /device:TPU:1, one launch (start us, length us, event | category | flops | bytes accessed | tf_op | source)
XLA Modules:
  0.0 271.9 jit_solution(10796436928851442409)
XLA Ops:
  7.2 2.5 broadcast_in_dim.57
  9.7 8.7 %all-to-all-start.2 = ((bf16[16,64,1024]{2,1,0:T(8,128)(2,1)}), bf16[16,64,1024]{2,1,0:T(8,128)(2,1)S(1)}, u32[]{:S(2)}, u32[]{:S(2)}) async-start(bf16[16,64,1024]{2,1,0:T(8,128)(2,1)} %broadcast_in_dim.57), calls=%async_computation.3 | async-start | bytes 4194304 | tf_op jit(solution)/shard_map/all_to_all | solution.py:51
  18.4 0.0 reduce-scatter.5.cloned.1.call-start
  18.5 0.0 copy-done.3
  18.5 30.9 %all-to-all-done.2 = bf16[16,64,1024]{2,1,0:T(8,128)(2,1)S(1)} async-done(((bf16[16,64,1024]{2,1,0:T(8,128)(2,1)}), bf16[16,64,1024]{2,1,0:T(8,128)(2,1)S(1)}, u32[]{:S(2)}, u32[]{:S(2)}) %all-to-all-start.2) | async-done | bytes 2097184 | tf_op jit(solution)/shard_map/all_to_all | solution.py:51
  49.4 2.8 %broadcast_in_dim.55 = pred[896,8,128]{2,1,0:T(8,128)(4,1)S(1)} broadcast(pred[896,8]{1,0:T(8,128)(4,1)S(1)} %bitcast.56), dimensions={0,1} | broadcast | bytes 924672 | tf_op jit(solution)/shard_map/broadcast_in_dim | solution.py:10
  52.2 5.5 %convolution_bitcast_fusion.2 = f32[1024,896]{0,1:T(8,128)} fusion(bf16[1024,1024]{1,0:T(8,128)(2,1)S(1)} %bitcast.49, bf16[896,1024]{1,0:T(8,128)(2,1)} %param.11, pred[112,8,8,128]{3,2,1,0:T(8,128)(4,1)S(1)} %bitcast.53), kind=kOutput, calls=%fused_computation.12 | convolution fusion | flops 1879965696 | bytes 8519680 | tf_op jit(solution)/shard_map/dot_general | solution.py:77
  57.7 0.0 copy-done.1
  57.7 0.0 reduce-scatter.5.cloned.1.call-update
  57.7 0.9 copy-done.2
  58.6 1.6 broadcast_in_dim.53
  60.2 4.6 %all-to-all-start = ((bf16[16,64,1024]{2,1,0:T(8,128)(2,1)}), bf16[16,64,1024]{2,1,0:T(8,128)(2,1)}, u32[]{:S(2)}, u32[]{:S(2)}) async-start(bf16[16,64,1024]{2,1,0:T(8,128)(2,1)} %broadcast_in_dim.53), calls=%async_computation | async-start | bytes 4194304 | tf_op jit(solution)/shard_map/all_to_all | solution.py:51
  64.8 0.0 reduce-scatter.3.cloned.1.call-start
  64.9 0.0 copy-done.4
  64.9 0.1 copy.15
  65.0 0.1 broadcast_bitcast_fusion
  65.1 0.1 copy.13
  65.2 0.1 broadcast_bitcast_fusion.1
  65.3 3.0 %copy.14 = bf16[1024,896]{0,1:T(8,128)(2,1)S(1)} copy(bf16[1024,896]{1,0:T(8,128)(2,1)} %param.9) | data formatting | bytes 3670016 | tf_op args[1]
  68.3 3.8 %copy.16 = bf16[1024,896]{0,1:T(8,128)(2,1)} copy(bf16[1024,896]{1,0:T(8,128)(2,1)} %param.10) | data formatting | bytes 3670016 | tf_op args[2]
  72.1 3.7 %bitcast_select_fusion.1 = (bf16[1024,896]{0,1:T(8,128)(2,1)}, bf16[1024,896]{0,1:T(8,128)(2,1)}) fusion(bf16[1024,896]{0,1:T(8,128)(2,1)} %copy.16, pred[1024,7]{0,1:T(8,128)(4,1)S(1)} %bitcast.57, bf16[1024,896]{0,1:T(8,128)(2,1)S(1)} %copy.14, pred[1024,7]{0,1:T(8,128)(4,1)S(1)} %bitcast.59), kind=kLoop, calls=%fused_computation.1 | loop fusion | flops 1835008 | bytes 7354368 | tf_op jit(solution)/shard_map/jit(_where)/select_n | solution.py:61
  75.7 17.3 %all-to-all-done = bf16[16,64,1024]{2,1,0:T(8,128)(2,1)} async-done(((bf16[16,64,1024]{2,1,0:T(8,128)(2,1)}), bf16[16,64,1024]{2,1,0:T(8,128)(2,1)}, u32[]{:S(2)}, u32[]{:S(2)}) %all-to-all-start) | async-done | bytes 2097184 | tf_op jit(solution)/shard_map/all_to_all | solution.py:51
  93.0 9.7 %convolution_bitcast_fusion.1 = f32[1024,1792]{0,1:T(8,128)} fusion(bf16[1024,1024]{1,0:T(8,128)(2,1)} %bitcast.2, bf16[1024,896]{0,1:T(8,128)(2,1)} %get-tuple-element.15, bf16[1024,896]{0,1:T(8,128)(2,1)} %get-tuple-element.16), kind=kOutput, calls=%fused_computation.5 | convolution fusion | flops 3765436416 | bytes 13107200 | tf_op jit(solution)/shard_map/dot_general | solution.py:74
  102.7 0.0 reduce-scatter.3.cloned.1.call-update
  102.7 0.0 all-gather.3.cloned.1.call-start
  102.7 0.0 reduce-scatter.5.cloned.1.call-done
  102.8 47.2 %reduce-scatter.3.cloned.1.call-done = f32[128,1792]{0,1:T(8,128)} async-done(((f32[1024,1792]{0,1:T(8,128)}), f32[128,1792]{0,1:T(8,128)}) %reduce-scatter.3.cloned.1.call-update) | async-done | bytes 917520 | tf_op jit(solution)/shard_map/reduce_scatter | solution.py:32
  149.9 2.3 multiply_convert_fusion.1
  152.2 0.0 all-gather.3.cloned.1.call-update
  152.2 0.0 all-gather.5.cloned.1.call-start
  152.3 0.8 pad_maximum_fusion.5
  153.1 0.0 all-gather.5.cloned.1.call-update
  153.1 25.7 %all-gather.3.cloned.1.call-done = bf16[1024,896]{0,1:T(8,128)(2,1)} async-done(((bf16[128,896]{0,1:T(8,128)(2,1)}), bf16[1024,896]{0,1:T(8,128)(2,1)}) %all-gather.3.cloned.1.call-update) | async-done | bytes 1835024 | tf_op jit(solution)/shard_map/all_gather | solution.py:38
  178.8 5.8 %convolution_convert_fusion = bf16[1024,1024]{1,0:T(8,128)(2,1)} fusion(bf16[1024,896]{0,1:T(8,128)(2,1)} %all-gather.3.cloned.1.call-done, bf16[896,1024]{1,0:T(8,128)(2,1)} %param.11, pred[112,8,8,128]{3,2,1,0:T(8,128)(4,1)S(1)} %bitcast.54), kind=kOutput, calls=%fused_computation.14 | convolution fusion | flops 1881014272 | bytes 6684672 | tf_op jit(solution)/shard_map/dot_general | solution.py:83
  184.5 6.7 %all-to-all-start.1 = ((bf16[16,64,1024]{2,1,0:T(8,128)(2,1)}), bf16[16,64,1024]{2,1,0:T(8,128)(2,1)S(1)}, u32[]{:S(2)}, u32[]{:S(2)}) async-start(bf16[16,64,1024]{2,1,0:T(8,128)(2,1)} %bitcast.52), calls=%async_computation.2 | async-start | bytes 4194304 | tf_op jit(solution)/shard_map/all_to_all | solution.py:44
  191.3 23.9 %all-gather.5.cloned.1.call-done = bf16[1024,1792]{0,1:T(8,128)(2,1)} async-done(((bf16[128,1792]{0,1:T(8,128)(2,1)}), bf16[1024,1792]{0,1:T(8,128)(2,1)}) %all-gather.5.cloned.1.call-update) | async-done | bytes 3670032 | tf_op jit(solution)/shard_map/all_gather | solution.py:38
  215.1 8.5 %fusion.3 = bf16[1024,1024]{1,0:T(8,128)(2,1)} fusion(bf16[1024,1792]{0,1:T(8,128)(2,1)} %all-gather.5.cloned.1.call-done, bf16[1024,896]{0,1:T(8,128)(2,1)} %get-tuple-element.15, bf16[1024,896]{0,1:T(8,128)(2,1)} %get-tuple-element.16), kind=kOutput, calls=%fused_computation.13 | convolution fusion | flops 3766484992 | bytes 9437184 | tf_op jit(solution)/shard_map/dot_general | solution.py:98
  223.7 0.2 all-to-all-done.1
  223.9 1.3 copy-done
  225.2 6.5 %all-to-all-start.3 = ((bf16[16,64,1024]{2,1,0:T(8,128)(2,1)}), bf16[16,64,1024]{2,1,0:T(8,128)(2,1)S(1)}, u32[]{:S(2)}, u32[]{:S(2)}) async-start(bf16[16,64,1024]{2,1,0:T(8,128)(2,1)} %bitcast.51), calls=%async_computation.5 | async-start | bytes 4194304 | tf_op jit(solution)/shard_map/all_to_all | solution.py:44
  231.7 5.5 %select_convert_fusion = bf16[896,1024]{1,0:T(8,128)(2,1)} fusion(pred[112,8,8,128]{3,2,1,0:T(8,128)(4,1)S(1)} %bitcast.55, bf16[1024,896]{0,1:T(8,128)(2,1)} %all-gather.3.cloned.1.call-done, bf16[1024,1024]{1,0:T(8,128)(2,1)} %bitcast.50), kind=kOutput, calls=%fused_computation.9 | convolution fusion | flops 1880883200 | bytes 6684672 | tf_op jit(solution)/shard_map/dot_general | solution.py:86
  237.2 2.7 reduce_sum.24
  239.8 6.7 %convolution_bitcast_fusion = bf16[1024,1792]{0,1:T(8,128)(2,1)S(1)} fusion(bf16[1024,1792]{0,1:T(8,128)(2,1)} %all-gather.5.cloned.1.call-done, bf16[1024,1024]{1,0:T(8,128)(2,1)} %bitcast.2), kind=kOutput, calls=%fused_computation.4 | convolution fusion | flops 3758096384 | bytes 9437184 | tf_op jit(solution)/shard_map/dot_general | solution.py:90
  246.5 2.9 %fusion.1 = (bf16[1024,896]{0,1:T(8,128)(2,1)}, bf16[1024,896]{0,1:T(8,128)(2,1)}) fusion(bf16[1024,1792]{0,1:T(8,128)(2,1)S(1)} %convolution_bitcast_fusion, pred[1024,7]{0,1:T(8,128)(4,1)S(1)} %bitcast.58, pred[1024,7]{0,1:T(8,128)(4,1)S(1)} %bitcast.60), kind=kLoop, calls=%fused_computation.7 | loop fusion | flops 1835008 | bytes 7354368 | tf_op jit(solution)/shard_map/convert_element_type | solution.py:95
  249.4 3.8 %copy.17 = bf16[1024,896]{1,0:T(8,128)(2,1)} copy(bf16[1024,896]{0,1:T(8,128)(2,1)} %get-tuple-element.11) | data formatting | bytes 3670016
  253.2 3.8 %copy.18 = bf16[1024,896]{1,0:T(8,128)(2,1)} copy(bf16[1024,896]{0,1:T(8,128)(2,1)} %get-tuple-element.10) | data formatting | bytes 3670016
  257.0 7.3 %all-to-all-done.3 = bf16[16,64,1024]{2,1,0:T(8,128)(2,1)S(1)} async-done(((bf16[16,64,1024]{2,1,0:T(8,128)(2,1)}), bf16[16,64,1024]{2,1,0:T(8,128)(2,1)S(1)}, u32[]{:S(2)}, u32[]{:S(2)}) %all-to-all-start.3) | async-done | bytes 2097184 | tf_op jit(solution)/shard_map/all_to_all | solution.py:44
  264.3 1.1 reduce_sum.25
  (13 shorter events, 0.1 us)
Async XLA Ops:
  9.7 8.8 %copy-start.3 = (s32[7,8]{1,0:T(8,128)S(1)}, s32[7,8]{1,0:T(8,128)}, u32[]{:S(2)}) copy-start(s32[7,8]{1,0:T(8,128)} %param.14) | copy-start | bytes 676
  9.7 39.7 %all-to-all-start.2 = ((bf16[16,64,1024]{2,1,0:T(8,128)(2,1)}), bf16[16,64,1024]{2,1,0:T(8,128)(2,1)S(1)}, u32[]{:S(2)}, u32[]{:S(2)}) async-start(bf16[16,64,1024]{2,1,0:T(8,128)(2,1)} %broadcast_in_dim.57), calls=%async_computation.3 | async-start | bytes 4194304 | tf_op jit(solution)/shard_map/all_to_all | solution.py:51
  18.4 84.3 %reduce-scatter.5.cloned.1.call-start = ((), (), s32[]{:S(2)}) async-start(), calls=%async_computation.8 | async-start | bytes 4128768 | tf_op jit(solution)/shard_map/reduce_scatter | solution.py:32
  49.4 8.4 %copy-start.1 = (bf16[16,64,1024]{2,1,0:T(8,128)(2,1)}, bf16[16,64,1024]{2,1,0:T(8,128)(2,1)S(1)}, u32[]{:S(2)}) copy-start(bf16[16,64,1024]{2,1,0:T(8,128)(2,1)S(1)} %all-to-all-done.2) | copy-start | bytes 6291460
  57.7 0.9 copy-start.2
  60.2 4.6 %copy-start.4 = (s32[8,7]{1,0:T(8,128)S(1)}, s32[8,7]{1,0:T(8,128)}, u32[]{:S(2)}) copy-start(s32[8,7]{1,0:T(8,128)} %param.13) | copy-start | bytes 676
  60.2 4.8 %copy-start.5 = (s32[8,7]{1,0:T(8,128)S(1)}, s32[8,7]{1,0:T(8,128)}, u32[]{:S(2)}) copy-start(s32[8,7]{1,0:T(8,128)} %param.12) | copy-start | bytes 676
  60.2 32.8 %all-to-all-start = ((bf16[16,64,1024]{2,1,0:T(8,128)(2,1)}), bf16[16,64,1024]{2,1,0:T(8,128)(2,1)}, u32[]{:S(2)}, u32[]{:S(2)}) async-start(bf16[16,64,1024]{2,1,0:T(8,128)(2,1)} %broadcast_in_dim.53), calls=%async_computation | async-start | bytes 4194304 | tf_op jit(solution)/shard_map/all_to_all | solution.py:51
  64.8 85.1 %reduce-scatter.3.cloned.1.call-start = ((), (), s32[]{:S(2)}) async-start(), calls=%async_computation.6 | async-start | bytes 8257536 | tf_op jit(solution)/shard_map/reduce_scatter | solution.py:32
  102.7 76.1 %all-gather.3.cloned.1.call-start = ((), (), s32[]{:S(2)}) async-start(), calls=%async_computation.7 | async-start | bytes 2064384 | tf_op jit(solution)/shard_map/all_gather | solution.py:38
  152.2 62.9 %all-gather.5.cloned.1.call-start = ((), (), s32[]{:S(2)}) async-start(), calls=%async_computation.9 | async-start | bytes 4128768 | tf_op jit(solution)/shard_map/all_gather | solution.py:38
  184.5 39.3 %all-to-all-start.1 = ((bf16[16,64,1024]{2,1,0:T(8,128)(2,1)}), bf16[16,64,1024]{2,1,0:T(8,128)(2,1)S(1)}, u32[]{:S(2)}, u32[]{:S(2)}) async-start(bf16[16,64,1024]{2,1,0:T(8,128)(2,1)} %bitcast.52), calls=%async_computation.2 | async-start | bytes 4194304 | tf_op jit(solution)/shard_map/all_to_all | solution.py:44
  223.9 1.3 copy-start
  225.2 39.2 %all-to-all-start.3 = ((bf16[16,64,1024]{2,1,0:T(8,128)(2,1)}), bf16[16,64,1024]{2,1,0:T(8,128)(2,1)S(1)}, u32[]{:S(2)}, u32[]{:S(2)}) async-start(bf16[16,64,1024]{2,1,0:T(8,128)(2,1)} %bitcast.51), calls=%async_computation.5 | async-start | bytes 4194304 | tf_op jit(solution)/shard_map/all_to_all | solution.py:44
Sparse Core Ops, SparseCore 0:
  57.9 33.3 reduce-scatter.4
  102.8 47.0 reduce-scatter.2
  152.4 26.3 all-gather.2
  180.9 34.2 all-gather.4

commit v3 on v2

v3 whole, which is shorter than its diff:
```python
import jax
import jax.numpy as jnp
from jax import lax
from jax.sharding import PartitionSpec as P

BLK = 128
CHUNKS = 2
GROUP = ("col", "depth")


def expand(mask):
    return jnp.repeat(jnp.repeat(mask, BLK, axis=0), BLK, axis=1) > 0


def swiglu(sums):
    width = sums.shape[1] // 2
    gate = sums[:, :width]
    up = sums[:, width:]
    sig = jax.nn.sigmoid(gate)
    return (gate * sig * up).astype(jnp.bfloat16)


def swiglu_back(sums, grad_act):
    width = sums.shape[1] // 2
    gate = sums[:, :width]
    up = sums[:, width:]
    sig = jax.nn.sigmoid(gate)
    grad_gate = grad_act * up * sig * (1.0 + gate * (1.0 - sig))
    grad_up = grad_act * gate * sig
    return jnp.concatenate([grad_gate, grad_up], axis=1).astype(jnp.bfloat16)


def row_sums(full):
    return lax.psum_scatter(full, "row", scatter_dimension=0, tiled=True)


def row_gather(block):
    return lax.all_gather(block, "row", axis=0, tiled=True)


def group_sums(full):
    parts = lax.axis_size(GROUP)
    rows = full.shape[0] // parts
    pieces = lax.all_to_all(
        full.astype(jnp.bfloat16).reshape((parts, rows) + full.shape[1:]), GROUP, 0, 0
    )
    return jnp.sum(pieces.astype(jnp.float32), axis=0)


def group_gather(block):
    parts = lax.axis_size(GROUP)
    copies = jnp.broadcast_to(block[None], (parts,) + block.shape)
    pieces = lax.all_to_all(copies, GROUP, 0, 0)
    return pieces.reshape((parts * block.shape[0],) + block.shape[1:])


def local(tokens, gate_weight, up_weight, down_weight, gate_mask, up_mask, down_mask, grad_out):
    zero_value = jnp.zeros((), jnp.bfloat16)
    keep_gate = expand(gate_mask)
    keep_up = expand(up_mask)
    keep_down = expand(down_mask)
    w_both = jnp.concatenate(
        [jnp.where(keep_gate, gate_weight, zero_value), jnp.where(keep_up, up_weight, zero_value)],
        axis=1,
    )
    w_down = jnp.where(keep_down, down_weight, zero_value)
    inner = (((0,), (0,)), ((), ()))
    outer = (((1,), (1,)), ((), ()))
    step = tokens.shape[0] // CHUNKS

    mixed_parts, input_parts = [], []
    grad_down = None
    grad_both = None
    for h in range(CHUNKS):
        grad_h = group_gather(grad_out[h * step : (h + 1) * step])
        x_h = group_gather(tokens[h * step : (h + 1) * step])
        grad_act = row_sums(lax.dot_general(grad_h, w_down, outer, preferred_element_type=jnp.float32))
        sums = row_sums(jnp.dot(x_h, w_both, preferred_element_type=jnp.float32))
        act_all = row_gather(swiglu(sums))
        grads_all = row_gather(swiglu_back(sums, grad_act))
        mixed_parts.append(group_sums(jnp.dot(act_all, w_down, preferred_element_type=jnp.float32)))
        down_term = lax.dot_general(act_all, grad_h, inner, preferred_element_type=jnp.float32)
        grad_down = down_term if grad_down is None else grad_down + down_term
        input_parts.append(
            group_sums(lax.dot_general(grads_all, w_both, outer, preferred_element_type=jnp.float32))
        )
        both_term = lax.dot_general(x_h, grads_all, inner, preferred_element_type=jnp.float32)
        grad_both = both_term if grad_both is None else grad_both + both_term

    mixed = jnp.concatenate(mixed_parts, axis=0).astype(jnp.bfloat16)
    grad_tokens = jnp.concatenate(input_parts, axis=0).astype(jnp.bfloat16)
    grad_down_weight = jnp.where(keep_down, grad_down, jnp.float32(0.0)).astype(jnp.bfloat16)
    width = grad_both.shape[1] // 2
    grad_gate_weight = jnp.where(keep_gate, grad_both[:, :width], jnp.float32(0.0)).astype(
        jnp.bfloat16
    )
    grad_up_weight = jnp.where(keep_up, grad_both[:, width:], jnp.float32(0.0)).astype(jnp.bfloat16)
    return (mixed, grad_tokens, grad_gate_weight, grad_up_weight, grad_down_weight)


def solution(mesh):
    return jax.shard_map(
        local,
        mesh=mesh,
        in_specs=(
            P(GROUP, "row"),
            P("row", GROUP),
            P("row", GROUP),
            P(GROUP, "row"),
            P("row", GROUP),
            P("row", GROUP),
            P(GROUP, "row"),
            P(GROUP, "row"),
        ),
        out_specs=(
            P(GROUP, "row"),
            P(GROUP, "row"),
            P("row", GROUP),
            P("row", GROUP),
            P(GROUP, "row"),
        ),
        check_vma=False,
    )
```

time: 273 us -> 309 us (1.13)
  blocking collectives: 0 us -> 71.3 us
  waiting for transfers between devices: 152 us -> 82.4 us
  local copies, waits for them, and re-layouts: 23.9 us -> 38 us
  starting transfers between devices: 26.7 us -> 35.6 us
  matrix products: 41.6 us -> 50.5 us
    all_gather x2, waiting for transfers between devices: 49.5 us -> 0.01 us  [row_gather(): return lax.all_gather(block, 'row', axis=0, tiled=True)]
    all_to_all x0 -> x2, blocking collectives: none -> 39.2 us  [group_gather(): pieces = lax.all_to_all(copies, GROUP, 0, 0)]
    all_gather x0 -> x2, blocking collectives: none -> 32.1 us  [row_gather(): return lax.all_gather(block, 'row', axis=0, tiled=True)]
    all_to_all x4 -> x6, waiting for transfers between devices: 55.6 us -> 30.8 us  [the longest x2 20.3 us: group_gather(): pieces = lax.all_to_all(copies, GROUP, 0, 0)]
    unnamed x20 -> x48, local copies, waits for them, and re-layouts: 16.7 us -> 31.6 us
    dot_general x6 -> x12, matrix products: 41.6 us -> 50.5 us  [the longest x2 12 us: local(): sums = row_sums(jnp.dot(x_h, w_both, preferred_element_type=jnp.float32))]
    all_to_all x4 -> x6, starting transfers between devices: 26.5 us -> 35.4 us  [the longest x4 22.6 us: group_sums(): lax.all_to_all(full.astype(jnp.bfloat16).reshape((parts, rows) + full.sha...]
    reduce_scatter x2 -> x4, waiting for transfers between devices: 47.2 us -> 51.5 us  [row_sums(): return lax.psum_scatter(full, 'row', scatter_dimension=0, tiled=True)]
  transfers between devices with their start and end apart: 8 -> 12, of which waited for: 7 -> 6; matrix products, arithmetic and copies ran while one was open for 23% -> 28% of each run, Pallas kernels for 0% -> 0%
where the time goes in v3:
time: 309 us; the launch traced here: 306 us
  waiting for transfers between devices  82.4 us (27%)
  blocking collectives  71.3 us (23%)
  matrix products  50.5 us (16%)
  local copies, waits for them, and re-layouts  38 us (12%)
  starting transfers between devices  35.6 us (12%)
  between operations  14.4 us (5%)
  other arithmetic  13.3 us (4%)
    reduce_scatter x4, waiting for transfers between devices, row_sums(): return lax.psum_scatter(full, 'row', scatter_dimension=0, tiled=True)  51.5 us
    all_to_all x2, blocking collectives, group_gather(): pieces = lax.all_to_all(copies, GROUP, 0, 0)  39.2 us
    all_gather x2, blocking collectives, row_gather(): return lax.all_gather(block, 'row', axis=0, tiled=True)  32.1 us
    unnamed x48, local copies, waits for them, and re-layouts  31.6 us
    all_to_all x4, starting transfers between devices, group_sums(): lax.all_to_all(full.astype(jnp.bfloat16).reshape((parts, rows) + full.sha...  22.6 us
    all_to_all x2, waiting for transfers between devices, group_gather(): pieces = lax.all_to_all(copies, GROUP, 0, 0)  20.3 us
    all_to_all x2, starting transfers between devices, group_gather(): pieces = lax.all_to_all(copies, GROUP, 0, 0)  12.8 us
    dot_general x2, matrix products, local(): sums = row_sums(jnp.dot(x_h, w_both, preferred_element_type=jnp.float32))  12 us
  transfers between devices with their start and end apart: 12, of which 6 were waited for; matrix products, arithmetic and copies ran while one was open for 28% of the time, Pallas kernels for 0%

profile of v3, /device:TPU:1, one launch (start us, length us, event | category | flops | bytes accessed | tf_op | source)
XLA Modules:
  0.0 305.6 jit_solution(9942141258547771238)
XLA Ops:
  8.1 1.1 broadcast_in_dim.70
  9.2 8.6 %all-to-all-start.4 = ((bf16[16,32,1024]{2,1,0:T(8,128)(2,1)}), bf16[16,32,1024]{2,1,0:T(8,128)(2,1)S(1)}, u32[]{:S(2)}, u32[]{:S(2)}) async-start(bf16[16,32,1024]{2,1,0:T(8,128)(2,1)} %broadcast_in_dim.70), calls=%async_computation.4 | async-start | bytes 2097152 | tf_op jit(solution)/shard_map/all_to_all | solution.py:53
  17.8 16.0 %all-to-all-done.4 = bf16[16,32,1024]{2,1,0:T(8,128)(2,1)S(1)} async-done(((bf16[16,32,1024]{2,1,0:T(8,128)(2,1)}), bf16[16,32,1024]{2,1,0:T(8,128)(2,1)S(1)}, u32[]{:S(2)}, u32[]{:S(2)}) %all-to-all-start.4) | async-done | bytes 1048608 | tf_op jit(solution)/shard_map/all_to_all | solution.py:53
  33.8 2.8 broadcast_in_dim.67
  36.6 0.9 copy-done.9
  37.6 2.7 convolution_bitcast_fusion.3
  40.3 1.8 copy.47
  43.0 1.1 broadcast_in_dim.65
  44.1 4.2 %all-to-all-start = ((bf16[16,32,1024]{2,1,0:T(8,128)(2,1)}), bf16[16,32,1024]{2,1,0:T(8,128)(2,1)S(1)}, u32[]{:S(2)}, u32[]{:S(2)}) async-start(bf16[16,32,1024]{2,1,0:T(8,128)(2,1)} %broadcast_in_dim.65), calls=%async_computation | async-start | bytes 2097152 | tf_op jit(solution)/shard_map/all_to_all | solution.py:53
  48.7 2.9 copy.30
  51.7 3.8 %copy.32 = bf16[1024,896]{0,1:T(8,128)(2,1)} copy(bf16[1024,896]{1,0:T(8,128)(2,1)} %param.10) | data formatting | bytes 3670016 | tf_op args[2]
  55.4 3.7 %bitcast_select_fusion.1 = (bf16[1024,896]{0,1:T(8,128)(2,1)}, bf16[1024,896]{0,1:T(8,128)(2,1)}) fusion(bf16[1024,896]{0,1:T(8,128)(2,1)} %copy.32, pred[1024,7]{0,1:T(8,128)(4,1)S(1)} %bitcast.86, bf16[1024,896]{0,1:T(8,128)(2,1)S(1)} %copy.30, pred[1024,7]{0,1:T(8,128)(4,1)S(1)} %bitcast.88), kind=kLoop, calls=%fused_computation.2 | loop fusion | flops 1835008 | bytes 7354368 | tf_op jit(solution)/shard_map/jit(_where)/select_n | solution.py:63
  59.1 4.3 %all-to-all-done = bf16[16,32,1024]{2,1,0:T(8,128)(2,1)S(1)} async-done(((bf16[16,32,1024]{2,1,0:T(8,128)(2,1)}), bf16[16,32,1024]{2,1,0:T(8,128)(2,1)S(1)}, u32[]{:S(2)}, u32[]{:S(2)}) %all-to-all-start) | async-done | bytes 1048608 | tf_op jit(solution)/shard_map/all_to_all | solution.py:53
  63.4 6.4 %convolution_bitcast_fusion.1 = f32[512,1792]{0,1:T(8,128)} fusion(bf16[512,1024]{1,0:T(8,128)(2,1)S(1)} %bitcast.73, bf16[1024,896]{0,1:T(8,128)(2,1)} %get-tuple-element.32, bf16[1024,896]{0,1:T(8,128)(2,1)} %get-tuple-element.33), kind=kOutput, calls=%fused_computation.11 | convolution fusion | flops 1886388224 | bytes 8388608 | tf_op jit(solution)/shard_map/dot_general | solution.py:78
  69.8 5.2 %copy.43 = f32[512,1792]{1,0:T(8,128)} copy(f32[512,1792]{0,1:T(8,128)} %convolution_bitcast_fusion.1) | data formatting | bytes 7340032
  75.2 20.6 %all_to_all.40 = bf16[16,32,1024]{2,1,0:T(8,128)(2,1)S(1)} all-to-all(bf16[16,32,1024]{2,1,0:T(8,128)(2,1)S(1)} %broadcast_in_dim.71), channel_id=1, replica_groups=mesh['row'=8,'col'=4,'depth'=4] {'col','depth'}, dimensions={0} | all-to-all | bytes 2097152 | tf_op jit(solution)/shard_map/all_to_all | solution.py:53
  95.8 1.0 copy-done.8
  96.8 1.2 convolution_bitcast_fusion.2
  98.0 1.7 copy.49
  99.9 18.7 %all_to_all.41 = bf16[16,32,1024]{2,1,0:T(8,128)(2,1)S(1)} all-to-all(bf16[16,32,1024]{2,1,0:T(8,128)(2,1)S(1)} %broadcast_in_dim.69), channel_id=1, replica_groups=mesh['row'=8,'col'=4,'depth'=4] {'col','depth'}, dimensions={0} | all-to-all | bytes 2097152 | tf_op jit(solution)/shard_map/all_to_all | solution.py:53
  118.5 1.0 copy-done.6
  119.5 5.5 %convolution_bitcast_fusion = f32[512,1792]{0,1:T(8,128)} fusion(bf16[512,1024]{1,0:T(8,128)(2,1)S(1)} %bitcast.75, bf16[1024,896]{0,1:T(8,128)(2,1)S(1)} %copy-done.3, bf16[1024,896]{0,1:T(8,128)(2,1)} %get-tuple-element.33), kind=kOutput, calls=%fused_computation.10 | convolution fusion | flops 1886388224 | bytes 8388608 | tf_op jit(solution)/shard_map/dot_general | solution.py:78
  125.0 5.2 %copy.45 = f32[512,1792]{1,0:T(8,128)} copy(f32[512,1792]{0,1:T(8,128)} %convolution_bitcast_fusion) | data formatting | bytes 7340032
  130.4 1.3 multiply_convert_fusion.3
  132.5 13.6 %reduce-scatter.19.cloned.1.call-done = f32[64,896]{1,0:T(8,128)} async-done(((f32[512,896]{1,0:T(8,128)}), f32[64,896]{1,0:T(8,128)}) %reduce-scatter.19.cloned.1.call-update) | async-done | bytes 229392 | tf_op jit(solution)/shard_map/reduce_scatter | solution.py:34
  146.1 37.8 %reduce-scatter.15.cloned.1.call-done = f32[64,1792]{1,0:T(8,128)} async-done(((f32[512,1792]{1,0:T(8,128)}), f32[64,1792]{1,0:T(8,128)}) %reduce-scatter.15.cloned.1.call-update) | async-done | bytes 458768 | tf_op jit(solution)/shard_map/reduce_scatter | solution.py:34
  183.9 1.3 multiply_convert_fusion.1
  186.0 18.2 %all_gather.12 = bf16[512,896]{1,0:T(8,128)(2,1)S(1)} all-gather(bf16[64,896]{1,0:T(8,128)(2,1)S(1)} %get-tuple-element.26), channel_id=1, replica_groups=mesh['row'=8,'col'=4,'depth'=4] {'row'}, dimensions={0}, use_global_device_ids=true | all-gather | bytes 1032192 | tf_op jit(solution)/shard_map/all_gather | solution.py:38
  204.2 3.9 %convolution_convert_fusion.1 = bf16[512,1024]{1,0:T(8,128)(2,1)} fusion(bf16[512,896]{1,0:T(8,128)(2,1)S(1)} %all_gather.12, bf16[896,1024]{1,0:T(8,128)(2,1)} %param.11, pred[112,8,8,128]{3,2,1,0:T(8,128)(4,1)S(1)} %bitcast.83), kind=kOutput, calls=%fused_computation.15 | convolution fusion | flops 940965888 | bytes 4718592 | tf_op jit(solution)/shard_map/dot_general | solution.py:81
  208.0 6.7 %all-to-all-start.1 = ((bf16[16,32,1024]{2,1,0:T(8,128)(2,1)}), bf16[16,32,1024]{2,1,0:T(8,128)(2,1)S(1)}, u32[]{:S(2)}, u32[]{:S(2)}) async-start(bf16[16,32,1024]{2,1,0:T(8,128)(2,1)} %bitcast.5), calls=%async_computation.1 | async-start | bytes 2097152 | tf_op jit(solution)/shard_map/all_to_all | solution.py:44
  214.7 13.9 %all_gather.13 = bf16[512,896]{1,0:T(8,128)(2,1)S(1)} all-gather(bf16[64,896]{1,0:T(8,128)(2,1)S(1)} %get-tuple-element.27), channel_id=1, replica_groups=mesh['row'=8,'col'=4,'depth'=4] {'row'}, dimensions={0}, use_global_device_ids=true | all-gather | bytes 1032192 | tf_op jit(solution)/shard_map/all_gather | solution.py:38
  228.6 0.9 copy-done.11
  229.5 3.8 %convolution_convert_fusion = bf16[512,1024]{1,0:T(8,128)(2,1)} fusion(bf16[512,896]{1,0:T(8,128)(2,1)S(1)} %all_gather.13, bf16[896,1024]{1,0:T(8,128)(2,1)} %param.11, pred[112,8,8,128]{3,2,1,0:T(8,128)(4,1)S(1)} %bitcast.84), kind=kOutput, calls=%fused_computation.14 | convolution fusion | flops 940965888 | bytes 4718592 | tf_op jit(solution)/shard_map/dot_general | solution.py:81
  233.4 6.9 %all-to-all-start.3 = ((bf16[16,32,1024]{2,1,0:T(8,128)(2,1)}), bf16[16,32,1024]{2,1,0:T(8,128)(2,1)S(1)}, u32[]{:S(2)}, u32[]{:S(2)}) async-start(bf16[16,32,1024]{2,1,0:T(8,128)(2,1)} %bitcast.79), calls=%async_computation.3 | async-start | bytes 2097152 | tf_op jit(solution)/shard_map/all_to_all | solution.py:44
  240.3 4.1 %fusion.5 = f32[896,1024]{1,0:T(8,128)} fusion(bf16[512,896]{1,0:T(8,128)(2,1)S(1)} %all_gather.12, bf16[512,1024]{1,0:T(8,128)(2,1)} %bitcast.72), kind=kOutput, calls=%fused_computation.40 | convolution fusion | flops 939524096 | bytes 5636096 | tf_op jit(solution)/shard_map/dot_general | solution.py:82
  244.4 5.7 %convolution_convert_fusion.3 = bf16[512,1024]{1,0:T(8,128)(2,1)} fusion(bf16[512,1792]{1,0:T(8,128)(2,1)} %all-gather.3.cloned.1.call-done, bf16[1024,896]{0,1:T(8,128)(2,1)} %get-tuple-element.32, bf16[1024,896]{0,1:T(8,128)(2,1)} %get-tuple-element.33), kind=kOutput, calls=%fused_computation.17 | convolution fusion | flops 1886912512 | bytes 6553600 | tf_op jit(solution)/shard_map/dot_general | solution.py:85
  250.1 6.8 %all-to-all-done.3 = bf16[16,32,1024]{2,1,0:T(8,128)(2,1)S(1)} async-done(((bf16[16,32,1024]{2,1,0:T(8,128)(2,1)}), bf16[16,32,1024]{2,1,0:T(8,128)(2,1)S(1)}, u32[]{:S(2)}, u32[]{:S(2)}) %all-to-all-start.3) | async-done | bytes 1048608 | tf_op jit(solution)/shard_map/all_to_all | solution.py:44
  257.0 4.4 %all-to-all-start.5 = ((bf16[16,32,1024]{2,1,0:T(8,128)(2,1)}), bf16[16,32,1024]{2,1,0:T(8,128)(2,1)S(1)}, u32[]{:S(2)}, u32[]{:S(2)}) async-start(bf16[16,32,1024]{2,1,0:T(8,128)(2,1)} %bitcast.11), calls=%async_computation.5 | async-start | bytes 2097152 | tf_op jit(solution)/shard_map/all_to_all | solution.py:44
  261.4 5.5 %select_convert_fusion = bf16[896,1024]{1,0:T(8,128)(2,1)} fusion(f32[896,1024]{1,0:T(8,128)} %fusion.5, pred[112,8,8,128]{3,2,1,0:T(8,128)(4,1)} %bitcast.81, bf16[512,896]{1,0:T(8,128)(2,1)} %copy-done.11, bf16[512,1024]{1,0:T(8,128)(2,1)} %bitcast.78), kind=kOutput, calls=%fused_computation.8 | convolution fusion | flops 942276608 | bytes 8388608 | tf_op jit(solution)/shard_map/dot_general | solution.py:82
  267.9 5.7 %convolution_convert_fusion.2 = bf16[512,1024]{1,0:T(8,128)(2,1)} fusion(bf16[512,1792]{1,0:T(8,128)(2,1)} %all-gather.5.cloned.1.call-done, bf16[1024,896]{0,1:T(8,128)(2,1)} %get-tuple-element.32, bf16[1024,896]{0,1:T(8,128)(2,1)} %get-tuple-element.33), kind=kOutput, calls=%fused_computation.16 | convolution fusion | flops 1886912512 | bytes 6553600 | tf_op jit(solution)/shard_map/dot_general | solution.py:85
  273.6 3.6 %all-to-all-done.5 = bf16[16,32,1024]{2,1,0:T(8,128)(2,1)S(1)} async-done(((bf16[16,32,1024]{2,1,0:T(8,128)(2,1)}), bf16[16,32,1024]{2,1,0:T(8,128)(2,1)S(1)}, u32[]{:S(2)}, u32[]{:S(2)}) %all-to-all-start.5) | async-done | bytes 1048608 | tf_op jit(solution)/shard_map/all_to_all | solution.py:44
  277.2 4.6 %all-to-all-start.7 = ((bf16[16,32,1024]{2,1,0:T(8,128)(2,1)}), bf16[16,32,1024]{2,1,0:T(8,128)(2,1)}, u32[]{:S(2)}, u32[]{:S(2)}) async-start(bf16[16,32,1024]{2,1,0:T(8,128)(2,1)} %bitcast.14), calls=%async_computation.7 | async-start | bytes 2097152 | tf_op jit(solution)/shard_map/all_to_all | solution.py:44
  281.8 3.8 %fusion.4 = f32[1792,1024]{1,0:T(8,128)S(1)} fusion(bf16[512,1792]{1,0:T(8,128)(2,1)} %all-gather.3.cloned.1.call-done, bf16[512,1024]{1,0:T(8,128)(2,1)S(1)} %bitcast.74), kind=kOutput, calls=%fused_computation.39 | convolution fusion | flops 1879048192 | bytes 10223616 | tf_op jit(solution)/shard_map/dot_general | solution.py:87
  285.6 2.3 add_bitcast_fusion
  287.9 2.3 fusion.1
  290.2 3.8 %copy.41 = bf16[1024,896]{1,0:T(8,128)(2,1)} copy(bf16[1024,896]{0,1:T(8,128)(2,1)} %get-tuple-element.21) | data formatting | bytes 3670016
  294.0 2.4 copy.42
  296.6 1.4 reduce.3
  (71 shorter events, 6.2 us)
Async XLA Ops:
  7.2 10.6 %copy-start.13 = (s32[7,8]{1,0:T(8,128)S(1)}, s32[7,8]{1,0:T(8,128)}, u32[]{:S(2)}) copy-start(s32[7,8]{1,0:T(8,128)} %param.14) | copy-start | bytes 676
  9.2 24.6 %all-to-all-start.4 = ((bf16[16,32,1024]{2,1,0:T(8,128)(2,1)}), bf16[16,32,1024]{2,1,0:T(8,128)(2,1)S(1)}, u32[]{:S(2)}, u32[]{:S(2)}) async-start(bf16[16,32,1024]{2,1,0:T(8,128)(2,1)} %broadcast_in_dim.70), calls=%async_computation.4 | async-start | bytes 2097152 | tf_op jit(solution)/shard_map/all_to_all | solution.py:53
  17.8 112.6 %reduce-scatter.17.cloned.1.call-start = ((), (), s32[]{:S(2)}) async-start(), calls=%async_computation.16 | async-start | bytes 2064384 | tf_op jit(solution)/shard_map/reduce_scatter | solution.py:34
  33.8 6.5 %copy-start.2 = (bf16[16,32,1024]{2,1,0:T(8,128)(2,1)}, bf16[16,32,1024]{2,1,0:T(8,128)(2,1)S(1)}, u32[]{:S(2)}) copy-start(bf16[16,32,1024]{2,1,0:T(8,128)(2,1)S(1)} %all-to-all-done.4) | copy-start | bytes 3145732
  36.6 0.9 copy-start.9
  42.0 0.9 copy-start.12
  42.9 5.4 %copy-start.14 = (s32[8,7]{1,0:T(8,128)S(1)}, s32[8,7]{1,0:T(8,128)}, u32[]{:S(2)}) copy-start(s32[8,7]{1,0:T(8,128)} %param.13) | copy-start | bytes 676
  42.9 5.6 %copy-start.15 = (s32[8,7]{1,0:T(8,128)S(1)}, s32[8,7]{1,0:T(8,128)}, u32[]{:S(2)}) copy-start(s32[8,7]{1,0:T(8,128)} %param.12) | copy-start | bytes 676
  44.1 19.4 %all-to-all-start = ((bf16[16,32,1024]{2,1,0:T(8,128)(2,1)}), bf16[16,32,1024]{2,1,0:T(8,128)(2,1)S(1)}, u32[]{:S(2)}, u32[]{:S(2)}) async-start(bf16[16,32,1024]{2,1,0:T(8,128)(2,1)} %broadcast_in_dim.65), calls=%async_computation | async-start | bytes 2097152 | tf_op jit(solution)/shard_map/all_to_all | solution.py:53
  48.3 82.1 %reduce-scatter.13.cloned.1.call-start = ((), (), s32[]{:S(2)}) async-start(), calls=%async_computation.14 | async-start | bytes 4128768 | tf_op jit(solution)/shard_map/reduce_scatter | solution.py:34
  63.4 6.4 %copy-start.4 = (bf16[16,32,1024]{2,1,0:T(8,128)(2,1)}, bf16[16,32,1024]{2,1,0:T(8,128)(2,1)S(1)}, u32[]{:S(2)}) copy-start(bf16[16,32,1024]{2,1,0:T(8,128)(2,1)S(1)} %all-to-all-done) | copy-start | bytes 3145732
  75.0 21.8 %copy-start.10 = (pred[896,8,128]{2,1,0:T(8,128)(4,1)S(1)}, pred[896,8,128]{2,1,0:T(8,128)(4,1)}, u32[]{:S(2)}) copy-start(pred[896,8,128]{2,1,0:T(8,128)(4,1)} %copy-done.9) | copy-start | bytes 2752516
  75.0 71.0 %reduce-scatter.19.cloned.1.call-start = ((), (), s32[]{:S(2)}) async-start(), calls=%async_computation.17 | async-start | bytes 2064384 | tf_op jit(solution)/shard_map/reduce_scatter | solution.py:34
  75.1 21.7 %copy-start.16 = (bf16[896,1024]{1,0:T(8,128)(2,1)S(1)}, bf16[896,1024]{1,0:T(8,128)(2,1)}, u32[]{:S(2)}) copy-start(bf16[896,1024]{1,0:T(8,128)(2,1)} %param.11) | copy-start | bytes 5505028
  95.8 1.0 copy-start.8
  99.7 19.8 %copy-start.3 = (bf16[1024,896]{0,1:T(8,128)(2,1)S(1)}, bf16[1024,896]{0,1:T(8,128)(2,1)}, u32[]{:S(2)}) copy-start(bf16[1024,896]{0,1:T(8,128)(2,1)} %get-tuple-element.32) | copy-start | bytes 5505028
  99.7 84.2 %reduce-scatter.15.cloned.1.call-start = ((), (), s32[]{:S(2)}) async-start(), calls=%async_computation.15 | async-start | bytes 4128768 | tf_op jit(solution)/shard_map/reduce_scatter | solution.py:34
  118.5 1.0 copy-start.6
  130.3 114.2 %all-gather.3.cloned.1.call-start = ((), (), s32[]{:S(2)}) async-start(), calls=%async_computation.12 | async-start | bytes 2064384 | tf_op jit(solution)/shard_map/all_gather | solution.py:38
  132.4 135.5 %all-gather.5.cloned.1.call-start = ((), (), s32[]{:S(2)}) async-start(), calls=%async_computation.13 | async-start | bytes 2064384 | tf_op jit(solution)/shard_map/all_gather | solution.py:38
  208.0 25.3 %all-to-all-start.1 = ((bf16[16,32,1024]{2,1,0:T(8,128)(2,1)}), bf16[16,32,1024]{2,1,0:T(8,128)(2,1)S(1)}, u32[]{:S(2)}, u32[]{:S(2)}) async-start(bf16[16,32,1024]{2,1,0:T(8,128)(2,1)} %bitcast.5), calls=%async_computation.1 | async-start | bytes 2097152 | tf_op jit(solution)/shard_map/all_to_all | solution.py:44
  228.6 0.9 copy-start.11
  233.4 11.1 %copy-start = (bf16[16,32,1024]{2,1,0:T(8,128)(2,1)}, bf16[16,32,1024]{2,1,0:T(8,128)(2,1)S(1)}, u32[]{:S(2)}) copy-start(bf16[16,32,1024]{2,1,0:T(8,128)(2,1)S(1)} %all-to-all-done.1) | copy-start | bytes 3145732
  233.4 23.6 %all-to-all-start.3 = ((bf16[16,32,1024]{2,1,0:T(8,128)(2,1)}), bf16[16,32,1024]{2,1,0:T(8,128)(2,1)S(1)}, u32[]{:S(2)}, u32[]{:S(2)}) async-start(bf16[16,32,1024]{2,1,0:T(8,128)(2,1)} %bitcast.79), calls=%async_computation.3 | async-start | bytes 2097152 | tf_op jit(solution)/shard_map/all_to_all | solution.py:44
  257.0 20.3 %all-to-all-start.5 = ((bf16[16,32,1024]{2,1,0:T(8,128)(2,1)}), bf16[16,32,1024]{2,1,0:T(8,128)(2,1)S(1)}, u32[]{:S(2)}, u32[]{:S(2)}) async-start(bf16[16,32,1024]{2,1,0:T(8,128)(2,1)} %bitcast.11), calls=%async_computation.5 | async-start | bytes 2097152 | tf_op jit(solution)/shard_map/all_to_all | solution.py:44
  261.4 5.5 %copy-start.1 = (bf16[16,32,1024]{2,1,0:T(8,128)(2,1)S(1)}, bf16[16,32,1024]{2,1,0:T(8,128)(2,1)}, u32[]{:S(2)}) copy-start(bf16[16,32,1024]{2,1,0:T(8,128)(2,1)} %copy-done) | copy-start | bytes 3145732
  273.6 8.2 %copy-start.5 = (bf16[16,32,1024]{2,1,0:T(8,128)(2,1)S(1)}, bf16[16,32,1024]{2,1,0:T(8,128)(2,1)}, u32[]{:S(2)}) copy-start(bf16[16,32,1024]{2,1,0:T(8,128)(2,1)} %copy-done.4) | copy-start | bytes 3145732
  277.2 19.4 %all-to-all-start.7 = ((bf16[16,32,1024]{2,1,0:T(8,128)(2,1)}), bf16[16,32,1024]{2,1,0:T(8,128)(2,1)}, u32[]{:S(2)}, u32[]{:S(2)}) async-start(bf16[16,32,1024]{2,1,0:T(8,128)(2,1)} %bitcast.14), calls=%async_computation.7 | async-start | bytes 2097152 | tf_op jit(solution)/shard_map/all_to_all | solution.py:44
  281.8 3.8 %copy-start.7 = (bf16[16,32,1024]{2,1,0:T(8,128)(2,1)S(1)}, bf16[16,32,1024]{2,1,0:T(8,128)(2,1)}, u32[]{:S(2)}) copy-start(bf16[16,32,1024]{2,1,0:T(8,128)(2,1)} %copy-done.6) | copy-start | bytes 3145732
  281.8 3.8 %copy-start.17 = (bf16[512,1792]{1,0:T(8,128)(2,1)S(1)}, bf16[512,1792]{1,0:T(8,128)(2,1)}, u32[]{:S(2)}) copy-start(bf16[512,1792]{1,0:T(8,128)(2,1)} %all-gather.5.cloned.1.call-done) | copy-start | bytes 5505028
Sparse Core Ops, SparseCore 0:
  42.2 30.0 reduce-scatter.16
  75.1 35.3 reduce-scatter.12
  113.6 32.4 reduce-scatter.18
  148.3 35.5 reduce-scatter.14
  185.5 27.6 all-gather.2
  214.7 25.0 all-gather.4

commit v4 on v2

--- a/solution.py
+++ b/solution.py
@@ -62,7 +62,6 @@
         axis=1,
     )
     w_down = jnp.where(keep_down, down_weight, zero_value)
-    grad_all = group_gather(grad_out)
     x_all = group_gather(tokens)
     total = x_all.shape[0]
     split_rows = total // lax.axis_size("row")
@@ -73,9 +72,6 @@
     def hidden_term(start, count):
         return jnp.dot(x_all, w_both, preferred_element_type=jnp.float32)
 
-    def act_term(start, count):
-        return lax.dot_general(grad_all, w_down, outer, preferred_element_type=jnp.float32)
-
     sums = row_sums(hidden_term, split_rows)
     act_all = row_gather(swiglu(sums))
 
@@ -83,10 +79,16 @@
         return jnp.dot(act_all, w_down, preferred_element_type=jnp.float32)
 
     mixed = group_sums(out_term, own_rows).astype(jnp.bfloat16)
+    grad_all = group_gather(grad_out)
     grad_down = lax.dot_general(act_all, grad_all, inner, preferred_element_type=jnp.float32)
     grad_down_weight = jnp.where(keep_down, grad_down, jnp.float32(0.0)).astype(jnp.bfloat16)
+
+    def act_term(start, count):
+        return lax.dot_general(grad_all, w_down, outer, preferred_element_type=jnp.float32)
+
     grad_act = row_sums(act_term, split_rows)
-    grads_all = row_gather(swiglu_back(sums, grad_act))
+    held_sums, grad_act = lax.optimization_barrier((sums, grad_act))
+    grads_all = row_gather(swiglu_back(held_sums, grad_act))
     grad_both = lax.dot_general(x_all, grads_all, inner, preferred_element_type=jnp.float32)
     width = grad_both.shape[1] // 2
     grad_gate_weight = jnp.where(keep_gate, grad_both[:, :width], jnp.float32(0.0)).astype(

time: 273 us -> 265 us (0.971)
  waiting for transfers between devices: 152 us -> 145 us
    reduce_scatter x2, waiting for transfers between devices: 47.2 us -> 36.9 us  [row_sums(): lax.psum_scatter(term(jnp.int32(0), lax.axis_size('row') * rows), 'row',...]
    unnamed x20 -> x22, local copies, waits for them, and re-layouts: 16.7 us -> 16.7 us
  transfers between devices with their start and end apart: 8 -> 8, of which waited for: 7 -> 7; matrix products, arithmetic and copies ran while one was open for 23% -> 24% of each run, Pallas kernels for 0% -> 0%
where the time goes in v4:
time: 265 us
  waiting for transfers between devices  145 us (55%)
  matrix products  41.1 us (16%)
  starting transfers between devices  26.3 us (10%)
  local copies, waits for them, and re-layouts  23.8 us (9%)
  other arithmetic  14.6 us (6%)
  between operations  13.9 us (5%)
    all_gather x2, waiting for transfers between devices, row_gather(): return lax.all_gather(block, 'row', axis=0, tiled=True)  51.9 us
    all_to_all x2, waiting for transfers between devices, group_gather(): pieces = lax.all_to_all(copies, ('col', 'depth'), 0, 0)  48.8 us
    reduce_scatter x2, waiting for transfers between devices, row_sums(): lax.psum_scatter(term(jnp.int32(0), lax.axis_size('row') * rows), 'row',...  36.9 us
    unnamed x22, local copies, waits for them, and re-layouts  16.7 us
    all_to_all x2, starting transfers between devices, group_sums(): lax.all_to_all(full.reshape((parts, rows) + full.shape[1:]), ('col', 'dep...  13.4 us
    all_to_all x2, starting transfers between devices, group_gather(): pieces = lax.all_to_all(copies, ('col', 'depth'), 0, 0)  12.7 us
    dot_general x1, matrix products, hidden_term(): return jnp.dot(x_all, w_both, preferred_element_type=jnp.float32)  9.66 us
    dot_general x1, matrix products, input_term(): lax.dot_general(grads_all, w_both, outer, preferred_element_type=jnp.floa...  8.53 us
  transfers between devices with their start and end apart: 8, of which 7 were waited for; matrix products, arithmetic and copies ran while one was open for 24% of the time, Pallas kernels for 0%

profile of v4, /device:TPU:1, one launch (start us, length us, event | category | flops | bytes accessed | tf_op | source)
XLA Modules:
  0.0 264.6 jit_solution(5946852873612733416)
XLA Ops:
  7.2 2.5 broadcast_in_dim.53
  9.7 8.8 %all-to-all-start = ((bf16[16,64,1024]{2,1,0:T(8,128)(2,1)}), bf16[16,64,1024]{2,1,0:T(8,128)(2,1)}, u32[]{:S(2)}, u32[]{:S(2)}) async-start(bf16[16,64,1024]{2,1,0:T(8,128)(2,1)} %broadcast_in_dim.53), calls=%async_computation | async-start | bytes 4194304 | tf_op jit(solution)/shard_map/all_to_all | solution.py:51
  18.5 0.0 reduce-scatter.3.cloned.1.call-start
  18.5 0.1 copy.15
  18.6 0.1 broadcast_bitcast_fusion
  18.7 0.1 copy.13
  18.8 0.1 broadcast_bitcast_fusion.1
  18.9 2.9 %copy.14 = bf16[1024,896]{0,1:T(8,128)(2,1)S(1)} copy(bf16[1024,896]{1,0:T(8,128)(2,1)} %param.9) | data formatting | bytes 3670016 | tf_op args[1]
  21.8 3.8 %copy.16 = bf16[1024,896]{0,1:T(8,128)(2,1)} copy(bf16[1024,896]{1,0:T(8,128)(2,1)} %param.10) | data formatting | bytes 3670016 | tf_op args[2]
  25.6 3.6 %bitcast_select_fusion.1 = (bf16[1024,896]{0,1:T(8,128)(2,1)}, bf16[1024,896]{0,1:T(8,128)(2,1)}) fusion(bf16[1024,896]{0,1:T(8,128)(2,1)} %copy.16, pred[1024,7]{0,1:T(8,128)(4,1)S(1)} %bitcast.57, bf16[1024,896]{0,1:T(8,128)(2,1)S(1)} %copy.14, pred[1024,7]{0,1:T(8,128)(4,1)S(1)} %bitcast.59), kind=kLoop, calls=%fused_computation.1 | loop fusion | flops 1835008 | bytes 7354368 | tf_op jit(solution)/shard_map/jit(_where)/select_n | solution.py:61
  29.2 20.2 %all-to-all-done = bf16[16,64,1024]{2,1,0:T(8,128)(2,1)} async-done(((bf16[16,64,1024]{2,1,0:T(8,128)(2,1)}), bf16[16,64,1024]{2,1,0:T(8,128)(2,1)}, u32[]{:S(2)}, u32[]{:S(2)}) %all-to-all-start) | async-done | bytes 2097184 | tf_op jit(solution)/shard_map/all_to_all | solution.py:51
  49.5 9.7 %convolution_bitcast_fusion.1 = f32[1024,1792]{0,1:T(8,128)} fusion(bf16[1024,1024]{1,0:T(8,128)(2,1)} %bitcast.2, bf16[1024,896]{0,1:T(8,128)(2,1)} %get-tuple-element.18, bf16[1024,896]{0,1:T(8,128)(2,1)} %get-tuple-element.19), kind=kOutput, calls=%fused_computation.5 | convolution fusion | flops 3765436416 | bytes 13107200 | tf_op jit(solution)/shard_map/dot_general | solution.py:73
  59.1 0.0 reduce-scatter.3.cloned.1.call-update
  59.2 0.9 copy-done.2
  60.0 1.6 broadcast_in_dim.57
  61.7 3.9 %all-to-all-start.2 = ((bf16[16,64,1024]{2,1,0:T(8,128)(2,1)}), bf16[16,64,1024]{2,1,0:T(8,128)(2,1)S(1)}, u32[]{:S(2)}, u32[]{:S(2)}) async-start(bf16[16,64,1024]{2,1,0:T(8,128)(2,1)} %broadcast_in_dim.57), calls=%async_computation.3 | async-start | bytes 4194304 | tf_op jit(solution)/shard_map/all_to_all | solution.py:51
  65.6 0.0 reduce-scatter.5.cloned.1.call-start
  65.7 0.0 copy-done.5
  65.7 28.5 %all-to-all-done.2 = bf16[16,64,1024]{2,1,0:T(8,128)(2,1)S(1)} async-done(((bf16[16,64,1024]{2,1,0:T(8,128)(2,1)}), bf16[16,64,1024]{2,1,0:T(8,128)(2,1)S(1)}, u32[]{:S(2)}, u32[]{:S(2)}) %all-to-all-start.2) | async-done | bytes 2097184 | tf_op jit(solution)/shard_map/all_to_all | solution.py:51
  94.3 2.8 %broadcast_in_dim.55 = pred[896,8,128]{2,1,0:T(8,128)(4,1)S(1)} broadcast(pred[896,8]{1,0:T(8,128)(4,1)S(1)} %bitcast.56), dimensions={0,1} | broadcast | bytes 924672 | tf_op jit(solution)/shard_map/broadcast_in_dim | solution.py:10
  97.1 5.6 %convolution_bitcast_fusion.2 = f32[1024,896]{0,1:T(8,128)} fusion(bf16[1024,1024]{1,0:T(8,128)(2,1)S(1)} %bitcast.49, bf16[896,1024]{1,0:T(8,128)(2,1)} %param.11, pred[112,8,8,128]{3,2,1,0:T(8,128)(4,1)S(1)} %bitcast.53), kind=kOutput, calls=%fused_computation.12 | convolution fusion | flops 1879965696 | bytes 8519680 | tf_op jit(solution)/shard_map/dot_general | solution.py:87
  102.7 0.0 reduce-scatter.5.cloned.1.call-update
  102.7 0.0 copy-start.6
  102.7 0.0 all-gather.3.cloned.1.call-start
  102.7 2.4 reduce-scatter.3.cloned.1.call-done
  105.1 2.0 fusion.6
  107.1 0.0 all-gather.3.cloned.1.call-update
  107.2 0.0 all-gather.5.cloned.1.call-start
  107.2 34.5 %reduce-scatter.5.cloned.1.call-done = f32[128,896]{0,1:T(8,128)} async-done(((f32[1024,896]{0,1:T(8,128)}), f32[128,896]{0,1:T(8,128)}) %reduce-scatter.5.cloned.1.call-update) | async-done | bytes 458768 | tf_op jit(solution)/shard_map/reduce_scatter | solution.py:32
  141.7 1.5 multiply_convert_fusion.1
  143.2 0.8 pad_maximum_fusion.5
  144.0 0.0 all-gather.5.cloned.1.call-update
  144.0 27.4 %all-gather.3.cloned.1.call-done = bf16[1024,896]{0,1:T(8,128)(2,1)} async-done(((bf16[128,896]{0,1:T(8,128)(2,1)}), bf16[1024,896]{0,1:T(8,128)(2,1)}) %all-gather.3.cloned.1.call-update) | async-done | bytes 1835024 | tf_op jit(solution)/shard_map/all_gather | solution.py:38
  171.4 5.2 %convolution_convert_fusion = bf16[1024,1024]{1,0:T(8,128)(2,1)} fusion(bf16[1024,896]{0,1:T(8,128)(2,1)} %all-gather.3.cloned.1.call-done, bf16[896,1024]{1,0:T(8,128)(2,1)S(1)} %copy-done.6, pred[112,8,8,128]{3,2,1,0:T(8,128)(4,1)S(1)} %bitcast.54), kind=kOutput, calls=%fused_computation.14 | convolution fusion | flops 1881014272 | bytes 6684672 | tf_op jit(solution)/shard_map/dot_general | solution.py:79
  176.7 6.7 %all-to-all-start.1 = ((bf16[16,64,1024]{2,1,0:T(8,128)(2,1)}), bf16[16,64,1024]{2,1,0:T(8,128)(2,1)S(1)}, u32[]{:S(2)}, u32[]{:S(2)}) async-start(bf16[16,64,1024]{2,1,0:T(8,128)(2,1)} %bitcast.52), calls=%async_computation.2 | async-start | bytes 4194304 | tf_op jit(solution)/shard_map/all_to_all | solution.py:44
  183.4 24.4 %all-gather.5.cloned.1.call-done = bf16[1024,1792]{0,1:T(8,128)(2,1)} async-done(((bf16[128,1792]{0,1:T(8,128)(2,1)}), bf16[1024,1792]{0,1:T(8,128)(2,1)}) %all-gather.5.cloned.1.call-update) | async-done | bytes 3670032 | tf_op jit(solution)/shard_map/all_gather | solution.py:38
  207.8 8.5 %fusion.3 = bf16[1024,1024]{1,0:T(8,128)(2,1)} fusion(bf16[1024,1792]{0,1:T(8,128)(2,1)} %all-gather.5.cloned.1.call-done, bf16[1024,896]{0,1:T(8,128)(2,1)} %get-tuple-element.18, bf16[1024,896]{0,1:T(8,128)(2,1)} %get-tuple-element.19), kind=kOutput, calls=%fused_computation.13 | convolution fusion | flops 3766484992 | bytes 9437184 | tf_op jit(solution)/shard_map/dot_general | solution.py:100
  216.4 0.0 all-to-all-done.1
  216.4 1.3 copy-done
  217.7 6.7 %all-to-all-start.3 = ((bf16[16,64,1024]{2,1,0:T(8,128)(2,1)}), bf16[16,64,1024]{2,1,0:T(8,128)(2,1)S(1)}, u32[]{:S(2)}, u32[]{:S(2)}) async-start(bf16[16,64,1024]{2,1,0:T(8,128)(2,1)} %bitcast.51), calls=%async_computation.5 | async-start | bytes 4194304 | tf_op jit(solution)/shard_map/all_to_all | solution.py:44
  224.4 5.5 %select_convert_fusion = bf16[896,1024]{1,0:T(8,128)(2,1)} fusion(pred[112,8,8,128]{3,2,1,0:T(8,128)(4,1)S(1)} %bitcast.55, bf16[1024,896]{0,1:T(8,128)(2,1)} %all-gather.3.cloned.1.call-done, bf16[1024,1024]{1,0:T(8,128)(2,1)} %bitcast.50), kind=kOutput, calls=%fused_computation.9 | convolution fusion | flops 1880883200 | bytes 6684672 | tf_op jit(solution)/shard_map/dot_general | solution.py:83
  229.8 2.7 %reduce_sum.24 = bf16[64,1024]{1,0:T(8,128)(2,1)} reduce(bf16[16,64,1024]{2,1,0:T(8,128)(2,1)} %copy-done, bf16[]{:T(256)} %constant.2.clone.1), dimensions={0}, to_apply=%region_1.2 | reduce | flops 983040 | bytes 2228226 | tf_op jit(solution)/shard_map/reduce_sum | solution.py:45
  232.5 6.7 %convolution_bitcast_fusion = bf16[1024,1792]{0,1:T(8,128)(2,1)S(1)} fusion(bf16[1024,1792]{0,1:T(8,128)(2,1)} %all-gather.5.cloned.1.call-done, bf16[1024,1024]{1,0:T(8,128)(2,1)} %bitcast.2), kind=kOutput, calls=%fused_computation.4 | convolution fusion | flops 3758096384 | bytes 9437184 | tf_op jit(solution)/shard_map/dot_general | solution.py:92
  239.2 2.9 %fusion.1 = (bf16[1024,896]{0,1:T(8,128)(2,1)}, bf16[1024,896]{0,1:T(8,128)(2,1)}) fusion(bf16[1024,1792]{0,1:T(8,128)(2,1)S(1)} %convolution_bitcast_fusion, pred[1024,7]{0,1:T(8,128)(4,1)S(1)} %bitcast.58, pred[1024,7]{0,1:T(8,128)(4,1)S(1)} %bitcast.60), kind=kLoop, calls=%fused_computation.7 | loop fusion | flops 1835008 | bytes 7354368 | tf_op jit(solution)/shard_map/convert_element_type | solution.py:97
  242.1 3.8 %copy.17 = bf16[1024,896]{1,0:T(8,128)(2,1)} copy(bf16[1024,896]{0,1:T(8,128)(2,1)} %get-tuple-element.15) | data formatting | bytes 3670016
  245.9 3.8 %copy.18 = bf16[1024,896]{1,0:T(8,128)(2,1)} copy(bf16[1024,896]{0,1:T(8,128)(2,1)} %get-tuple-element.14) | data formatting | bytes 3670016
  249.7 7.3 %all-to-all-done.3 = bf16[16,64,1024]{2,1,0:T(8,128)(2,1)S(1)} async-done(((bf16[16,64,1024]{2,1,0:T(8,128)(2,1)}), bf16[16,64,1024]{2,1,0:T(8,128)(2,1)S(1)}, u32[]{:S(2)}, u32[]{:S(2)}) %all-to-all-start.3) | async-done | bytes 2097184 | tf_op jit(solution)/shard_map/all_to_all | solution.py:44
  257.0 1.1 reduce_sum.25
  (16 shorter events, 0.1 us)
Async XLA Ops:
  9.7 8.8 %copy-start.3 = (s32[8,7]{1,0:T(8,128)S(1)}, s32[8,7]{1,0:T(8,128)}, u32[]{:S(2)}) copy-start(s32[8,7]{1,0:T(8,128)} %param.13) | copy-start | bytes 676
  9.7 9.0 %copy-start.4 = (s32[8,7]{1,0:T(8,128)S(1)}, s32[8,7]{1,0:T(8,128)}, u32[]{:S(2)}) copy-start(s32[8,7]{1,0:T(8,128)} %param.12) | copy-start | bytes 676
  9.7 39.8 %all-to-all-start = ((bf16[16,64,1024]{2,1,0:T(8,128)(2,1)}), bf16[16,64,1024]{2,1,0:T(8,128)(2,1)}, u32[]{:S(2)}, u32[]{:S(2)}) async-start(bf16[16,64,1024]{2,1,0:T(8,128)(2,1)} %broadcast_in_dim.53), calls=%async_computation | async-start | bytes 4194304 | tf_op jit(solution)/shard_map/all_to_all | solution.py:51
  18.5 86.7 %reduce-scatter.3.cloned.1.call-start = ((), (), s32[]{:S(2)}) async-start(), calls=%async_computation.6 | async-start | bytes 8257536 | tf_op jit(solution)/shard_map/reduce_scatter | solution.py:32
  59.1 0.9 copy-start.2
  61.7 4.0 %copy-start.5 = (s32[7,8]{1,0:T(8,128)S(1)}, s32[7,8]{1,0:T(8,128)}, u32[]{:S(2)}) copy-start(s32[7,8]{1,0:T(8,128)} %param.14) | copy-start | bytes 676
  61.7 32.6 %all-to-all-start.2 = ((bf16[16,64,1024]{2,1,0:T(8,128)(2,1)}), bf16[16,64,1024]{2,1,0:T(8,128)(2,1)S(1)}, u32[]{:S(2)}, u32[]{:S(2)}) async-start(bf16[16,64,1024]{2,1,0:T(8,128)(2,1)} %broadcast_in_dim.57), calls=%async_computation.3 | async-start | bytes 4194304 | tf_op jit(solution)/shard_map/all_to_all | solution.py:51
  65.6 76.0 %reduce-scatter.5.cloned.1.call-start = ((), (), s32[]{:S(2)}) async-start(), calls=%async_computation.8 | async-start | bytes 4128768 | tf_op jit(solution)/shard_map/reduce_scatter | solution.py:32
  94.2 8.4 %copy-start.1 = (bf16[16,64,1024]{2,1,0:T(8,128)(2,1)}, bf16[16,64,1024]{2,1,0:T(8,128)(2,1)S(1)}, u32[]{:S(2)}) copy-start(bf16[16,64,1024]{2,1,0:T(8,128)(2,1)S(1)} %all-to-all-done.2) | copy-start | bytes 6291460
  102.7 68.8 %copy-start.6 = (bf16[896,1024]{1,0:T(8,128)(2,1)S(1)}, bf16[896,1024]{1,0:T(8,128)(2,1)}, u32[]{:S(2)}) copy-start(bf16[896,1024]{1,0:T(8,128)(2,1)} %param.11) | copy-start | bytes 5505028
  102.7 68.7 %all-gather.3.cloned.1.call-start = ((), (), s32[]{:S(2)}) async-start(), calls=%async_computation.7 | async-start | bytes 2064384 | tf_op jit(solution)/shard_map/all_gather | solution.py:38
  107.2 100.7 %all-gather.5.cloned.1.call-start = ((), (), s32[]{:S(2)}) async-start(), calls=%async_computation.9 | async-start | bytes 4128768 | tf_op jit(solution)/shard_map/all_gather | solution.py:38
  176.7 39.7 %all-to-all-start.1 = ((bf16[16,64,1024]{2,1,0:T(8,128)(2,1)}), bf16[16,64,1024]{2,1,0:T(8,128)(2,1)S(1)}, u32[]{:S(2)}, u32[]{:S(2)}) async-start(bf16[16,64,1024]{2,1,0:T(8,128)(2,1)} %bitcast.52), calls=%async_computation.2 | async-start | bytes 4194304 | tf_op jit(solution)/shard_map/all_to_all | solution.py:44
  216.4 1.3 copy-start
  217.7 39.3 %all-to-all-start.3 = ((bf16[16,64,1024]{2,1,0:T(8,128)(2,1)}), bf16[16,64,1024]{2,1,0:T(8,128)(2,1)S(1)}, u32[]{:S(2)}, u32[]{:S(2)}) async-start(bf16[16,64,1024]{2,1,0:T(8,128)(2,1)} %bitcast.51), calls=%async_computation.5 | async-start | bytes 4194304 | tf_op jit(solution)/shard_map/all_to_all | solution.py:44
Sparse Core Ops, SparseCore 0:
  59.3 45.8 reduce-scatter.2
  107.5 34.0 reduce-scatter.4
  143.4 28.0 all-gather.2
  173.5 34.2 all-gather.4

commit v5 on v4

--- a/solution.py
+++ b/solution.py
@@ -38,6 +38,13 @@
     return lax.all_gather(block, "row", axis=0, tiled=True)
 
 
+def row_gather_direct(block):
+    parts = lax.axis_size("row")
+    copies = jnp.broadcast_to(block[None], (parts,) + block.shape)
+    pieces = lax.all_to_all(copies, "row", 0, 0)
+    return pieces.reshape((parts * block.shape[0],) + block.shape[1:])
+
+
 def group_sums(term, rows):
     parts = lax.axis_size(("col", "depth"))
     full = term(jnp.int32(0), rows * parts).astype(jnp.bfloat16)
@@ -63,23 +70,21 @@
     )
     w_down = jnp.where(keep_down, down_weight, zero_value)
     x_all = group_gather(tokens)
-    total = x_all.shape[0]
-    split_rows = total // lax.axis_size("row")
+    split_rows = x_all.shape[0] // lax.axis_size("row")
     own_rows = tokens.shape[0]
     inner = (((0,), (0,)), ((), ()))
     outer = (((1,), (1,)), ((), ()))
 
-    def hidden_term(start, count):
-        return jnp.dot(x_all, w_both, preferred_element_type=jnp.float32)
-
-    sums = row_sums(hidden_term, split_rows)
-    act_all = row_gather(swiglu(sums))
+    hidden = jnp.dot(x_all, w_both, preferred_element_type=jnp.float32)
+    sums = row_sums(lambda start, count: hidden, split_rows)
+    grad_out, _ = lax.optimization_barrier((grad_out, hidden))
+    grad_all = group_gather(grad_out)
+    act_all = row_gather_direct(swiglu(sums))
 
     def out_term(start, count):
         return jnp.dot(act_all, w_down, preferred_element_type=jnp.float32)
 
     mixed = group_sums(out_term, own_rows).astype(jnp.bfloat16)
-    grad_all = group_gather(grad_out)
     grad_down = lax.dot_general(act_all, grad_all, inner, preferred_element_type=jnp.float32)
     grad_down_weight = jnp.where(keep_down, grad_down, jnp.float32(0.0)).astype(jnp.bfloat16)
 
@@ -87,7 +92,7 @@
         return lax.dot_general(grad_all, w_down, outer, preferred_element_type=jnp.float32)
 
     grad_act = row_sums(act_term, split_rows)
-    held_sums, grad_act = lax.optimization_barrier((sums, grad_act))
+    held_sums, grad_act, _ = lax.optimization_barrier((sums, grad_act, act_all))
     grads_all = row_gather(swiglu_back(held_sums, grad_act))
     grad_both = lax.dot_general(x_all, grads_all, inner, preferred_element_type=jnp.float32)
     width = grad_both.shape[1] // 2

time: 265 us -> 252 us (0.951)
  waiting for transfers between devices: 145 us -> 124 us
  starting transfers between devices: 26.3 us -> 31.2 us
  local copies, waits for them, and re-layouts: 23.8 us -> 26.5 us
    all_gather x2 -> x1, waiting for transfers between devices: 51.9 us -> 23.4 us  [row_gather(): return lax.all_gather(block, 'row', axis=0, tiled=True)]
    reduce_scatter x2, waiting for transfers between devices: 36.9 us -> 44.7 us  [row_sums(): lax.psum_scatter(term(jnp.int32(0), lax.axis_size('row') * rows), 'row',...]
    all_to_all x0 -> x1, starting transfers between devices: none -> 6.21 us  [row_gather_direct(): pieces = lax.all_to_all(copies, 'row', 0, 0)]
    unnamed x22 -> x28, local copies, waits for them, and re-layouts: 16.7 us -> 17.6 us
  transfers between devices with their start and end apart: 8 -> 8, of which waited for: 7 -> 6; matrix products, arithmetic and copies ran while one was open for 24% -> 25% of each run, Pallas kernels for 0% -> 0%
where the time goes in v5:
time: 252 us; the launch traced here: 251 us
  waiting for transfers between devices  124 us (49%)
  matrix products  41.5 us (16%)
  starting transfers between devices  31.2 us (12%)
  local copies, waits for them, and re-layouts  26.5 us (11%)
  other arithmetic  14 us (6%)
  between operations  13.9 us (6%)
    all_to_all x2, waiting for transfers between devices, group_gather(): pieces = lax.all_to_all(copies, ('col', 'depth'), 0, 0)  48.8 us
    reduce_scatter x2, waiting for transfers between devices, row_sums(): lax.psum_scatter(term(jnp.int32(0), lax.axis_size('row') * rows), 'row',...  44.7 us
    all_gather x1, waiting for transfers between devices, row_gather(): return lax.all_gather(block, 'row', axis=0, tiled=True)  23.4 us
    unnamed x28, local copies, waits for them, and re-layouts  17.6 us
    all_to_all x2, starting transfers between devices, group_gather(): pieces = lax.all_to_all(copies, ('col', 'depth'), 0, 0)  12.7 us
    all_to_all x2, starting transfers between devices, group_sums(): lax.all_to_all(full.reshape((parts, rows) + full.shape[1:]), ('col', 'dep...  12.2 us
    dot_general x1, matrix products, local(): hidden = jnp.dot(x_all, w_both, preferred_element_type=jnp.float32)  9.67 us
    dot_general x1, matrix products, input_term(): lax.dot_general(grads_all, w_both, outer, preferred_element_type=jnp.floa...  8.54 us
  transfers between devices with their start and end apart: 8, of which 6 were waited for; matrix products, arithmetic and copies ran while one was open for 25% of the time, Pallas kernels for 0%

profile of v5, /device:TPU:1, one launch (start us, length us, event | category | flops | bytes accessed | tf_op | source)
XLA Modules:
  0.0 251.1 jit_solution(7816544209429622609)
XLA Ops:
  7.2 2.5 broadcast_in_dim.59
  9.7 8.8 %all-to-all-start = ((bf16[16,64,1024]{2,1,0:T(8,128)(2,1)}), bf16[16,64,1024]{2,1,0:T(8,128)(2,1)}, u32[]{:S(2)}, u32[]{:S(2)}) async-start(bf16[16,64,1024]{2,1,0:T(8,128)(2,1)} %broadcast_in_dim.59), calls=%async_computation | async-start | bytes 4194304 | tf_op jit(solution)/shard_map/all_to_all | solution.py:58
  18.4 0.0 reduce-scatter.3.cloned.1.call-start
  18.5 0.1 copy.13
  18.6 0.1 copy.15
  18.7 0.1 broadcast_bitcast_fusion
  18.8 0.1 broadcast_bitcast_fusion.1
  18.9 2.9 %copy.14 = bf16[1024,896]{0,1:T(8,128)(2,1)S(1)} copy(bf16[1024,896]{1,0:T(8,128)(2,1)} %param.9) | data formatting | bytes 3670016 | tf_op args[1]
  21.8 3.8 %copy.16 = bf16[1024,896]{0,1:T(8,128)(2,1)} copy(bf16[1024,896]{1,0:T(8,128)(2,1)} %param.10) | data formatting | bytes 3670016 | tf_op args[2]
  25.6 3.6 %bitcast_select_fusion.1 = (bf16[1024,896]{0,1:T(8,128)(2,1)}, bf16[1024,896]{0,1:T(8,128)(2,1)}) fusion(bf16[1024,896]{0,1:T(8,128)(2,1)} %copy.16, pred[1024,7]{0,1:T(8,128)(4,1)S(1)} %bitcast.58, bf16[1024,896]{0,1:T(8,128)(2,1)S(1)} %copy.14, pred[1024,7]{0,1:T(8,128)(4,1)S(1)} %bitcast.60), kind=kLoop, calls=%fused_computation.1 | loop fusion | flops 1835008 | bytes 7354368 | tf_op jit(solution)/shard_map/jit(_where)/select_n | solution.py:68
  29.2 20.2 %all-to-all-done = bf16[16,64,1024]{2,1,0:T(8,128)(2,1)} async-done(((bf16[16,64,1024]{2,1,0:T(8,128)(2,1)}), bf16[16,64,1024]{2,1,0:T(8,128)(2,1)}, u32[]{:S(2)}, u32[]{:S(2)}) %all-to-all-start) | async-done | bytes 2097184 | tf_op jit(solution)/shard_map/all_to_all | solution.py:58
  49.5 9.7 %convolution_bitcast_fusion.1 = f32[1024,1792]{0,1:T(8,128)} fusion(bf16[1024,1024]{1,0:T(8,128)(2,1)} %bitcast.2, bf16[1024,896]{0,1:T(8,128)(2,1)} %get-tuple-element.20, bf16[1024,896]{0,1:T(8,128)(2,1)} %get-tuple-element.21), kind=kOutput, calls=%fused_computation.5 | convolution fusion | flops 3765436416 | bytes 13107200 | tf_op jit(solution)/shard_map/dot_general | solution.py:78
  59.1 0.0 reduce-scatter.3.cloned.1.call-update
  59.2 0.9 copy-done.6
  60.0 1.7 broadcast_in_dim.64
  61.7 3.9 %all-to-all-start.3 = ((bf16[16,64,1024]{2,1,0:T(8,128)(2,1)}), bf16[16,64,1024]{2,1,0:T(8,128)(2,1)S(1)}, u32[]{:S(2)}, u32[]{:S(2)}) async-start(bf16[16,64,1024]{2,1,0:T(8,128)(2,1)} %broadcast_in_dim.64), calls=%async_computation.4 | async-start | bytes 4194304 | tf_op jit(solution)/shard_map/all_to_all | solution.py:58
  65.7 0.0 reduce-scatter.5.cloned.1.call-start
  65.7 28.5 %all-to-all-done.3 = bf16[16,64,1024]{2,1,0:T(8,128)(2,1)S(1)} async-done(((bf16[16,64,1024]{2,1,0:T(8,128)(2,1)}), bf16[16,64,1024]{2,1,0:T(8,128)(2,1)S(1)}, u32[]{:S(2)}, u32[]{:S(2)}) %all-to-all-start.3) | async-done | bytes 2097184 | tf_op jit(solution)/shard_map/all_to_all | solution.py:58
  94.3 2.8 %broadcast_in_dim.62 = pred[896,8,128]{2,1,0:T(8,128)(4,1)S(1)} broadcast(pred[896,8]{1,0:T(8,128)(4,1)S(1)} %bitcast.57), dimensions={0,1} | broadcast | bytes 924672 | tf_op jit(solution)/shard_map/broadcast_in_dim | solution.py:10
  97.1 0.0 copy-start.4
  97.1 1.0 copy-done.4
  98.1 5.6 %fusion.4 = f32[1024,896]{0,1:T(8,128)} fusion(bf16[1024,1024]{1,0:T(8,128)(2,1)S(1)} %bitcast.48, bf16[896,1024]{1,0:T(8,128)(2,1)} %param.11, pred[112,8,8,128]{3,2,1,0:T(8,128)(4,1)S(1)} %bitcast.54), kind=kOutput, calls=%fused_computation.14 | convolution fusion | flops 1879965696 | bytes 8519680 | tf_op jit(solution)/shard_map/dot_general | solution.py:92
  103.7 0.0 reduce-scatter.5.cloned.1.call-update
  103.7 1.4 reduce-scatter.3.cloned.1.call-done
  105.1 1.3 fusion.7
  106.4 0.2 copy.17
  106.6 1.5 broadcast_in_dim.60
  108.1 6.2 %all-to-all-start.1 = ((bf16[8,128,896]{2,1,0:T(8,128)(2,1)}), bf16[8,128,896]{2,1,0:T(8,128)(2,1)S(1)}, u32[]{:S(2)}, u32[]{:S(2)}) async-start(bf16[8,128,896]{2,1,0:T(8,128)(2,1)} %broadcast_in_dim.60), calls=%async_computation.2 | async-start | bytes 3670016 | tf_op jit(solution)/shard_map/all_to_all | solution.py:44
  114.3 43.3 %reduce-scatter.5.cloned.1.call-done = f32[128,896]{0,1:T(8,128)} async-done(((f32[1024,896]{0,1:T(8,128)}), f32[128,896]{0,1:T(8,128)}) %reduce-scatter.5.cloned.1.call-update) | async-done | bytes 458768 | tf_op jit(solution)/shard_map/reduce_scatter | solution.py:32
  157.6 0.0 all-to-all-done.1
  157.6 1.6 multiply_convert_fusion.1
  159.1 0.8 pad_maximum_fusion.5
  159.9 0.0 all-gather.2.cloned.1.call-update
  160.0 5.4 %convolution_convert_fusion = bf16[1024,1024]{1,0:T(8,128)(2,1)} fusion(bf16[1024,896]{1,0:T(8,128)(2,1)S(1)} %bitcast.52, bf16[896,1024]{1,0:T(8,128)(2,1)} %param.11, pred[112,8,8,128]{3,2,1,0:T(8,128)(4,1)} %bitcast.55), kind=kOutput, calls=%fused_computation.13 | convolution fusion | flops 1881014272 | bytes 6684672 | tf_op jit(solution)/shard_map/dot_general | solution.py:85
  165.4 5.5 %all-to-all-start.2 = ((bf16[16,64,1024]{2,1,0:T(8,128)(2,1)}), bf16[16,64,1024]{2,1,0:T(8,128)(2,1)S(1)}, u32[]{:S(2)}, u32[]{:S(2)}) async-start(bf16[16,64,1024]{2,1,0:T(8,128)(2,1)} %bitcast.51), calls=%async_computation.3 | async-start | bytes 4194304 | tf_op jit(solution)/shard_map/all_to_all | solution.py:51
  170.9 23.4 %all-gather.2.cloned.1.call-done = bf16[1024,1792]{0,1:T(8,128)(2,1)} async-done(((bf16[128,1792]{0,1:T(8,128)(2,1)}), bf16[1024,1792]{0,1:T(8,128)(2,1)}) %all-gather.2.cloned.1.call-update) | async-done | bytes 3670032 | tf_op jit(solution)/shard_map/all_gather | solution.py:38
  194.3 8.5 %fusion.3 = bf16[1024,1024]{1,0:T(8,128)(2,1)} fusion(bf16[1024,1792]{0,1:T(8,128)(2,1)} %all-gather.2.cloned.1.call-done, bf16[1024,896]{0,1:T(8,128)(2,1)} %get-tuple-element.20, bf16[1024,896]{0,1:T(8,128)(2,1)} %get-tuple-element.21), kind=kOutput, calls=%fused_computation.12 | convolution fusion | flops 3766484992 | bytes 9437184 | tf_op jit(solution)/shard_map/dot_general | solution.py:105
  202.8 0.0 all-to-all-done.2
  202.9 1.3 copy-done
  204.2 6.7 %all-to-all-start.4 = ((bf16[16,64,1024]{2,1,0:T(8,128)(2,1)}), bf16[16,64,1024]{2,1,0:T(8,128)(2,1)S(1)}, u32[]{:S(2)}, u32[]{:S(2)}) async-start(bf16[16,64,1024]{2,1,0:T(8,128)(2,1)} %bitcast.50), calls=%async_computation.6 | async-start | bytes 4194304 | tf_op jit(solution)/shard_map/all_to_all | solution.py:51
  210.9 5.6 %select_convert_fusion = bf16[896,1024]{1,0:T(8,128)(2,1)} fusion(pred[112,8,8,128]{3,2,1,0:T(8,128)(4,1)S(1)} %bitcast.56, bf16[1024,896]{1,0:T(8,128)(2,1)} %bitcast.53, bf16[1024,1024]{1,0:T(8,128)(2,1)} %bitcast.49), kind=kOutput, calls=%fused_computation.9 | convolution fusion | flops 1880883200 | bytes 6684672 | tf_op jit(solution)/shard_map/dot_general | solution.py:88
  216.5 2.7 %reduce_sum.24 = bf16[64,1024]{1,0:T(8,128)(2,1)} reduce(bf16[16,64,1024]{2,1,0:T(8,128)(2,1)} %copy-done, bf16[]{:T(256)} %constant.2.clone.1), dimensions={0}, to_apply=%region_1.2 | reduce | flops 983040 | bytes 2228226 | tf_op jit(solution)/shard_map/reduce_sum | solution.py:52
  219.2 6.7 %convolution_bitcast_fusion = bf16[1024,1792]{0,1:T(8,128)(2,1)S(1)} fusion(bf16[1024,1792]{0,1:T(8,128)(2,1)} %all-gather.2.cloned.1.call-done, bf16[1024,1024]{1,0:T(8,128)(2,1)} %bitcast.2), kind=kOutput, calls=%fused_computation.4 | convolution fusion | flops 3758096384 | bytes 9437184 | tf_op jit(solution)/shard_map/dot_general | solution.py:97
  225.8 2.9 %fusion.1 = (bf16[1024,896]{0,1:T(8,128)(2,1)}, bf16[1024,896]{0,1:T(8,128)(2,1)}) fusion(bf16[1024,1792]{0,1:T(8,128)(2,1)S(1)} %convolution_bitcast_fusion, pred[1024,7]{0,1:T(8,128)(4,1)S(1)} %bitcast.59, pred[1024,7]{0,1:T(8,128)(4,1)S(1)} %bitcast.61), kind=kLoop, calls=%fused_computation.7 | loop fusion | flops 1835008 | bytes 7354368 | tf_op jit(solution)/shard_map/convert_element_type | solution.py:102
  228.8 3.8 %copy.20 = bf16[1024,896]{1,0:T(8,128)(2,1)} copy(bf16[1024,896]{0,1:T(8,128)(2,1)} %get-tuple-element.16) | data formatting | bytes 3670016
  232.6 3.8 %copy.19 = bf16[1024,896]{1,0:T(8,128)(2,1)} copy(bf16[1024,896]{0,1:T(8,128)(2,1)} %get-tuple-element.17) | data formatting | bytes 3670016
  236.4 7.1 %all-to-all-done.4 = bf16[16,64,1024]{2,1,0:T(8,128)(2,1)S(1)} async-done(((bf16[16,64,1024]{2,1,0:T(8,128)(2,1)}), bf16[16,64,1024]{2,1,0:T(8,128)(2,1)S(1)}, u32[]{:S(2)}, u32[]{:S(2)}) %all-to-all-start.4) | async-done | bytes 2097184 | tf_op jit(solution)/shard_map/all_to_all | solution.py:51
  243.5 1.1 reduce_sum.25
  (23 shorter events, 0.1 us)
Async XLA Ops:
  9.7 8.8 %copy-start.7 = (s32[8,7]{1,0:T(8,128)S(1)}, s32[8,7]{1,0:T(8,128)}, u32[]{:S(2)}) copy-start(s32[8,7]{1,0:T(8,128)} %param.12) | copy-start | bytes 676
  9.7 8.9 %copy-start.8 = (s32[8,7]{1,0:T(8,128)S(1)}, s32[8,7]{1,0:T(8,128)}, u32[]{:S(2)}) copy-start(s32[8,7]{1,0:T(8,128)} %param.13) | copy-start | bytes 676
  9.7 39.8 %all-to-all-start = ((bf16[16,64,1024]{2,1,0:T(8,128)(2,1)}), bf16[16,64,1024]{2,1,0:T(8,128)(2,1)}, u32[]{:S(2)}, u32[]{:S(2)}) async-start(bf16[16,64,1024]{2,1,0:T(8,128)(2,1)} %broadcast_in_dim.59), calls=%async_computation | async-start | bytes 4194304 | tf_op jit(solution)/shard_map/all_to_all | solution.py:58
  18.4 86.7 %reduce-scatter.3.cloned.1.call-start = ((), (), s32[]{:S(2)}) async-start(), calls=%async_computation.7 | async-start | bytes 8257536 | tf_op jit(solution)/shard_map/reduce_scatter | solution.py:32
  59.1 0.9 copy-start.6
  61.7 4.0 %copy-start.9 = (s32[7,8]{1,0:T(8,128)S(1)}, s32[7,8]{1,0:T(8,128)}, u32[]{:S(2)}) copy-start(s32[7,8]{1,0:T(8,128)} %param.14) | copy-start | bytes 676
  61.7 32.6 %all-to-all-start.3 = ((bf16[16,64,1024]{2,1,0:T(8,128)(2,1)}), bf16[16,64,1024]{2,1,0:T(8,128)(2,1)S(1)}, u32[]{:S(2)}, u32[]{:S(2)}) async-start(bf16[16,64,1024]{2,1,0:T(8,128)(2,1)} %broadcast_in_dim.64), calls=%async_computation.4 | async-start | bytes 4194304 | tf_op jit(solution)/shard_map/all_to_all | solution.py:58
  65.7 91.9 %reduce-scatter.5.cloned.1.call-start = ((), (), s32[]{:S(2)}) async-start(), calls=%async_computation.8 | async-start | bytes 4128768 | tf_op jit(solution)/shard_map/reduce_scatter | solution.py:32
  94.3 9.4 %copy-start.2 = (bf16[16,64,1024]{2,1,0:T(8,128)(2,1)}, bf16[16,64,1024]{2,1,0:T(8,128)(2,1)S(1)}, u32[]{:S(2)}) copy-start(bf16[16,64,1024]{2,1,0:T(8,128)(2,1)S(1)} %all-to-all-done.3) | copy-start | bytes 6291460
  97.1 1.0 copy-start.4
  108.0 49.5 %copy-start.1 = (f32[128,1792]{0,1:T(8,128)S(1)}, f32[128,1792]{0,1:T(8,128)}, u32[]{:S(2)}) copy-start(f32[128,1792]{0,1:T(8,128)} %reduce-scatter.3.cloned.1.call-done) | copy-start | bytes 2752516
  108.1 49.5 %all-to-all-start.1 = ((bf16[8,128,896]{2,1,0:T(8,128)(2,1)}), bf16[8,128,896]{2,1,0:T(8,128)(2,1)S(1)}, u32[]{:S(2)}, u32[]{:S(2)}) async-start(bf16[8,128,896]{2,1,0:T(8,128)(2,1)} %broadcast_in_dim.60), calls=%async_computation.2 | async-start | bytes 3670016 | tf_op jit(solution)/shard_map/all_to_all | solution.py:44
  114.3 80.0 %all-gather.2.cloned.1.call-start = ((), (), s32[]{:S(2)}) async-start(), calls=%async_computation.9 | async-start | bytes 4128768 | tf_op jit(solution)/shard_map/all_gather | solution.py:38
  157.6 7.8 %copy-start.3 = (bf16[8,128,896]{2,1,0:T(8,128)(2,1)}, bf16[8,128,896]{2,1,0:T(8,128)(2,1)S(1)}, u32[]{:S(2)}) copy-start(bf16[8,128,896]{2,1,0:T(8,128)(2,1)S(1)} %all-to-all-done.1) | copy-start | bytes 5505028
  165.4 37.4 %all-to-all-start.2 = ((bf16[16,64,1024]{2,1,0:T(8,128)(2,1)}), bf16[16,64,1024]{2,1,0:T(8,128)(2,1)S(1)}, u32[]{:S(2)}, u32[]{:S(2)}) async-start(bf16[16,64,1024]{2,1,0:T(8,128)(2,1)} %bitcast.51), calls=%async_computation.3 | async-start | bytes 4194304 | tf_op jit(solution)/shard_map/all_to_all | solution.py:51
  202.8 1.3 copy-start
  202.8 8.0 %copy-start.5 = (pred[896,8,128]{2,1,0:T(8,128)(4,1)S(1)}, pred[896,8,128]{2,1,0:T(8,128)(4,1)}, u32[]{:S(2)}) copy-start(pred[896,8,128]{2,1,0:T(8,128)(4,1)} %copy-done.4) | copy-start | bytes 2752516
  204.2 39.3 %all-to-all-start.4 = ((bf16[16,64,1024]{2,1,0:T(8,128)(2,1)}), bf16[16,64,1024]{2,1,0:T(8,128)(2,1)S(1)}, u32[]{:S(2)}, u32[]{:S(2)}) async-start(bf16[16,64,1024]{2,1,0:T(8,128)(2,1)} %bitcast.50), calls=%async_computation.6 | async-start | bytes 4194304 | tf_op jit(solution)/shard_map/all_to_all | solution.py:51
Sparse Core Ops, SparseCore 0:
  59.3 45.7 reduce-scatter.2
  107.5 49.9 reduce-scatter.4
  160.1 34.1 all-gather.1

commit v6 on v5

--- a/solution.py
+++ b/solution.py
@@ -36,6 +36,15 @@
 
 def row_gather(block):
     return lax.all_gather(block, "row", axis=0, tiled=True)
+
+
+def row_sums_direct(full):
+    parts = lax.axis_size("row")
+    rows = full.shape[0] // parts
+    pieces = lax.all_to_all(
+        full.astype(jnp.bfloat16).reshape((parts, rows) + full.shape[1:]), "row", 0, 0
+    )
+    return jnp.sum(pieces.astype(jnp.float32), axis=0)
 
 
 def row_gather_direct(block):
@@ -79,7 +88,7 @@
     sums = row_sums(lambda start, count: hidden, split_rows)
     grad_out, _ = lax.optimization_barrier((grad_out, hidden))
     grad_all = group_gather(grad_out)
-    act_all = row_gather_direct(swiglu(sums))
+    act_all = row_gather(swiglu(sums))
 
     def out_term(start, count):
         return jnp.dot(act_all, w_down, preferred_element_type=jnp.float32)
@@ -91,7 +100,7 @@
     def act_term(start, count):
         return lax.dot_general(grad_all, w_down, outer, preferred_element_type=jnp.float32)
 
-    grad_act = row_sums(act_term, split_rows)
+    grad_act = row_sums_direct(act_term(0, split_rows))
     held_sums, grad_act, _ = lax.optimization_barrier((sums, grad_act, act_all))
     grads_all = row_gather(swiglu_back(held_sums, grad_act))
     grad_both = lax.dot_general(x_all, grads_all, inner, preferred_element_type=jnp.float32)

time: 252 us -> 241 us (0.956)
  waiting for transfers between devices: 124 us -> 89.3 us
  blocking collectives: 0 us -> 34.4 us
  starting transfers between devices: 31.2 us -> 24.2 us
    all_to_all x0 -> x1, blocking collectives: none -> 34.4 us  [row_sums_direct(): lax.all_to_all(full.astype(jnp.bfloat16).reshape((parts, rows) + full.sha...]
    all_to_all x2, waiting for transfers between devices: 48.8 us -> 20.2 us  [group_gather(): pieces = lax.all_to_all(copies, ('col', 'depth'), 0, 0)]
    all_to_all x1 -> x0, starting transfers between devices: 6.21 us -> none  [row_gather_direct(): pieces = lax.all_to_all(copies, 'row', 0, 0)]
    reduce_scatter x2 -> x1, waiting for transfers between devices: 44.7 us -> 39.5 us  [row_sums(): lax.psum_scatter(term(jnp.int32(0), lax.axis_size('row') * rows), 'row',...]
    all_gather x1 -> x2, waiting for transfers between devices: 23.4 us -> 20.8 us  [row_gather(): return lax.all_gather(block, 'row', axis=0, tiled=True)]
    unnamed x28 -> x22, local copies, waits for them, and re-layouts: 17.6 us -> 17.4 us
  transfers between devices with their start and end apart: 8 -> 7, of which waited for: 6 -> 5; matrix products, arithmetic and copies ran while one was open for 25% -> 25% of each run, Pallas kernels for 0% -> 0%
where the time goes in v6:
time: 241 us; the launch traced here: 240 us
  waiting for transfers between devices  89.3 us (37%)
  matrix products  40.1 us (17%)
  blocking collectives  34.4 us (14%)
  local copies, waits for them, and re-layouts  24.7 us (10%)
  starting transfers between devices  24.2 us (10%)
  between operations  13.9 us (6%)
  other arithmetic  13.6 us (6%)
    reduce_scatter x1, waiting for transfers between devices, row_sums(): lax.psum_scatter(term(jnp.int32(0), lax.axis_size('row') * rows), 'row',...  39.5 us
    all_to_all x1, blocking collectives, row_sums_direct(): lax.all_to_all(full.astype(jnp.bfloat16).reshape((parts, rows) + full.sha...  34.4 us
    all_gather x2, waiting for transfers between devices, row_gather(): return lax.all_gather(block, 'row', axis=0, tiled=True)  20.8 us
    all_to_all x2, waiting for transfers between devices, group_gather(): pieces = lax.all_to_all(copies, ('col', 'depth'), 0, 0)  20.2 us
    unnamed x22, local copies, waits for them, and re-layouts  17.4 us
    all_to_all x2, starting transfers between devices, group_gather(): pieces = lax.all_to_all(copies, ('col', 'depth'), 0, 0)  12.7 us
    all_to_all x2, starting transfers between devices, group_sums(): lax.all_to_all(full.reshape((parts, rows) + full.shape[1:]), ('col', 'dep...  11.4 us
    dot_general x1, matrix products, local(): hidden = jnp.dot(x_all, w_both, preferred_element_type=jnp.float32)  9.7 us
  transfers between devices with their start and end apart: 7, of which 5 were waited for; matrix products, arithmetic and copies ran while one was open for 25% of the time, Pallas kernels for 0%

profile of v6, /device:TPU:1, one launch (start us, length us, event | category | flops | bytes accessed | tf_op | source)
XLA Modules:
  0.0 240.2 jit_solution(8354290432766855114)
XLA Ops:
  7.2 2.5 %broadcast_in_dim.53 = bf16[16,64,1024]{2,1,0:T(8,128)(2,1)} broadcast(bf16[64,1024]{1,0:T(8,128)(2,1)} %param.8), dimensions={1,2} | broadcast | bytes 2228224 | tf_op jit(solution)/shard_map/broadcast_in_dim | solution.py:66
  9.7 8.8 %all-to-all-start = ((bf16[16,64,1024]{2,1,0:T(8,128)(2,1)}), bf16[16,64,1024]{2,1,0:T(8,128)(2,1)}, u32[]{:S(2)}, u32[]{:S(2)}) async-start(bf16[16,64,1024]{2,1,0:T(8,128)(2,1)} %broadcast_in_dim.53), calls=%async_computation | async-start | bytes 4194304 | tf_op jit(solution)/shard_map/all_to_all | solution.py:67
  18.4 0.0 reduce-scatter.2.cloned.1.call-start
  18.5 0.0 copy-done.4
  18.5 0.1 copy.19
  18.6 0.1 copy.21
  18.7 0.1 broadcast_bitcast_fusion
  18.8 0.1 broadcast_bitcast_fusion.1
  18.9 2.9 %copy.20 = bf16[1024,896]{0,1:T(8,128)(2,1)S(1)} copy(bf16[1024,896]{1,0:T(8,128)(2,1)} %param.9) | data formatting | bytes 3670016 | tf_op args[1]
  21.8 3.8 %copy.22 = bf16[1024,896]{0,1:T(8,128)(2,1)} copy(bf16[1024,896]{1,0:T(8,128)(2,1)} %param.10) | data formatting | bytes 3670016 | tf_op args[2]
  25.6 3.6 %bitcast_select_fusion.1 = (bf16[1024,896]{0,1:T(8,128)(2,1)}, bf16[1024,896]{0,1:T(8,128)(2,1)}) fusion(bf16[1024,896]{0,1:T(8,128)(2,1)} %copy.22, pred[1024,7]{0,1:T(8,128)(4,1)S(1)} %bitcast.57, bf16[1024,896]{0,1:T(8,128)(2,1)S(1)} %copy.20, pred[1024,7]{0,1:T(8,128)(4,1)S(1)} %bitcast.59), kind=kLoop, calls=%fused_computation.1 | loop fusion | flops 1835008 | bytes 7354368 | tf_op jit(solution)/shard_map/jit(_where)/select_n | solution.py:77
  29.2 20.2 %all-to-all-done = bf16[16,64,1024]{2,1,0:T(8,128)(2,1)} async-done(((bf16[16,64,1024]{2,1,0:T(8,128)(2,1)}), bf16[16,64,1024]{2,1,0:T(8,128)(2,1)}, u32[]{:S(2)}, u32[]{:S(2)}) %all-to-all-start) | async-done | bytes 2097184 | tf_op jit(solution)/shard_map/all_to_all | solution.py:67
  49.4 9.7 %convolution_bitcast_fusion.1 = f32[1024,1792]{0,1:T(8,128)} fusion(bf16[1024,1024]{1,0:T(8,128)(2,1)} %bitcast.2, bf16[1024,896]{0,1:T(8,128)(2,1)} %get-tuple-element.25, bf16[1024,896]{0,1:T(8,128)(2,1)} %get-tuple-element.26), kind=kOutput, calls=%fused_computation.5 | convolution fusion | flops 3765436416 | bytes 13107200 | tf_op jit(solution)/shard_map/dot_general | solution.py:87
  59.1 0.0 reduce-scatter.2.cloned.1.call-update
  59.2 0.9 copy-done.3
  60.0 1.6 broadcast_in_dim.57
  61.6 3.9 %all-to-all-start.2 = ((bf16[16,64,1024]{2,1,0:T(8,128)(2,1)}), bf16[16,64,1024]{2,1,0:T(8,128)(2,1)S(1)}, u32[]{:S(2)}, u32[]{:S(2)}) async-start(bf16[16,64,1024]{2,1,0:T(8,128)(2,1)} %broadcast_in_dim.57), calls=%async_computation.3 | async-start | bytes 4194304 | tf_op jit(solution)/shard_map/all_to_all | solution.py:67
  65.6 0.0 all-gather.3.cloned.1.call-start
  65.6 39.5 %reduce-scatter.2.cloned.1.call-done = f32[128,1792]{0,1:T(8,128)} async-done(((f32[1024,1792]{0,1:T(8,128)}), f32[128,1792]{0,1:T(8,128)}) %reduce-scatter.2.cloned.1.call-update) | async-done | bytes 917520 | tf_op jit(solution)/shard_map/reduce_scatter | solution.py:32
  105.2 2.0 fusion.6
  107.1 0.0 all-gather.3.cloned.1.call-update
  107.2 0.0 all-gather.5.cloned.1.call-start
  107.2 0.0 all-to-all-done.2
  107.3 2.8 %broadcast_in_dim.55 = pred[896,8,128]{2,1,0:T(8,128)(4,1)S(1)} broadcast(pred[896,8]{1,0:T(8,128)(4,1)S(1)} %bitcast.56), dimensions={0,1} | broadcast | bytes 924672 | tf_op jit(solution)/shard_map/broadcast_in_dim | solution.py:10
  110.1 3.9 %convolution_convert_fusion.1 = bf16[1024,896]{1,0:T(8,128)(2,1)S(1)} fusion(bf16[1024,1024]{1,0:T(8,128)(2,1)S(1)} %bitcast.48, bf16[896,1024]{1,0:T(8,128)(2,1)} %param.11, pred[112,8,8,128]{3,2,1,0:T(8,128)(4,1)S(1)} %bitcast.53), kind=kOutput, calls=%fused_computation.15 | convolution fusion | flops 1880883200 | bytes 6684672 | tf_op jit(solution)/shard_map/dot_general | solution.py:101
  114.0 34.4 %all_to_all.25 = bf16[8,128,896]{2,1,0:T(8,128)(2,1)S(1)} all-to-all(bf16[8,128,896]{2,1,0:T(8,128)(2,1)S(1)} %bitcast.52), channel_id=1, replica_groups=mesh['row'=8,'col'=4,'depth'=4] {'row'}, dimensions={0} | all-to-all | bytes 3670016 | tf_op jit(solution)/shard_map/all_to_all | solution.py:44
  148.4 0.3 convert_reduce_fusion
  148.6 0.0 all-gather.3.cloned.1.call-done
  148.6 0.2 copy.23
  148.8 0.7 copy-done.1
  149.5 0.2 multiply_convert_fusion.1
  149.8 0.8 pad_maximum_fusion.5
  150.6 0.0 all-gather.5.cloned.1.call-update
  150.6 5.9 %convolution_convert_fusion = bf16[1024,1024]{1,0:T(8,128)(2,1)} fusion(bf16[1024,896]{0,1:T(8,128)(2,1)} %all-gather.3.cloned.1.call-done, bf16[896,1024]{1,0:T(8,128)(2,1)} %param.11, pred[112,8,8,128]{3,2,1,0:T(8,128)(4,1)S(1)} %bitcast.54), kind=kOutput, calls=%fused_computation.14 | convolution fusion | flops 1881014272 | bytes 6684672 | tf_op jit(solution)/shard_map/dot_general | solution.py:94
  156.5 6.7 %all-to-all-start.1 = ((bf16[16,64,1024]{2,1,0:T(8,128)(2,1)}), bf16[16,64,1024]{2,1,0:T(8,128)(2,1)S(1)}, u32[]{:S(2)}, u32[]{:S(2)}) async-start(bf16[16,64,1024]{2,1,0:T(8,128)(2,1)} %bitcast.51), calls=%async_computation.2 | async-start | bytes 4194304 | tf_op jit(solution)/shard_map/all_to_all | solution.py:60
  163.2 20.7 %all-gather.5.cloned.1.call-done = bf16[1024,1792]{0,1:T(8,128)(2,1)} async-done(((bf16[128,1792]{0,1:T(8,128)(2,1)}), bf16[1024,1792]{0,1:T(8,128)(2,1)}) %all-gather.5.cloned.1.call-update) | async-done | bytes 3670032 | tf_op jit(solution)/shard_map/all_gather | solution.py:38
  183.9 8.5 %fusion.3 = bf16[1024,1024]{1,0:T(8,128)(2,1)} fusion(bf16[1024,1792]{0,1:T(8,128)(2,1)} %all-gather.5.cloned.1.call-done, bf16[1024,896]{0,1:T(8,128)(2,1)} %get-tuple-element.25, bf16[1024,896]{0,1:T(8,128)(2,1)} %get-tuple-element.26), kind=kOutput, calls=%fused_computation.13 | convolution fusion | flops 3766484992 | bytes 9437184 | tf_op jit(solution)/shard_map/dot_general | solution.py:114
  192.4 2.0 all-to-all-done.1
  194.4 1.4 copy-done
  195.8 4.7 %all-to-all-start.4 = ((bf16[16,64,1024]{2,1,0:T(8,128)(2,1)}), bf16[16,64,1024]{2,1,0:T(8,128)(2,1)S(1)}, u32[]{:S(2)}, u32[]{:S(2)}) async-start(bf16[16,64,1024]{2,1,0:T(8,128)(2,1)} %bitcast.50), calls=%async_computation.5 | async-start | bytes 4194304 | tf_op jit(solution)/shard_map/all_to_all | solution.py:60
  200.5 5.5 %select_convert_fusion = bf16[896,1024]{1,0:T(8,128)(2,1)} fusion(pred[112,8,8,128]{3,2,1,0:T(8,128)(4,1)S(1)} %bitcast.55, bf16[1024,896]{0,1:T(8,128)(2,1)} %all-gather.3.cloned.1.call-done, bf16[1024,1024]{1,0:T(8,128)(2,1)} %bitcast.49), kind=kOutput, calls=%fused_computation.9 | convolution fusion | flops 1880883200 | bytes 6684672 | tf_op jit(solution)/shard_map/dot_general | solution.py:97
  206.0 2.7 %reduce_sum.33 = bf16[64,1024]{1,0:T(8,128)(2,1)} reduce(bf16[16,64,1024]{2,1,0:T(8,128)(2,1)} %copy-done, bf16[]{:T(256)} %constant.2.clone.1), dimensions={0}, to_apply=%region_1.2 | reduce | flops 983040 | bytes 2228226 | tf_op jit(solution)/shard_map/reduce_sum | solution.py:61
  208.7 6.7 %convolution_bitcast_fusion = bf16[1024,1792]{0,1:T(8,128)(2,1)S(1)} fusion(bf16[1024,1792]{0,1:T(8,128)(2,1)} %all-gather.5.cloned.1.call-done, bf16[1024,1024]{1,0:T(8,128)(2,1)} %bitcast.2), kind=kOutput, calls=%fused_computation.4 | convolution fusion | flops 3758096384 | bytes 9437184 | tf_op jit(solution)/shard_map/dot_general | solution.py:106
  215.3 3.0 %fusion.1 = (bf16[1024,896]{0,1:T(8,128)(2,1)}, bf16[1024,896]{0,1:T(8,128)(2,1)}) fusion(bf16[1024,1792]{0,1:T(8,128)(2,1)S(1)} %convolution_bitcast_fusion, pred[1024,7]{0,1:T(8,128)(4,1)S(1)} %bitcast.58, pred[1024,7]{0,1:T(8,128)(4,1)S(1)} %bitcast.60), kind=kLoop, calls=%fused_computation.7 | loop fusion | flops 1835008 | bytes 7354368 | tf_op jit(solution)/shard_map/convert_element_type | solution.py:111
  218.3 3.8 %copy.26 = bf16[1024,896]{1,0:T(8,128)(2,1)} copy(bf16[1024,896]{0,1:T(8,128)(2,1)} %get-tuple-element.21) | data formatting | bytes 3670016
  222.1 3.8 %copy.25 = bf16[1024,896]{1,0:T(8,128)(2,1)} copy(bf16[1024,896]{0,1:T(8,128)(2,1)} %get-tuple-element.22) | data formatting | bytes 3670016
  225.9 6.7 %all-to-all-done.4 = bf16[16,64,1024]{2,1,0:T(8,128)(2,1)S(1)} async-done(((bf16[16,64,1024]{2,1,0:T(8,128)(2,1)}), bf16[16,64,1024]{2,1,0:T(8,128)(2,1)S(1)}, u32[]{:S(2)}, u32[]{:S(2)}) %all-to-all-start.4) | async-done | bytes 2097184 | tf_op jit(solution)/shard_map/all_to_all | solution.py:60
  232.6 1.1 reduce_sum.35
  (16 shorter events, 0.1 us)
Async XLA Ops:
  9.6 8.8 %copy-start.4 = (s32[8,7]{1,0:T(8,128)S(1)}, s32[8,7]{1,0:T(8,128)}, u32[]{:S(2)}) copy-start(s32[8,7]{1,0:T(8,128)} %param.12) | copy-start | bytes 676
  9.7 8.9 %copy-start.5 = (s32[8,7]{1,0:T(8,128)S(1)}, s32[8,7]{1,0:T(8,128)}, u32[]{:S(2)}) copy-start(s32[8,7]{1,0:T(8,128)} %param.13) | copy-start | bytes 676
  9.7 39.8 %all-to-all-start = ((bf16[16,64,1024]{2,1,0:T(8,128)(2,1)}), bf16[16,64,1024]{2,1,0:T(8,128)(2,1)}, u32[]{:S(2)}, u32[]{:S(2)}) async-start(bf16[16,64,1024]{2,1,0:T(8,128)(2,1)} %broadcast_in_dim.53), calls=%async_computation | async-start | bytes 4194304 | tf_op jit(solution)/shard_map/all_to_all | solution.py:67
  18.4 86.7 %reduce-scatter.2.cloned.1.call-start = ((), (), s32[]{:S(2)}) async-start(), calls=%async_computation.6 | async-start | bytes 8257536 | tf_op jit(solution)/shard_map/reduce_scatter | solution.py:32
  59.1 0.9 copy-start.3
  61.6 45.6 %copy-start.6 = (s32[7,8]{1,0:T(8,128)S(1)}, s32[7,8]{1,0:T(8,128)}, u32[]{:S(2)}) copy-start(s32[7,8]{1,0:T(8,128)} %param.14) | copy-start | bytes 676
  61.6 45.6 %all-to-all-start.2 = ((bf16[16,64,1024]{2,1,0:T(8,128)(2,1)}), bf16[16,64,1024]{2,1,0:T(8,128)(2,1)S(1)}, u32[]{:S(2)}, u32[]{:S(2)}) async-start(bf16[16,64,1024]{2,1,0:T(8,128)(2,1)} %broadcast_in_dim.57), calls=%async_computation.3 | async-start | bytes 4194304 | tf_op jit(solution)/shard_map/all_to_all | solution.py:67
  65.6 83.0 %all-gather.3.cloned.1.call-start = ((), (), s32[]{:S(2)}) async-start(), calls=%async_computation.7 | async-start | bytes 2064384 | tf_op jit(solution)/shard_map/all_gather | solution.py:38
  107.2 76.8 %all-gather.5.cloned.1.call-start = ((), (), s32[]{:S(2)}) async-start(), calls=%async_computation.8 | async-start | bytes 4128768 | tf_op jit(solution)/shard_map/all_gather | solution.py:38
  107.2 6.7 %copy-start.2 = (bf16[16,64,1024]{2,1,0:T(8,128)(2,1)}, bf16[16,64,1024]{2,1,0:T(8,128)(2,1)S(1)}, u32[]{:S(2)}) copy-start(bf16[16,64,1024]{2,1,0:T(8,128)(2,1)S(1)} %all-to-all-done.2) | copy-start | bytes 6291460
  148.3 1.2 copy-start.1
  156.5 38.0 %all-to-all-start.1 = ((bf16[16,64,1024]{2,1,0:T(8,128)(2,1)}), bf16[16,64,1024]{2,1,0:T(8,128)(2,1)S(1)}, u32[]{:S(2)}, u32[]{:S(2)}) async-start(bf16[16,64,1024]{2,1,0:T(8,128)(2,1)} %bitcast.51), calls=%async_computation.2 | async-start | bytes 4194304 | tf_op jit(solution)/shard_map/all_to_all | solution.py:60
  194.4 1.4 copy-start
  195.8 36.7 %all-to-all-start.4 = ((bf16[16,64,1024]{2,1,0:T(8,128)(2,1)}), bf16[16,64,1024]{2,1,0:T(8,128)(2,1)S(1)}, u32[]{:S(2)}, u32[]{:S(2)}) async-start(bf16[16,64,1024]{2,1,0:T(8,128)(2,1)} %bitcast.50), calls=%async_computation.5 | async-start | bytes 4194304 | tf_op jit(solution)/shard_map/all_to_all | solution.py:60
Sparse Core Ops, SparseCore 0:
  59.3 45.8 reduce-scatter.1
  107.4 38.9 all-gather.2
  150.7 33.1 all-gather.4

commit v7 on v6

--- a/solution.py
+++ b/solution.py
@@ -88,7 +88,9 @@
     sums = row_sums(lambda start, count: hidden, split_rows)
     grad_out, _ = lax.optimization_barrier((grad_out, hidden))
     grad_all = group_gather(grad_out)
-    act_all = row_gather(swiglu(sums))
+    act_partial = lax.dot_general(grad_all, w_down, outer, preferred_element_type=jnp.float32)
+    act_sums, act_partial = lax.optimization_barrier((sums, act_partial))
+    act_all = row_gather(swiglu(act_sums))
 
     def out_term(start, count):
         return jnp.dot(act_all, w_down, preferred_element_type=jnp.float32)
@@ -97,10 +99,7 @@
     grad_down = lax.dot_general(act_all, grad_all, inner, preferred_element_type=jnp.float32)
     grad_down_weight = jnp.where(keep_down, grad_down, jnp.float32(0.0)).astype(jnp.bfloat16)
 
-    def act_term(start, count):
-        return lax.dot_general(grad_all, w_down, outer, preferred_element_type=jnp.float32)
-
-    grad_act = row_sums_direct(act_term(0, split_rows))
+    grad_act = row_sums_direct(act_partial)
     held_sums, grad_act, _ = lax.optimization_barrier((sums, grad_act, act_all))
     grads_all = row_gather(swiglu_back(held_sums, grad_act))
     grad_both = lax.dot_general(x_all, grads_all, inner, preferred_element_type=jnp.float32)

time: 241 us -> 238 us (0.988)
  waiting for transfers between devices: 89.3 us -> 84.5 us
    reduce_scatter x1, waiting for transfers between devices: 39.5 us -> 2.95 us  [row_sums(): lax.psum_scatter(term(jnp.int32(0), lax.axis_size('row') * rows), 'row',...]
    all_to_all x2, waiting for transfers between devices: 20.2 us -> 48.8 us  [group_gather(): pieces = lax.all_to_all(copies, ('col', 'depth'), 0, 0)]
    all_gather x2, waiting for transfers between devices: 20.8 us -> 23.9 us  [row_gather(): return lax.all_gather(block, 'row', axis=0, tiled=True)]
  transfers between devices with their start and end apart: 7 -> 7, of which waited for: 5 -> 7; matrix products, arithmetic and copies ran while one was open for 25% -> 25% of each run, Pallas kernels for 0% -> 0%
where the time goes in v7:
time: 238 us; the launch traced here: 237 us
  waiting for transfers between devices  84.5 us (36%)
  matrix products  41.4 us (17%)
  blocking collectives  35.3 us (15%)
  starting transfers between devices  24.7 us (10%)
  local copies, waits for them, and re-layouts  24 us (10%)
  between operations  13.9 us (6%)
  other arithmetic  13.6 us (6%)
    all_to_all x2, waiting for transfers between devices, group_gather(): pieces = lax.all_to_all(copies, ('col', 'depth'), 0, 0)  48.8 us
    all_to_all x1, blocking collectives, row_sums_direct(): lax.all_to_all(full.astype(jnp.bfloat16).reshape((parts, rows) + full.sha...  35.3 us
    all_gather x2, waiting for transfers between devices, row_gather(): return lax.all_gather(block, 'row', axis=0, tiled=True)  23.9 us
    unnamed x22, local copies, waits for them, and re-layouts  16.7 us
    all_to_all x2, starting transfers between devices, group_gather(): pieces = lax.all_to_all(copies, ('col', 'depth'), 0, 0)  12.7 us
    all_to_all x2, starting transfers between devices, group_sums(): lax.all_to_all(full.reshape((parts, rows) + full.shape[1:]), ('col', 'dep...  11.8 us
    dot_general x1, matrix products, local(): hidden = jnp.dot(x_all, w_both, preferred_element_type=jnp.float32)  9.66 us
    all_to_all x2, waiting for transfers between devices, group_sums(): lax.all_to_all(full.reshape((parts, rows) + full.shape[1:]), ('col', 'dep...  8.81 us
  transfers between devices with their start and end apart: 7, of which 7 were waited for; matrix products, arithmetic and copies ran while one was open for 25% of the time, Pallas kernels for 0%

profile of v7, /device:TPU:1, one launch (start us, length us, event | category | flops | bytes accessed | tf_op | source)
XLA Modules:
  0.0 237.3 jit_solution(7514739238827438388)
XLA Ops:
  7.2 2.5 %broadcast_in_dim.53 = bf16[16,64,1024]{2,1,0:T(8,128)(2,1)} broadcast(bf16[64,1024]{1,0:T(8,128)(2,1)} %param.8), dimensions={1,2} | broadcast | bytes 2228224 | tf_op jit(solution)/shard_map/broadcast_in_dim | solution.py:66
  9.7 8.8 %all-to-all-start = ((bf16[16,64,1024]{2,1,0:T(8,128)(2,1)}), bf16[16,64,1024]{2,1,0:T(8,128)(2,1)}, u32[]{:S(2)}, u32[]{:S(2)}) async-start(bf16[16,64,1024]{2,1,0:T(8,128)(2,1)} %broadcast_in_dim.53), calls=%async_computation | async-start | bytes 4194304 | tf_op jit(solution)/shard_map/all_to_all | solution.py:67
  18.4 0.0 reduce-scatter.2.cloned.1.call-start
  18.5 0.1 copy.19
  18.6 0.0 copy-done.5
  18.6 0.1 copy.21
  18.7 0.1 broadcast_bitcast_fusion
  18.8 0.1 broadcast_bitcast_fusion.1
  18.9 2.9 %copy.20 = bf16[1024,896]{0,1:T(8,128)(2,1)S(1)} copy(bf16[1024,896]{1,0:T(8,128)(2,1)} %param.9) | data formatting | bytes 3670016 | tf_op args[1]
  21.8 3.8 %copy.22 = bf16[1024,896]{0,1:T(8,128)(2,1)} copy(bf16[1024,896]{1,0:T(8,128)(2,1)} %param.10) | data formatting | bytes 3670016 | tf_op args[2]
  25.6 3.6 %bitcast_select_fusion.1 = (bf16[1024,896]{0,1:T(8,128)(2,1)}, bf16[1024,896]{0,1:T(8,128)(2,1)}) fusion(bf16[1024,896]{0,1:T(8,128)(2,1)} %copy.22, pred[1024,7]{0,1:T(8,128)(4,1)S(1)} %bitcast.57, bf16[1024,896]{0,1:T(8,128)(2,1)S(1)} %copy.20, pred[1024,7]{0,1:T(8,128)(4,1)S(1)} %bitcast.59), kind=kLoop, calls=%fused_computation.1 | loop fusion | flops 1835008 | bytes 7354368 | tf_op jit(solution)/shard_map/jit(_where)/select_n | solution.py:77
  29.2 20.2 %all-to-all-done = bf16[16,64,1024]{2,1,0:T(8,128)(2,1)} async-done(((bf16[16,64,1024]{2,1,0:T(8,128)(2,1)}), bf16[16,64,1024]{2,1,0:T(8,128)(2,1)}, u32[]{:S(2)}, u32[]{:S(2)}) %all-to-all-start) | async-done | bytes 2097184 | tf_op jit(solution)/shard_map/all_to_all | solution.py:67
  49.4 9.7 %convolution_bitcast_fusion.1 = f32[1024,1792]{0,1:T(8,128)} fusion(bf16[1024,1024]{1,0:T(8,128)(2,1)} %bitcast.2, bf16[1024,896]{0,1:T(8,128)(2,1)} %get-tuple-element.29, bf16[1024,896]{0,1:T(8,128)(2,1)} %get-tuple-element.30), kind=kOutput, calls=%fused_computation.5 | convolution fusion | flops 3765436416 | bytes 13107200 | tf_op jit(solution)/shard_map/dot_general | solution.py:87
  59.1 0.0 reduce-scatter.2.cloned.1.call-update
  59.1 0.9 copy-done.3
  60.0 1.6 broadcast_in_dim.54
  61.6 3.9 %all-to-all-start.1 = ((bf16[16,64,1024]{2,1,0:T(8,128)(2,1)}), bf16[16,64,1024]{2,1,0:T(8,128)(2,1)S(1)}, u32[]{:S(2)}, u32[]{:S(2)}) async-start(bf16[16,64,1024]{2,1,0:T(8,128)(2,1)} %broadcast_in_dim.54), calls=%async_computation.2 | async-start | bytes 4194304 | tf_op jit(solution)/shard_map/all_to_all | solution.py:67
  65.5 0.0 all-gather.3.cloned.1.call-start
  65.6 28.5 %all-to-all-done.1 = bf16[16,64,1024]{2,1,0:T(8,128)(2,1)S(1)} async-done(((bf16[16,64,1024]{2,1,0:T(8,128)(2,1)}), bf16[16,64,1024]{2,1,0:T(8,128)(2,1)S(1)}, u32[]{:S(2)}, u32[]{:S(2)}) %all-to-all-start.1) | async-done | bytes 2097184 | tf_op jit(solution)/shard_map/all_to_all | solution.py:67
  94.2 2.8 %broadcast_in_dim.56 = pred[896,8,128]{2,1,0:T(8,128)(4,1)S(1)} broadcast(pred[896,8]{1,0:T(8,128)(4,1)S(1)} %bitcast.56), dimensions={0,1} | broadcast | bytes 924672 | tf_op jit(solution)/shard_map/broadcast_in_dim | solution.py:10
  97.0 5.2 %fusion.4 = bf16[1024,896]{1,0:T(8,128)(2,1)} fusion(bf16[1024,1024]{1,0:T(8,128)(2,1)S(1)} %bitcast.48, bf16[896,1024]{1,0:T(8,128)(2,1)} %param.11, pred[112,8,8,128]{3,2,1,0:T(8,128)(4,1)S(1)} %bitcast.53), kind=kOutput, calls=%fused_computation.15 | convolution fusion | flops 1879965696 | bytes 6684672 | tf_op jit(solution)/shard_map/dot_general | solution.py:91
  102.2 3.0 %reduce-scatter.2.cloned.1.call-done = f32[128,1792]{0,1:T(8,128)} async-done(((f32[1024,1792]{0,1:T(8,128)}), f32[128,1792]{0,1:T(8,128)}) %reduce-scatter.2.cloned.1.call-update) | async-done | bytes 917520 | tf_op jit(solution)/shard_map/reduce_scatter | solution.py:32
  105.1 2.0 multiply_convert_fusion.2
  107.1 0.0 all-gather.3.cloned.1.call-update
  107.1 0.0 all-gather.5.cloned.1.call-start
  107.2 35.3 %all_to_all.25 = bf16[8,128,896]{2,1,0:T(8,128)(2,1)S(1)} all-to-all(bf16[8,128,896]{2,1,0:T(8,128)(2,1)} %bitcast.52), channel_id=1, replica_groups=mesh['row'=8,'col'=4,'depth'=4] {'row'}, dimensions={0} | all-to-all | bytes 3670016 | tf_op jit(solution)/shard_map/all_to_all | solution.py:44
  142.5 0.3 convert_reduce_fusion
  142.8 1.6 all-gather.3.cloned.1.call-done
  144.3 0.2 copy.23
  144.5 0.0 copy-done.1
  144.5 0.2 multiply_convert_fusion.1
  144.8 0.8 pad_maximum_fusion.5
  145.6 0.0 all-gather.5.cloned.1.call-update
  145.6 5.9 %convolution_convert_fusion = bf16[1024,1024]{1,0:T(8,128)(2,1)} fusion(bf16[1024,896]{0,1:T(8,128)(2,1)} %all-gather.3.cloned.1.call-done, bf16[896,1024]{1,0:T(8,128)(2,1)} %param.11, pred[112,8,8,128]{3,2,1,0:T(8,128)(4,1)S(1)} %bitcast.54), kind=kOutput, calls=%fused_computation.14 | convolution fusion | flops 1881014272 | bytes 6684672 | tf_op jit(solution)/shard_map/dot_general | solution.py:96
  151.5 6.7 %all-to-all-start.2 = ((bf16[16,64,1024]{2,1,0:T(8,128)(2,1)}), bf16[16,64,1024]{2,1,0:T(8,128)(2,1)S(1)}, u32[]{:S(2)}, u32[]{:S(2)}) async-start(bf16[16,64,1024]{2,1,0:T(8,128)(2,1)} %bitcast.51), calls=%async_computation.3 | async-start | bytes 4194304 | tf_op jit(solution)/shard_map/all_to_all | solution.py:60
  158.2 22.3 %all-gather.5.cloned.1.call-done = bf16[1024,1792]{0,1:T(8,128)(2,1)} async-done(((bf16[128,1792]{0,1:T(8,128)(2,1)}), bf16[1024,1792]{0,1:T(8,128)(2,1)}) %all-gather.5.cloned.1.call-update) | async-done | bytes 3670032 | tf_op jit(solution)/shard_map/all_gather | solution.py:38
  180.5 8.5 %fusion.3 = bf16[1024,1024]{1,0:T(8,128)(2,1)} fusion(bf16[1024,1792]{0,1:T(8,128)(2,1)} %all-gather.5.cloned.1.call-done, bf16[1024,896]{0,1:T(8,128)(2,1)} %get-tuple-element.29, bf16[1024,896]{0,1:T(8,128)(2,1)} %get-tuple-element.30), kind=kOutput, calls=%fused_computation.13 | convolution fusion | flops 3766484992 | bytes 9437184 | tf_op jit(solution)/shard_map/dot_general | solution.py:113
  189.0 1.6 all-to-all-done.2
  190.6 1.4 copy-done
  192.0 5.1 %all-to-all-start.4 = ((bf16[16,64,1024]{2,1,0:T(8,128)(2,1)}), bf16[16,64,1024]{2,1,0:T(8,128)(2,1)S(1)}, u32[]{:S(2)}, u32[]{:S(2)}) async-start(bf16[16,64,1024]{2,1,0:T(8,128)(2,1)} %bitcast.50), calls=%async_computation.5 | async-start | bytes 4194304 | tf_op jit(solution)/shard_map/all_to_all | solution.py:60
  197.1 5.5 %select_convert_fusion = bf16[896,1024]{1,0:T(8,128)(2,1)} fusion(pred[112,8,8,128]{3,2,1,0:T(8,128)(4,1)S(1)} %bitcast.55, bf16[1024,896]{0,1:T(8,128)(2,1)} %all-gather.3.cloned.1.call-done, bf16[1024,1024]{1,0:T(8,128)(2,1)} %bitcast.49), kind=kOutput, calls=%fused_computation.9 | convolution fusion | flops 1880883200 | bytes 6684672 | tf_op jit(solution)/shard_map/dot_general | solution.py:99
  202.6 2.7 %reduce_sum.33 = bf16[64,1024]{1,0:T(8,128)(2,1)} reduce(bf16[16,64,1024]{2,1,0:T(8,128)(2,1)} %copy-done, bf16[]{:T(256)} %constant.2.clone.1), dimensions={0}, to_apply=%region_1.2 | reduce | flops 983040 | bytes 2228226 | tf_op jit(solution)/shard_map/reduce_sum | solution.py:61
  205.3 6.7 %convolution_bitcast_fusion = bf16[1024,1792]{0,1:T(8,128)(2,1)S(1)} fusion(bf16[1024,1792]{0,1:T(8,128)(2,1)} %all-gather.5.cloned.1.call-done, bf16[1024,1024]{1,0:T(8,128)(2,1)} %bitcast.2), kind=kOutput, calls=%fused_computation.4 | convolution fusion | flops 3758096384 | bytes 9437184 | tf_op jit(solution)/shard_map/dot_general | solution.py:105
  211.9 3.0 %fusion.1 = (bf16[1024,896]{0,1:T(8,128)(2,1)}, bf16[1024,896]{0,1:T(8,128)(2,1)}) fusion(bf16[1024,1792]{0,1:T(8,128)(2,1)S(1)} %convolution_bitcast_fusion, pred[1024,7]{0,1:T(8,128)(4,1)S(1)} %bitcast.58, pred[1024,7]{0,1:T(8,128)(4,1)S(1)} %bitcast.60), kind=kLoop, calls=%fused_computation.7 | loop fusion | flops 1835008 | bytes 7354368 | tf_op jit(solution)/shard_map/convert_element_type | solution.py:110
  214.9 3.8 %copy.26 = bf16[1024,896]{1,0:T(8,128)(2,1)} copy(bf16[1024,896]{0,1:T(8,128)(2,1)} %get-tuple-element.25) | data formatting | bytes 3670016
  218.7 3.8 %copy.25 = bf16[1024,896]{1,0:T(8,128)(2,1)} copy(bf16[1024,896]{0,1:T(8,128)(2,1)} %get-tuple-element.26) | data formatting | bytes 3670016
  222.5 7.2 %all-to-all-done.4 = bf16[16,64,1024]{2,1,0:T(8,128)(2,1)S(1)} async-done(((bf16[16,64,1024]{2,1,0:T(8,128)(2,1)}), bf16[16,64,1024]{2,1,0:T(8,128)(2,1)S(1)}, u32[]{:S(2)}, u32[]{:S(2)}) %all-to-all-start.4) | async-done | bytes 2097184 | tf_op jit(solution)/shard_map/all_to_all | solution.py:60
  229.7 1.1 reduce_sum.35
  (16 shorter events, 0.1 us)
Async XLA Ops:
  9.6 8.8 %copy-start.4 = (s32[8,7]{1,0:T(8,128)S(1)}, s32[8,7]{1,0:T(8,128)}, u32[]{:S(2)}) copy-start(s32[8,7]{1,0:T(8,128)} %param.12) | copy-start | bytes 676
  9.7 8.9 %copy-start.5 = (s32[8,7]{1,0:T(8,128)S(1)}, s32[8,7]{1,0:T(8,128)}, u32[]{:S(2)}) copy-start(s32[8,7]{1,0:T(8,128)} %param.13) | copy-start | bytes 676
  9.7 39.8 %all-to-all-start = ((bf16[16,64,1024]{2,1,0:T(8,128)(2,1)}), bf16[16,64,1024]{2,1,0:T(8,128)(2,1)}, u32[]{:S(2)}, u32[]{:S(2)}) async-start(bf16[16,64,1024]{2,1,0:T(8,128)(2,1)} %broadcast_in_dim.53), calls=%async_computation | async-start | bytes 4194304 | tf_op jit(solution)/shard_map/all_to_all | solution.py:67
  18.4 86.7 %reduce-scatter.2.cloned.1.call-start = ((), (), s32[]{:S(2)}) async-start(), calls=%async_computation.6 | async-start | bytes 8257536 | tf_op jit(solution)/shard_map/reduce_scatter | solution.py:32
  59.1 0.9 copy-start.3
  61.6 4.0 %copy-start.6 = (s32[7,8]{1,0:T(8,128)S(1)}, s32[7,8]{1,0:T(8,128)}, u32[]{:S(2)}) copy-start(s32[7,8]{1,0:T(8,128)} %param.14) | copy-start | bytes 676
  61.6 32.6 %all-to-all-start.1 = ((bf16[16,64,1024]{2,1,0:T(8,128)(2,1)}), bf16[16,64,1024]{2,1,0:T(8,128)(2,1)S(1)}, u32[]{:S(2)}, u32[]{:S(2)}) async-start(bf16[16,64,1024]{2,1,0:T(8,128)(2,1)} %broadcast_in_dim.54), calls=%async_computation.2 | async-start | bytes 4194304 | tf_op jit(solution)/shard_map/all_to_all | solution.py:67
  65.5 78.8 %all-gather.3.cloned.1.call-start = ((), (), s32[]{:S(2)}) async-start(), calls=%async_computation.7 | async-start | bytes 2064384 | tf_op jit(solution)/shard_map/all_gather | solution.py:38
  94.2 8.0 %copy-start.2 = (bf16[16,64,1024]{2,1,0:T(8,128)(2,1)}, bf16[16,64,1024]{2,1,0:T(8,128)(2,1)S(1)}, u32[]{:S(2)}) copy-start(bf16[16,64,1024]{2,1,0:T(8,128)(2,1)S(1)} %all-to-all-done.1) | copy-start | bytes 6291460
  107.1 73.4 %all-gather.5.cloned.1.call-start = ((), (), s32[]{:S(2)}) async-start(), calls=%async_computation.8 | async-start | bytes 4128768 | tf_op jit(solution)/shard_map/all_gather | solution.py:38
  142.5 2.0 copy-start.1
  151.5 39.1 %all-to-all-start.2 = ((bf16[16,64,1024]{2,1,0:T(8,128)(2,1)}), bf16[16,64,1024]{2,1,0:T(8,128)(2,1)S(1)}, u32[]{:S(2)}, u32[]{:S(2)}) async-start(bf16[16,64,1024]{2,1,0:T(8,128)(2,1)} %bitcast.51), calls=%async_computation.3 | async-start | bytes 4194304 | tf_op jit(solution)/shard_map/all_to_all | solution.py:60
  190.6 1.4 copy-start
  192.0 37.8 %all-to-all-start.4 = ((bf16[16,64,1024]{2,1,0:T(8,128)(2,1)}), bf16[16,64,1024]{2,1,0:T(8,128)(2,1)S(1)}, u32[]{:S(2)}, u32[]{:S(2)}) async-start(bf16[16,64,1024]{2,1,0:T(8,128)(2,1)} %bitcast.50), calls=%async_computation.5 | async-start | bytes 4194304 | tf_op jit(solution)/shard_map/all_to_all | solution.py:60
Sparse Core Ops, SparseCore 0:
  59.3 45.8 reduce-scatter.1
  107.2 37.0 all-gather.2
  146.6 33.8 all-gather.4

commit v8 on v7

--- a/solution.py
+++ b/solution.py
@@ -4,6 +4,7 @@
 from jax.sharding import PartitionSpec as P
 
 BLK = 128
+GROUP = ("col", "depth")
 
 
 def expand(mask):
@@ -86,10 +87,10 @@
 
     hidden = jnp.dot(x_all, w_both, preferred_element_type=jnp.float32)
     sums = row_sums(lambda start, count: hidden, split_rows)
-    grad_out, _ = lax.optimization_barrier((grad_out, hidden))
-    grad_all = group_gather(grad_out)
+    grad_all = lax.all_gather(grad_out, GROUP, axis=0, tiled=True)
     act_partial = lax.dot_general(grad_all, w_down, outer, preferred_element_type=jnp.float32)
-    act_sums, act_partial = lax.optimization_barrier((sums, act_partial))
+    grad_act = row_sums_direct(act_partial)
+    act_sums, grad_act = lax.optimization_barrier((sums, grad_act))
     act_all = row_gather(swiglu(act_sums))
 
     def out_term(start, count):
@@ -99,8 +100,7 @@
     grad_down = lax.dot_general(act_all, grad_all, inner, preferred_element_type=jnp.float32)
     grad_down_weight = jnp.where(keep_down, grad_down, jnp.float32(0.0)).astype(jnp.bfloat16)
 
-    grad_act = row_sums_direct(act_partial)
-    held_sums, grad_act, _ = lax.optimization_barrier((sums, grad_act, act_all))
+    held_sums, grad_act, _ = lax.optimization_barrier((act_sums, grad_act, act_all))
     grads_all = row_gather(swiglu_back(held_sums, grad_act))
     grad_both = lax.dot_general(x_all, grads_all, inner, preferred_element_type=jnp.float32)
     width = grad_both.shape[1] // 2

time: 238 us -> 249 us (1.046)
  waiting for transfers between devices: 84.5 us -> 96 us
  starting transfers between devices: 24.7 us -> 19.6 us
  blocking collectives: 35.3 us -> 39.9 us
    all_to_all x2 -> x1, waiting for transfers between devices: 48.8 us -> 22.4 us  [group_gather(): pieces = lax.all_to_all(copies, ('col', 'depth'), 0, 0)]
    all_gather x2, waiting for transfers between devices: 23.9 us -> 47.7 us  [row_gather(): return lax.all_gather(block, 'row', axis=0, tiled=True)]
    all_gather x0 -> x1, waiting for transfers between devices: none -> 8.17 us  [local(): grad_all = lax.all_gather(grad_out, GROUP, axis=0, tiled=True)]
    reduce_scatter x1, waiting for transfers between devices: 2.95 us -> 8.67 us  [row_sums(): lax.psum_scatter(term(jnp.int32(0), lax.axis_size('row') * rows), 'row',...]
    all_to_all x1, blocking collectives: 35.3 us -> 39.9 us  [row_sums_direct(): lax.all_to_all(full.astype(jnp.bfloat16).reshape((parts, rows) + full.sha...]
    all_to_all x2 -> x1, starting transfers between devices: 12.7 us -> 8.64 us  [group_gather(): pieces = lax.all_to_all(copies, ('col', 'depth'), 0, 0)]
    unnamed x22 -> x18, local copies, waits for them, and re-layouts: 16.7 us -> 16.5 us
  transfers between devices with their start and end apart: 7 -> 7, of which waited for: 7 -> 7; matrix products, arithmetic and copies ran while one was open for 25% -> 28% of each run, Pallas kernels for 0% -> 0%
where the time goes in v8:
time: 249 us; the launch traced here: 248 us
  waiting for transfers between devices  96 us (39%)
  matrix products  40 us (16%)
  blocking collectives  39.9 us (16%)
  local copies, waits for them, and re-layouts  22.4 us (9%)
  starting transfers between devices  19.6 us (8%)
  between operations  15.8 us (6%)
  other arithmetic  14.7 us (6%)
    all_gather x2, waiting for transfers between devices, row_gather(): return lax.all_gather(block, 'row', axis=0, tiled=True)  47.7 us
    all_to_all x1, blocking collectives, row_sums_direct(): lax.all_to_all(full.astype(jnp.bfloat16).reshape((parts, rows) + full.sha...  39.9 us
    all_to_all x1, waiting for transfers between devices, group_gather(): pieces = lax.all_to_all(copies, ('col', 'depth'), 0, 0)  22.4 us
    unnamed x18, local copies, waits for them, and re-layouts  16.5 us
    all_to_all x2, starting transfers between devices, group_sums(): lax.all_to_all(full.reshape((parts, rows) + full.shape[1:]), ('col', 'dep...  10.8 us
    dot_general x1, matrix products, local(): hidden = jnp.dot(x_all, w_both, preferred_element_type=jnp.float32)  9.67 us
    reduce_scatter x1, waiting for transfers between devices, row_sums(): lax.psum_scatter(term(jnp.int32(0), lax.axis_size('row') * rows), 'row',...  8.67 us
    all_to_all x1, starting transfers between devices, group_gather(): pieces = lax.all_to_all(copies, ('col', 'depth'), 0, 0)  8.64 us
  transfers between devices with their start and end apart: 7, of which 7 were waited for; matrix products, arithmetic and copies ran while one was open for 28% of the time, Pallas kernels for 0%

profile of v8, /device:TPU:1, one launch (start us, length us, event | category | flops | bytes accessed | tf_op | source)
XLA Modules:
  0.0 248.3 jit_solution(11368157197921686129)
XLA Ops:
  8.0 0.0 all-gather.4.cloned.1.call-start
  8.0 0.7 all-gather.4.cloned.1.call-update
  8.7 2.5 %broadcast_in_dim.47 = bf16[16,64,1024]{2,1,0:T(8,128)(2,1)} broadcast(bf16[64,1024]{1,0:T(8,128)(2,1)} %param.8), dimensions={1,2} | broadcast | bytes 2228224 | tf_op jit(solution)/shard_map/broadcast_in_dim | solution.py:67
  11.2 8.6 %all-to-all-start = ((bf16[16,64,1024]{2,1,0:T(8,128)(2,1)}), bf16[16,64,1024]{2,1,0:T(8,128)(2,1)}, u32[]{:S(2)}, u32[]{:S(2)}) async-start(bf16[16,64,1024]{2,1,0:T(8,128)(2,1)} %broadcast_in_dim.47), calls=%async_computation | async-start | bytes 4194304 | tf_op jit(solution)/shard_map/all_to_all | solution.py:68
  19.9 0.0 copy-start.1
  19.9 0.0 reduce-scatter.2.cloned.1.call-start
  19.9 2.9 %copy.22 = bf16[1024,896]{0,1:T(8,128)(2,1)S(1)} copy(bf16[1024,896]{1,0:T(8,128)(2,1)} %param.10) | data formatting | bytes 3670016 | tf_op args[2]
  22.9 0.0 copy-start.2
  22.9 0.1 copy.21
  23.0 0.1 broadcast_bitcast_fusion
  23.1 3.8 %copy.20 = bf16[1024,896]{0,1:T(8,128)(2,1)} copy(bf16[1024,896]{1,0:T(8,128)(2,1)} %param.9) | data formatting | bytes 3670016 | tf_op args[1]
  26.9 0.1 copy.19
  27.0 0.1 broadcast_bitcast_fusion.1
  27.1 3.6 %bitcast_select_fusion.1 = (bf16[1024,896]{0,1:T(8,128)(2,1)}, bf16[1024,896]{0,1:T(8,128)(2,1)}) fusion(bf16[1024,896]{0,1:T(8,128)(2,1)S(1)} %copy.22, pred[1024,7]{0,1:T(8,128)(4,1)S(1)} %bitcast.59, bf16[1024,896]{0,1:T(8,128)(2,1)} %copy.20, pred[1024,7]{0,1:T(8,128)(4,1)S(1)} %bitcast.61), kind=kLoop, calls=%fused_computation.1 | loop fusion | flops 1835008 | bytes 7354368 | tf_op jit(solution)/shard_map/jit(_where)/select_n | solution.py:78
  30.7 22.4 %all-to-all-done = bf16[16,64,1024]{2,1,0:T(8,128)(2,1)} async-done(((bf16[16,64,1024]{2,1,0:T(8,128)(2,1)}), bf16[16,64,1024]{2,1,0:T(8,128)(2,1)}, u32[]{:S(2)}, u32[]{:S(2)}) %all-to-all-start) | async-done | bytes 2097184 | tf_op jit(solution)/shard_map/all_to_all | solution.py:68
  53.1 9.7 %convolution_bitcast_fusion.1 = f32[1024,1792]{0,1:T(8,128)} fusion(bf16[1024,1024]{1,0:T(8,128)(2,1)} %bitcast.2, bf16[1024,896]{0,1:T(8,128)(2,1)} %get-tuple-element.27, bf16[1024,896]{0,1:T(8,128)(2,1)} %get-tuple-element.28), kind=kOutput, calls=%fused_computation.5 | convolution fusion | flops 3765436416 | bytes 13107200 | tf_op jit(solution)/shard_map/dot_general | solution.py:88
  62.8 0.0 reduce-scatter.2.cloned.1.call-update
  62.8 0.0 all-gather.6.cloned.1.call-start
  62.9 0.6 copy-done.3
  63.5 8.2 %all-gather.4.cloned.1.call-done = bf16[1024,1024]{1,0:T(8,128)(2,1)} async-done(((bf16[64,1024]{1,0:T(8,128)(2,1)}), bf16[1024,1024]{1,0:T(8,128)(2,1)}) %all-gather.4.cloned.1.call-update) | async-done | bytes 2097168 | tf_op jit(solution)/shard_map/all_gather | solution.py:90
  71.7 2.8 %broadcast_in_dim.49 = pred[896,8,128]{2,1,0:T(8,128)(4,1)S(1)} broadcast(pred[896,8]{1,0:T(8,128)(4,1)S(1)} %bitcast.58), dimensions={0,1} | broadcast | bytes 924672 | tf_op jit(solution)/shard_map/broadcast_in_dim | solution.py:11
  74.5 3.8 %convert_bitcast_fusion = bf16[112,8,8,128]{3,2,1,0:T(8,128)(2,1)S(1)} fusion(bf16[1024,1024]{1,0:T(8,128)(2,1)} %all-gather.4.cloned.1.call-done, bf16[896,1024]{1,0:T(8,128)(2,1)S(1)} %copy-done.4, pred[112,8,8,128]{3,2,1,0:T(8,128)(4,1)S(1)} %bitcast.55), kind=kOutput, calls=%fused_computation.16 | convolution fusion | flops 1880883200 | bytes 6684672 | tf_op jit(solution)/shard_map/dot_general | solution.py:91
  78.2 0.3 copy.37
  78.6 39.9 %all_to_all.20 = bf16[8,128,896]{1,2,0:T(8,128)(2,1)S(1)} all-to-all(bf16[8,128,896]{1,2,0:T(8,128)(2,1)S(1)} %bitcast.52), channel_id=1, replica_groups=mesh['row'=8,'col'=4,'depth'=4] {'row'}, dimensions={0} | all-to-all | bytes 3670016 | tf_op jit(solution)/shard_map/all_to_all | solution.py:45
  118.5 0.3 convert_reduce_fusion
  118.8 8.7 %reduce-scatter.2.cloned.1.call-done = f32[128,1792]{0,1:T(8,128)} async-done(((f32[1024,1792]{0,1:T(8,128)}), f32[128,1792]{0,1:T(8,128)}) %reduce-scatter.2.cloned.1.call-update) | async-done | bytes 917520 | tf_op jit(solution)/shard_map/reduce_scatter | solution.py:33
  127.4 2.0 multiply_convert_fusion.2
  129.4 0.0 all-gather.6.cloned.1.call-update
  129.4 0.0 all-gather.8.cloned.1.call-start
  129.5 26.2 %all-gather.6.cloned.1.call-done = bf16[1024,896]{0,1:T(8,128)(2,1)} async-done(((bf16[128,896]{0,1:T(8,128)(2,1)}), bf16[1024,896]{0,1:T(8,128)(2,1)}) %all-gather.6.cloned.1.call-update) | async-done | bytes 1835024 | tf_op jit(solution)/shard_map/all_gather | solution.py:39
  155.7 1.4 multiply_convert_fusion.1
  157.1 0.8 pad_maximum_fusion.5
  157.9 0.0 all-gather.8.cloned.1.call-update
  157.9 5.9 %convolution_convert_fusion = bf16[1024,1024]{1,0:T(8,128)(2,1)} fusion(bf16[1024,896]{0,1:T(8,128)(2,1)} %all-gather.6.cloned.1.call-done, bf16[896,1024]{1,0:T(8,128)(2,1)} %param.11, pred[112,8,8,128]{3,2,1,0:T(8,128)(4,1)S(1)} %bitcast.56), kind=kOutput, calls=%fused_computation.14 | convolution fusion | flops 1881014272 | bytes 6684672 | tf_op jit(solution)/shard_map/dot_general | solution.py:97
  163.8 6.7 %all-to-all-start.2 = ((bf16[16,64,1024]{2,1,0:T(8,128)(2,1)}), bf16[16,64,1024]{2,1,0:T(8,128)(2,1)S(1)}, u32[]{:S(2)}, u32[]{:S(2)}) async-start(bf16[16,64,1024]{2,1,0:T(8,128)(2,1)} %bitcast.54), calls=%async_computation.3 | async-start | bytes 4194304 | tf_op jit(solution)/shard_map/all_to_all | solution.py:61
  170.5 21.5 %all-gather.8.cloned.1.call-done = bf16[1024,1792]{0,1:T(8,128)(2,1)} async-done(((bf16[128,1792]{0,1:T(8,128)(2,1)}), bf16[1024,1792]{0,1:T(8,128)(2,1)}) %all-gather.8.cloned.1.call-update) | async-done | bytes 3670032 | tf_op jit(solution)/shard_map/all_gather | solution.py:39
  192.0 8.5 %fusion.3 = bf16[1024,1024]{1,0:T(8,128)(2,1)} fusion(bf16[1024,1792]{0,1:T(8,128)(2,1)} %all-gather.8.cloned.1.call-done, bf16[1024,896]{0,1:T(8,128)(2,1)} %get-tuple-element.27, bf16[1024,896]{0,1:T(8,128)(2,1)} %get-tuple-element.28), kind=kOutput, calls=%fused_computation.13 | convolution fusion | flops 3766484992 | bytes 9437184 | tf_op jit(solution)/shard_map/dot_general | solution.py:113
  200.5 2.6 %all-to-all-done.2 = bf16[16,64,1024]{2,1,0:T(8,128)(2,1)S(1)} async-done(((bf16[16,64,1024]{2,1,0:T(8,128)(2,1)}), bf16[16,64,1024]{2,1,0:T(8,128)(2,1)S(1)}, u32[]{:S(2)}, u32[]{:S(2)}) %all-to-all-start.2) | async-done | bytes 2097184 | tf_op jit(solution)/shard_map/all_to_all | solution.py:61
  203.1 1.4 copy-done
  204.5 4.1 %all-to-all-start.3 = ((bf16[16,64,1024]{2,1,0:T(8,128)(2,1)}), bf16[16,64,1024]{2,1,0:T(8,128)(2,1)S(1)}, u32[]{:S(2)}, u32[]{:S(2)}) async-start(bf16[16,64,1024]{2,1,0:T(8,128)(2,1)} %bitcast.53), calls=%async_computation.4 | async-start | bytes 4194304 | tf_op jit(solution)/shard_map/all_to_all | solution.py:61
  208.7 5.5 %select_convert_fusion = bf16[896,1024]{1,0:T(8,128)(2,1)} fusion(pred[112,8,8,128]{3,2,1,0:T(8,128)(4,1)S(1)} %bitcast.57, bf16[1024,896]{0,1:T(8,128)(2,1)} %all-gather.6.cloned.1.call-done, bf16[1024,1024]{1,0:T(8,128)(2,1)} %all-gather.4.cloned.1.call-done), kind=kOutput, calls=%fused_computation.9 | convolution fusion | flops 1880883200 | bytes 6684672 | tf_op jit(solution)/shard_map/dot_general | solution.py:100
  214.1 2.7 %reduce_sum.34 = bf16[64,1024]{1,0:T(8,128)(2,1)} reduce(bf16[16,64,1024]{2,1,0:T(8,128)(2,1)} %copy-done, bf16[]{:T(256)} %constant.2.clone.1), dimensions={0}, to_apply=%region_2.3 | reduce | flops 983040 | bytes 2228226 | tf_op jit(solution)/shard_map/reduce_sum | solution.py:62
  216.8 6.7 %convolution_bitcast_fusion = bf16[1024,1792]{0,1:T(8,128)(2,1)S(1)} fusion(bf16[1024,1792]{0,1:T(8,128)(2,1)} %all-gather.8.cloned.1.call-done, bf16[1024,1024]{1,0:T(8,128)(2,1)} %bitcast.2), kind=kOutput, calls=%fused_computation.4 | convolution fusion | flops 3758096384 | bytes 9437184 | tf_op jit(solution)/shard_map/dot_general | solution.py:105
  223.5 2.9 %fusion.1 = (bf16[1024,896]{0,1:T(8,128)(2,1)}, bf16[1024,896]{0,1:T(8,128)(2,1)}) fusion(bf16[1024,1792]{0,1:T(8,128)(2,1)S(1)} %convolution_bitcast_fusion, pred[1024,7]{0,1:T(8,128)(4,1)S(1)} %bitcast.60, pred[1024,7]{0,1:T(8,128)(4,1)S(1)} %bitcast.62), kind=kLoop, calls=%fused_computation.7 | loop fusion | flops 1835008 | bytes 7354368 | tf_op jit(solution)/shard_map/convert_element_type | solution.py:110
  226.4 3.8 %copy.24 = bf16[1024,896]{1,0:T(8,128)(2,1)} copy(bf16[1024,896]{0,1:T(8,128)(2,1)} %get-tuple-element.24) | data formatting | bytes 3670016
  230.2 3.8 %copy.25 = bf16[1024,896]{1,0:T(8,128)(2,1)} copy(bf16[1024,896]{0,1:T(8,128)(2,1)} %get-tuple-element.23) | data formatting | bytes 3670016
  234.0 5.7 %all-to-all-done.3 = bf16[16,64,1024]{2,1,0:T(8,128)(2,1)S(1)} async-done(((bf16[16,64,1024]{2,1,0:T(8,128)(2,1)}), bf16[16,64,1024]{2,1,0:T(8,128)(2,1)S(1)}, u32[]{:S(2)}, u32[]{:S(2)}) %all-to-all-start.3) | async-done | bytes 2097184 | tf_op jit(solution)/shard_map/all_to_all | solution.py:61
  239.7 1.1 reduce_sum.35
  (12 shorter events, 0.1 us)
Async XLA Ops:
  8.0 63.6 %all-gather.4.cloned.1.call-start = ((), (), s32[]{:S(2)}) async-start(), calls=%async_computation.6 | async-start | bytes 2228224 | tf_op jit(solution)/shard_map/all_gather | solution.py:90
  11.2 41.9 %all-to-all-start = ((bf16[16,64,1024]{2,1,0:T(8,128)(2,1)}), bf16[16,64,1024]{2,1,0:T(8,128)(2,1)}, u32[]{:S(2)}, u32[]{:S(2)}) async-start(bf16[16,64,1024]{2,1,0:T(8,128)(2,1)} %broadcast_in_dim.47), calls=%async_computation | async-start | bytes 4194304 | tf_op jit(solution)/shard_map/all_to_all | solution.py:68
  19.9 3.0 %copy-start.1 = (s32[8,7]{1,0:T(8,128)S(1)}, s32[8,7]{1,0:T(8,128)}, u32[]{:S(2)}) copy-start(s32[8,7]{1,0:T(8,128)} %param.13) | copy-start | bytes 676
  19.9 107.5 %reduce-scatter.2.cloned.1.call-start = ((), (), s32[]{:S(2)}) async-start(), calls=%async_computation.5 | async-start | bytes 8257536 | tf_op jit(solution)/shard_map/reduce_scatter | solution.py:33
  22.9 4.0 %copy-start.2 = (s32[8,7]{1,0:T(8,128)S(1)}, s32[8,7]{1,0:T(8,128)}, u32[]{:S(2)}) copy-start(s32[8,7]{1,0:T(8,128)} %param.12) | copy-start | bytes 676
  62.8 0.7 copy-start.3
  62.8 11.7 %copy-start.4 = (bf16[896,1024]{1,0:T(8,128)(2,1)S(1)}, bf16[896,1024]{1,0:T(8,128)(2,1)}, u32[]{:S(2)}) copy-start(bf16[896,1024]{1,0:T(8,128)(2,1)} %param.11) | copy-start | bytes 5505028
  62.8 92.9 %all-gather.6.cloned.1.call-start = ((), (), s32[]{:S(2)}) async-start(), calls=%async_computation.7 | async-start | bytes 2064384 | tf_op jit(solution)/shard_map/all_gather | solution.py:39
  129.4 62.6 %all-gather.8.cloned.1.call-start = ((), (), s32[]{:S(2)}) async-start(), calls=%async_computation.8 | async-start | bytes 4128768 | tf_op jit(solution)/shard_map/all_gather | solution.py:39
  163.8 39.3 %all-to-all-start.2 = ((bf16[16,64,1024]{2,1,0:T(8,128)(2,1)}), bf16[16,64,1024]{2,1,0:T(8,128)(2,1)S(1)}, u32[]{:S(2)}, u32[]{:S(2)}) async-start(bf16[16,64,1024]{2,1,0:T(8,128)(2,1)} %bitcast.54), calls=%async_computation.3 | async-start | bytes 4194304 | tf_op jit(solution)/shard_map/all_to_all | solution.py:61
  203.1 1.4 copy-start
  204.5 35.1 %all-to-all-start.3 = ((bf16[16,64,1024]{2,1,0:T(8,128)(2,1)}), bf16[16,64,1024]{2,1,0:T(8,128)(2,1)S(1)}, u32[]{:S(2)}, u32[]{:S(2)}) async-start(bf16[16,64,1024]{2,1,0:T(8,128)(2,1)} %bitcast.53), calls=%async_computation.4 | async-start | bytes 4194304 | tf_op jit(solution)/shard_map/all_to_all | solution.py:61
Sparse Core Ops, SparseCore 0:
  10.9 60.6 all-gather.3
Sparse Core Ops, SparseCore 1:
  62.9 64.5 reduce-scatter.1
  129.6 26.1 all-gather.5
  158.0 34.0 all-gather.7

commit v9 on v7

--- a/solution.py
+++ b/solution.py
@@ -45,6 +45,26 @@
         full.astype(jnp.bfloat16).reshape((parts, rows) + full.shape[1:]), "row", 0, 0
     )
     return jnp.sum(pieces.astype(jnp.float32), axis=0)
+
+
+def row_sums_paired(full):
+    parts = lax.axis_size("row")
+    chips = parts // 2
+    rows = full.shape[0] // parts
+    member = lax.axis_index("row")
+    core = member % 2
+    chip = member // 2
+    blocks = full.reshape((chips, 2, rows) + full.shape[1:])
+    give = jnp.take(blocks, 1 - core, axis=1)
+    keep = jnp.take(blocks, core, axis=1)
+    pair = keep + lax.ppermute(give, "row", [(i, i ^ 1) for i in range(parts)])
+    sent = pair.astype(jnp.bfloat16)
+    total = jnp.take(pair, chip, axis=0)
+    for hop in range(1, chips):
+        piece = jnp.take(sent, (chip + hop) % chips, axis=0)
+        moved = lax.ppermute(piece, "row", [(i, (i + 2 * hop) % parts) for i in range(parts)])
+        total = total + moved.astype(jnp.float32)
+    return total
 
 
 def row_gather_direct(block):
@@ -99,7 +119,7 @@
     grad_down = lax.dot_general(act_all, grad_all, inner, preferred_element_type=jnp.float32)
     grad_down_weight = jnp.where(keep_down, grad_down, jnp.float32(0.0)).astype(jnp.bfloat16)
 
-    grad_act = row_sums_direct(act_partial)
+    grad_act = row_sums_paired(act_partial)
     held_sums, grad_act, _ = lax.optimization_barrier((sums, grad_act, act_all))
     grads_all = row_gather(swiglu_back(held_sums, grad_act))
     grad_both = lax.dot_general(x_all, grads_all, inner, preferred_element_type=jnp.float32)

time: 238 us -> 236 us (level)
  blocking collectives: 35.3 us -> 0 us
  waiting for transfers between devices: 84.5 us -> 97 us
  local copies, waits for them, and re-layouts: 24 us -> 31.7 us
  starting transfers between devices: 24.7 us -> 31.2 us
  other arithmetic: 13.6 us -> 18.9 us
    all_to_all x1 -> x0, blocking collectives: 35.3 us -> none  [row_sums_direct(): lax.all_to_all(full.astype(jnp.bfloat16).reshape((parts, rows) + full.sha...]
    ppermute x0 -> x4, waiting for transfers between devices: none -> 14.7 us  [the longest x3 12.4 us: row_sums_paired(): lax.ppermute(piece, 'row', [(i, (i + 2 * hop) % parts) for i in range(par...]
    ppermute x0 -> x4, starting transfers between devices: none -> 5.29 us  [the longest x3 4.11 us: row_sums_paired(): lax.ppermute(piece, 'row', [(i, (i + 2 * hop) % parts) for i in range(par...]
    another operation x0 -> x1, local copies, waits for them, and re-layouts: none -> 4.21 us  [row_sums_paired(): keep = jnp.take(blocks, core, axis=1)]
    unnamed x22 -> x24, local copies, waits for them, and re-layouts: 16.7 us -> 20.3 us
    convert_element_type x0 -> x1, other arithmetic: none -> 2.97 us  [row_sums_paired(): sent = pair.astype(jnp.bfloat16)]
  transfers between devices with their start and end apart: 7 -> 11, of which waited for: 7 -> 9; matrix products, arithmetic and copies ran while one was open for 25% -> 32% of each run, Pallas kernels for 0% -> 0%
where the time goes in v9:
time: 236 us; the launch traced here: 235 us
  waiting for transfers between devices  97 us (41%)
  matrix products  42 us (18%)
  local copies, waits for them, and re-layouts  31.7 us (13%)
  starting transfers between devices  31.2 us (13%)
  other arithmetic  18.9 us (8%)
  between operations  13.9 us (6%)
    all_to_all x2, waiting for transfers between devices, group_gather(): pieces = lax.all_to_all(copies, ('col', 'depth'), 0, 0)  48.8 us
    all_gather x2, waiting for transfers between devices, row_gather(): return lax.all_gather(block, 'row', axis=0, tiled=True)  22.5 us
    unnamed x24, local copies, waits for them, and re-layouts  20.3 us
    all_to_all x2, starting transfers between devices, group_sums(): lax.all_to_all(full.reshape((parts, rows) + full.shape[1:]), ('col', 'dep...  13.1 us
    all_to_all x2, starting transfers between devices, group_gather(): pieces = lax.all_to_all(copies, ('col', 'depth'), 0, 0)  12.7 us
    ppermute x3, waiting for transfers between devices, row_sums_paired(): lax.ppermute(piece, 'row', [(i, (i + 2 * hop) % parts) for i in range(par...  12.4 us
    dot_general x1, matrix products, local(): hidden = jnp.dot(x_all, w_both, preferred_element_type=jnp.float32)  9.65 us
    all_to_all x2, waiting for transfers between devices, group_sums(): lax.all_to_all(full.reshape((parts, rows) + full.shape[1:]), ('col', 'dep...  8.91 us
  transfers between devices with their start and end apart: 11, of which 9 were waited for; matrix products, arithmetic and copies ran while one was open for 32% of the time, Pallas kernels for 0%

profile of v9, /device:TPU:1, one launch (start us, length us, event | category | flops | bytes accessed | tf_op | source)
XLA Modules:
  0.0 234.7 jit_solution(17151122908588174062)
XLA Ops:
  7.2 2.5 %broadcast_in_dim.83 = bf16[16,64,1024]{2,1,0:T(8,128)(2,1)} broadcast(bf16[64,1024]{1,0:T(8,128)(2,1)} %param.12), dimensions={1,2} | broadcast | bytes 2228224 | tf_op jit(solution)/shard_map/broadcast_in_dim | solution.py:86
  9.7 8.8 %all-to-all-start = ((bf16[16,64,1024]{2,1,0:T(8,128)(2,1)}), bf16[16,64,1024]{2,1,0:T(8,128)(2,1)}, u32[]{:S(2)}, u32[]{:S(2)}) async-start(bf16[16,64,1024]{2,1,0:T(8,128)(2,1)} %broadcast_in_dim.83), calls=%async_computation | async-start | bytes 4194304 | tf_op jit(solution)/shard_map/all_to_all | solution.py:87
  18.5 0.1 copy.19
  18.6 0.1 copy.21
  18.7 0.1 broadcast_bitcast_fusion
  18.9 2.9 %copy.20 = bf16[1024,896]{0,1:T(8,128)(2,1)S(1)} copy(bf16[1024,896]{1,0:T(8,128)(2,1)} %param.13) | data formatting | bytes 3670016 | tf_op args[1]
  21.8 3.8 %copy.22 = bf16[1024,896]{0,1:T(8,128)(2,1)} copy(bf16[1024,896]{1,0:T(8,128)(2,1)} %param.14) | data formatting | bytes 3670016 | tf_op args[2]
  25.6 3.6 %bitcast_select_fusion.1 = (bf16[1024,896]{0,1:T(8,128)(2,1)}, bf16[1024,896]{0,1:T(8,128)(2,1)}) fusion(bf16[1024,896]{0,1:T(8,128)(2,1)} %copy.22, pred[1024,7]{0,1:T(8,128)(4,1)S(1)} %bitcast.74, bf16[1024,896]{0,1:T(8,128)(2,1)S(1)} %copy.20, pred[1024,7]{0,1:T(8,128)(4,1)S(1)} %bitcast.76), kind=kLoop, calls=%fused_computation.1 | loop fusion | flops 1835008 | bytes 7354368 | tf_op jit(solution)/shard_map/jit(_where)/select_n | solution.py:97
  29.2 20.2 %all-to-all-done = bf16[16,64,1024]{2,1,0:T(8,128)(2,1)} async-done(((bf16[16,64,1024]{2,1,0:T(8,128)(2,1)}), bf16[16,64,1024]{2,1,0:T(8,128)(2,1)}, u32[]{:S(2)}, u32[]{:S(2)}) %all-to-all-start) | async-done | bytes 2097184 | tf_op jit(solution)/shard_map/all_to_all | solution.py:87
  49.5 9.6 %convolution_bitcast_fusion.1 = f32[1024,1792]{0,1:T(8,128)} fusion(bf16[1024,1024]{1,0:T(8,128)(2,1)} %bitcast.2, bf16[1024,896]{0,1:T(8,128)(2,1)} %get-tuple-element.71, bf16[1024,896]{0,1:T(8,128)(2,1)} %get-tuple-element.72), kind=kOutput, calls=%fused_computation.5 | convolution fusion | flops 3765436416 | bytes 13107200 | tf_op jit(solution)/shard_map/dot_general | solution.py:107
  59.1 0.9 copy-done.3
  60.0 1.7 broadcast_in_dim.84
  61.7 3.9 %all-to-all-start.1 = ((bf16[16,64,1024]{2,1,0:T(8,128)(2,1)}), bf16[16,64,1024]{2,1,0:T(8,128)(2,1)S(1)}, u32[]{:S(2)}, u32[]{:S(2)}) async-start(bf16[16,64,1024]{2,1,0:T(8,128)(2,1)} %broadcast_in_dim.84), calls=%async_computation.2 | async-start | bytes 4194304 | tf_op jit(solution)/shard_map/all_to_all | solution.py:87
  65.8 28.5 %all-to-all-done.1 = bf16[16,64,1024]{2,1,0:T(8,128)(2,1)S(1)} async-done(((bf16[16,64,1024]{2,1,0:T(8,128)(2,1)}), bf16[16,64,1024]{2,1,0:T(8,128)(2,1)S(1)}, u32[]{:S(2)}, u32[]{:S(2)}) %all-to-all-start.1) | async-done | bytes 2097184 | tf_op jit(solution)/shard_map/all_to_all | solution.py:87
  94.3 2.8 %broadcast_in_dim.86 = pred[896,8,128]{2,1,0:T(8,128)(4,1)S(1)} broadcast(pred[896,8]{1,0:T(8,128)(4,1)S(1)} %bitcast.73), dimensions={0,1} | broadcast | bytes 924672 | tf_op jit(solution)/shard_map/broadcast_in_dim | solution.py:10
  97.1 5.9 %fusion.4 = f32[1024,896]{1,0:T(8,128)} fusion(bf16[1024,1024]{1,0:T(8,128)(2,1)S(1)} %bitcast.66, bf16[896,1024]{1,0:T(8,128)(2,1)} %param.15, pred[112,8,8,128]{3,2,1,0:T(8,128)(4,1)S(1)} %bitcast.70), kind=kOutput, calls=%fused_computation.16 | convolution fusion | flops 1879965696 | bytes 8519680 | tf_op jit(solution)/shard_map/dot_general | solution.py:111
  103.0 2.1 reduce-scatter.2.cloned.1.call-done
  105.1 2.0 multiply_convert_fusion.2
  107.2 4.2 %constant_dynamic-slice_fusion.1 = (f32[4,1,128,896]{3,2,1,0:T(8,128)}, f32[4,1,128,896]{3,2,1,0:T(8,128)}) fusion(f32[4,2,128,896]{3,2,1,0:T(8,128)} %bitcast.65, s32[]{:T(128)S(6)} %select_n.92, s32[]{:T(128)S(6)} %select_n.94), kind=kLoop, calls=%fused_computation.38 | loop fusion | bytes 7340040 | tf_op jit(solution)/shard_map/jit(_take) | solution.py:59
  111.4 1.8 copy.28
  113.2 1.4 select_bitcast_fusion
  114.6 1.2 collective-permute-start
  115.7 1.8 copy.27
  117.6 2.2 collective-permute-done
  119.8 3.0 %fusion.13 = (bf16[4,128,896]{1,2,0:T(8,128)(2,1)S(1)}, f32[4,128,896]{1,2,0:T(8,128)}) fusion(f32[4,128,896]{1,2,0:T(8,128)} %collective-permute-done, f32[4,1,128,896]{2,3,0,1:T(8,128)S(1)} %copy.27, pred[]{:T(512)S(6)} %and.48), kind=kLoop, calls=%fused_computation.43 | loop fusion | flops 1376256 | bytes 6422529 | tf_op jit(solution)/shard_map/convert_element_type | solution.py:61
  122.9 1.1 collective-permute-start.1
  124.0 1.6 collective-permute-start.3
  125.6 1.4 collective-permute-start.2
  127.0 7.7 %collective-permute-done.1 = bf16[128,896]{0,1:T(8,128)(2,1)S(1)} collective-permute-done((bf16[128,896]{0,1:T(8,128)(2,1)S(1)}, bf16[128,896]{0,1:T(8,128)(2,1)S(1)}, u32[]{:S(2)}, u32[]{:S(2)}) %collective-permute-start.1) | collective-permute-done | bytes 229408 | tf_op jit(solution)/shard_map/ppermute | solution.py:65
  134.7 4.7 %collective-permute-done.2 = bf16[128,896]{0,1:T(8,128)(2,1)S(1)} collective-permute-done((bf16[128,896]{0,1:T(8,128)(2,1)S(1)}, bf16[128,896]{0,1:T(8,128)(2,1)S(1)}, u32[]{:S(2)}, u32[]{:S(2)}) %collective-permute-start.2) | collective-permute-done | bytes 229408 | tf_op jit(solution)/shard_map/ppermute | solution.py:65
  139.4 1.1 fusion.8
  140.6 0.2 multiply_convert_fusion.1
  140.8 0.8 pad_maximum_fusion.5
  141.6 5.8 %convolution_convert_fusion = bf16[1024,1024]{1,0:T(8,128)(2,1)} fusion(bf16[1024,896]{0,1:T(8,128)(2,1)} %all-gather.3.cloned.1.call-done, bf16[896,1024]{1,0:T(8,128)(2,1)} %param.15, pred[112,8,8,128]{3,2,1,0:T(8,128)(4,1)S(1)} %bitcast.71), kind=kOutput, calls=%fused_computation.13 | convolution fusion | flops 1881014272 | bytes 6684672 | tf_op jit(solution)/shard_map/dot_general | solution.py:116
  147.5 8.0 %all-to-all-start.2 = ((bf16[16,64,1024]{2,1,0:T(8,128)(2,1)}), bf16[16,64,1024]{2,1,0:T(8,128)(2,1)S(1)}, u32[]{:S(2)}, u32[]{:S(2)}) async-start(bf16[16,64,1024]{2,1,0:T(8,128)(2,1)} %bitcast.69), calls=%async_computation.3 | async-start | bytes 4194304 | tf_op jit(solution)/shard_map/all_to_all | solution.py:80
  155.5 22.4 %all-gather.5.cloned.1.call-done = bf16[1024,1792]{0,1:T(8,128)(2,1)} async-done(((bf16[128,1792]{0,1:T(8,128)(2,1)}), bf16[1024,1792]{0,1:T(8,128)(2,1)}) %all-gather.5.cloned.1.call-update) | async-done | bytes 3670032 | tf_op jit(solution)/shard_map/all_gather | solution.py:38
  177.9 8.5 %fusion.3 = bf16[1024,1024]{1,0:T(8,128)(2,1)} fusion(bf16[1024,1792]{0,1:T(8,128)(2,1)} %all-gather.5.cloned.1.call-done, bf16[1024,896]{0,1:T(8,128)(2,1)} %get-tuple-element.71, bf16[1024,896]{0,1:T(8,128)(2,1)} %get-tuple-element.72), kind=kOutput, calls=%fused_computation.12 | convolution fusion | flops 3766484992 | bytes 9437184 | tf_op jit(solution)/shard_map/dot_general | solution.py:133
  186.5 1.7 all-to-all-done.2
  188.1 1.3 copy-done
  189.5 5.1 %all-to-all-start.3 = ((bf16[16,64,1024]{2,1,0:T(8,128)(2,1)}), bf16[16,64,1024]{2,1,0:T(8,128)(2,1)S(1)}, u32[]{:S(2)}, u32[]{:S(2)}) async-start(bf16[16,64,1024]{2,1,0:T(8,128)(2,1)} %bitcast.68), calls=%async_computation.4 | async-start | bytes 4194304 | tf_op jit(solution)/shard_map/all_to_all | solution.py:80
  194.5 5.5 %select_convert_fusion = bf16[896,1024]{1,0:T(8,128)(2,1)} fusion(pred[112,8,8,128]{3,2,1,0:T(8,128)(4,1)S(1)} %bitcast.72, bf16[1024,896]{0,1:T(8,128)(2,1)} %all-gather.3.cloned.1.call-done, bf16[1024,1024]{1,0:T(8,128)(2,1)} %bitcast.67), kind=kOutput, calls=%fused_computation.9 | convolution fusion | flops 1880883200 | bytes 6684672 | tf_op jit(solution)/shard_map/dot_general | solution.py:119
  200.0 2.7 %reduce_sum.24 = bf16[64,1024]{1,0:T(8,128)(2,1)} reduce(bf16[16,64,1024]{2,1,0:T(8,128)(2,1)} %copy-done, bf16[]{:T(256)} %constant.84.clone.1), dimensions={0}, to_apply=%region_1.2 | reduce | flops 983040 | bytes 2228226 | tf_op jit(solution)/shard_map/reduce_sum | solution.py:81
  202.6 6.7 %convolution_bitcast_fusion = bf16[1024,1792]{0,1:T(8,128)(2,1)S(1)} fusion(bf16[1024,1792]{0,1:T(8,128)(2,1)} %all-gather.5.cloned.1.call-done, bf16[1024,1024]{1,0:T(8,128)(2,1)} %bitcast.2), kind=kOutput, calls=%fused_computation.4 | convolution fusion | flops 3758096384 | bytes 9437184 | tf_op jit(solution)/shard_map/dot_general | solution.py:125
  209.3 3.0 %fusion.1 = (bf16[1024,896]{0,1:T(8,128)(2,1)}, bf16[1024,896]{0,1:T(8,128)(2,1)}) fusion(bf16[1024,1792]{0,1:T(8,128)(2,1)S(1)} %convolution_bitcast_fusion, pred[1024,7]{0,1:T(8,128)(4,1)S(1)} %bitcast.75, pred[1024,7]{0,1:T(8,128)(4,1)S(1)} %bitcast.77), kind=kLoop, calls=%fused_computation.7 | loop fusion | flops 1835008 | bytes 7354368 | tf_op jit(solution)/shard_map/convert_element_type | solution.py:130
  212.3 3.8 %copy.26 = bf16[1024,896]{1,0:T(8,128)(2,1)} copy(bf16[1024,896]{0,1:T(8,128)(2,1)} %get-tuple-element.62) | data formatting | bytes 3670016
  216.1 3.8 %copy.25 = bf16[1024,896]{1,0:T(8,128)(2,1)} copy(bf16[1024,896]{0,1:T(8,128)(2,1)} %get-tuple-element.63) | data formatting | bytes 3670016
  219.9 7.2 %all-to-all-done.3 = bf16[16,64,1024]{2,1,0:T(8,128)(2,1)S(1)} async-done(((bf16[16,64,1024]{2,1,0:T(8,128)(2,1)}), bf16[16,64,1024]{2,1,0:T(8,128)(2,1)S(1)}, u32[]{:S(2)}, u32[]{:S(2)}) %all-to-all-start.3) | async-done | bytes 2097184 | tf_op jit(solution)/shard_map/all_to_all | solution.py:80
  227.1 1.1 reduce_sum.25
  (28 shorter events, 0.4 us)
Async XLA Ops:
  9.7 8.8 %copy-start.4 = (s32[8,7]{1,0:T(8,128)S(1)}, s32[8,7]{1,0:T(8,128)}, u32[]{:S(2)}) copy-start(s32[8,7]{1,0:T(8,128)} %param.16) | copy-start | bytes 676
  9.7 8.9 %copy-start.5 = (s32[8,7]{1,0:T(8,128)S(1)}, s32[8,7]{1,0:T(8,128)}, u32[]{:S(2)}) copy-start(s32[8,7]{1,0:T(8,128)} %param.17) | copy-start | bytes 676
  9.7 39.8 %all-to-all-start = ((bf16[16,64,1024]{2,1,0:T(8,128)(2,1)}), bf16[16,64,1024]{2,1,0:T(8,128)(2,1)}, u32[]{:S(2)}, u32[]{:S(2)}) async-start(bf16[16,64,1024]{2,1,0:T(8,128)(2,1)} %broadcast_in_dim.83), calls=%async_computation | async-start | bytes 4194304 | tf_op jit(solution)/shard_map/all_to_all | solution.py:87
  18.4 86.7 %reduce-scatter.2.cloned.1.call-start = ((), (), s32[]{:S(2)}) async-start(), calls=%async_computation.5 | async-start | bytes 8257536 | tf_op jit(solution)/shard_map/reduce_scatter | solution.py:32
  59.1 0.9 copy-start.3
  61.7 4.0 %copy-start.6 = (s32[7,8]{1,0:T(8,128)S(1)}, s32[7,8]{1,0:T(8,128)}, u32[]{:S(2)}) copy-start(s32[7,8]{1,0:T(8,128)} %param.18) | copy-start | bytes 676
  61.7 32.6 %all-to-all-start.1 = ((bf16[16,64,1024]{2,1,0:T(8,128)(2,1)}), bf16[16,64,1024]{2,1,0:T(8,128)(2,1)S(1)}, u32[]{:S(2)}, u32[]{:S(2)}) async-start(bf16[16,64,1024]{2,1,0:T(8,128)(2,1)} %broadcast_in_dim.84), calls=%async_computation.2 | async-start | bytes 4194304 | tf_op jit(solution)/shard_map/all_to_all | solution.py:87
  65.7 74.9 %all-gather.3.cloned.1.call-start = ((), (), s32[]{:S(2)}) async-start(), calls=%async_computation.6 | async-start | bytes 2064384 | tf_op jit(solution)/shard_map/all_gather | solution.py:38
  94.3 8.7 %copy-start.2 = (bf16[16,64,1024]{2,1,0:T(8,128)(2,1)}, bf16[16,64,1024]{2,1,0:T(8,128)(2,1)S(1)}, u32[]{:S(2)}) copy-start(bf16[16,64,1024]{2,1,0:T(8,128)(2,1)S(1)} %all-to-all-done.1) | copy-start | bytes 6291460
  107.1 70.8 %all-gather.5.cloned.1.call-start = ((), (), s32[]{:S(2)}) async-start(), calls=%async_computation.7 | async-start | bytes 4128768 | tf_op jit(solution)/shard_map/all_gather | solution.py:38
  114.6 5.3 %collective-permute-start = (f32[4,128,896]{1,2,0:T(8,128)}, f32[4,128,896]{1,2,0:T(8,128)}, u32[]{:S(2)}, u32[]{:S(2)}) collective-permute-start(f32[4,128,896]{1,2,0:T(8,128)} %select_bitcast_fusion), channel_id=1, source_target_pairs={{0,16},{16,0},{32,48},{48,32},{64,80},{80,64},{96,112},{112,96},{1... | collective-permute-start | bytes 5505032 | tf_op jit(solution)/shard_map/ppermute | solution.py:60
  122.8 17.8 %copy-start.1 = (f32[128,1792]{0,1:T(8,128)S(1)}, f32[128,1792]{0,1:T(8,128)}, u32[]{:S(2)}) copy-start(f32[128,1792]{0,1:T(8,128)} %reduce-scatter.2.cloned.1.call-done) | copy-start | bytes 2752516
  122.9 11.8 %collective-permute-start.1 = (bf16[128,896]{0,1:T(8,128)(2,1)S(1)}, bf16[128,896]{0,1:T(8,128)(2,1)S(1)}, u32[]{:S(2)}, u32[]{:S(2)}) collective-permute-start(bf16[128,896]{0,1:T(8,128)(2,1)S(1)} %get-tuple-element.68), channel_id=1, source_target_pairs={{0,32},{16,48},{32,64},{48,80},{64,96},{80,112},{96,0},{112,16},{1... | collective-permute-start | bytes 688136 | tf_op jit(solution)/shard_map/ppermute | solution.py:65
  124.0 10.7 %collective-permute-start.3 = (bf16[128,896]{0,1:T(8,128)(2,1)S(1)}, bf16[128,896]{0,1:T(8,128)(2,1)S(1)}, u32[]{:S(2)}, u32[]{:S(2)}) collective-permute-start(bf16[128,896]{0,1:T(8,128)(2,1)S(1)} %get-tuple-element.69), channel_id=1, source_target_pairs={{0,96},{16,112},{32,0},{48,16},{64,32},{80,48},{96,64},{112,80},{1... | collective-permute-start | bytes 688136 | tf_op jit(solution)/shard_map/ppermute | solution.py:65
  125.6 13.8 %collective-permute-start.2 = (bf16[128,896]{0,1:T(8,128)(2,1)S(1)}, bf16[128,896]{0,1:T(8,128)(2,1)S(1)}, u32[]{:S(2)}, u32[]{:S(2)}) collective-permute-start(bf16[128,896]{0,1:T(8,128)(2,1)S(1)} %get-tuple-element.70), channel_id=1, source_target_pairs={{0,64},{16,80},{32,96},{48,112},{64,0},{80,16},{96,32},{112,48},{1... | collective-permute-start | bytes 688136 | tf_op jit(solution)/shard_map/ppermute | solution.py:65
  147.5 40.7 %all-to-all-start.2 = ((bf16[16,64,1024]{2,1,0:T(8,128)(2,1)}), bf16[16,64,1024]{2,1,0:T(8,128)(2,1)S(1)}, u32[]{:S(2)}, u32[]{:S(2)}) async-start(bf16[16,64,1024]{2,1,0:T(8,128)(2,1)} %bitcast.69), calls=%async_computation.3 | async-start | bytes 4194304 | tf_op jit(solution)/shard_map/all_to_all | solution.py:80
  188.1 1.3 copy-start
  189.5 37.7 %all-to-all-start.3 = ((bf16[16,64,1024]{2,1,0:T(8,128)(2,1)}), bf16[16,64,1024]{2,1,0:T(8,128)(2,1)S(1)}, u32[]{:S(2)}, u32[]{:S(2)}) async-start(bf16[16,64,1024]{2,1,0:T(8,128)(2,1)} %bitcast.68), calls=%async_computation.4 | async-start | bytes 4194304 | tf_op jit(solution)/shard_map/all_to_all | solution.py:80
Sparse Core Ops, SparseCore 0:
  59.3 45.8 reduce-scatter.1
  107.2 31.9 all-gather.2
  141.8 36.1 all-gather.4

commit v10 on v9

--- a/solution.py
+++ b/solution.py
@@ -104,9 +104,12 @@
     inner = (((0,), (0,)), ((), ()))
     outer = (((1,), (1,)), ((), ()))
 
-    hidden = jnp.dot(x_all, w_both, preferred_element_type=jnp.float32)
-    sums = row_sums(lambda start, count: hidden, split_rows)
-    grad_out, _ = lax.optimization_barrier((grad_out, hidden))
+    half = w_both.shape[1] // 2
+    gate_part = jnp.dot(x_all, w_both[:, :half], preferred_element_type=jnp.float32)
+    up_part = jnp.dot(x_all, w_both[:, half:], preferred_element_type=jnp.float32)
+    gate_sums = row_sums(lambda start, count: gate_part, split_rows)
+    grad_out, _, _ = lax.optimization_barrier((grad_out, gate_part, up_part))
+    sums = jnp.concatenate([gate_sums, row_sums_paired(up_part)], axis=1)
     grad_all = group_gather(grad_out)
     act_partial = lax.dot_general(grad_all, w_down, outer, preferred_element_type=jnp.float32)
     act_sums, act_partial = lax.optimization_barrier((sums, act_partial))

time: 236 us -> 259 us (1.097)
  local copies, waits for them, and re-layouts: 31.7 us -> 42.8 us
  starting transfers between devices: 31.2 us -> 35.5 us
  matrix products: 42 us -> 45.4 us
    dot_general x0 -> x1, local copies, waits for them, and re-layouts: none -> 5.04 us  [local(): jnp.dot(x_all, w_both[:, half:], preferred_element_type=jnp.float32)]
    another operation x1 -> x2, local copies, waits for them, and re-layouts: 4.21 us -> 8.38 us  [row_sums_paired(): keep = jnp.take(blocks, core, axis=1)]
    ppermute x3 -> x6, starting transfers between devices: 4.11 us -> 7.49 us  [row_sums_paired(): lax.ppermute(piece, 'row', [(i, (i + 2 * hop) % parts) for i in range(par...]
    all_to_all x2, waiting for transfers between devices: 48.8 us -> 51.4 us  [group_gather(): pieces = lax.all_to_all(copies, ('col', 'depth'), 0, 0)]
    dot_general x1 -> x2, matrix products: 9.65 us -> 12.2 us  [the longest x1 6.15 us: local(): jnp.dot(x_all, w_both[:, half:], preferred_element_type=jnp.float32)]
    unnamed x24 -> x26, local copies, waits for them, and re-layouts: 20.3 us -> 22.2 us
    ppermute x3 -> x6, waiting for transfers between devices: 12.4 us -> 13.9 us  [row_sums_paired(): lax.ppermute(piece, 'row', [(i, (i + 2 * hop) % parts) for i in range(par...]
  transfers between devices with their start and end apart: 11 -> 15, of which waited for: 9 -> 9; matrix products, arithmetic and copies ran while one was open for 32% -> 37% of each run, Pallas kernels for 0% -> 0%
where the time goes in v10:
time: 259 us; the launch traced here: 258 us
  waiting for transfers between devices  98.8 us (38%)
  matrix products  45.4 us (18%)
  local copies, waits for them, and re-layouts  42.8 us (17%)
  starting transfers between devices  35.5 us (14%)
  other arithmetic  21.2 us (8%)
  between operations  14.2 us (5%)
    all_to_all x2, waiting for transfers between devices, group_gather(): pieces = lax.all_to_all(copies, ('col', 'depth'), 0, 0)  51.4 us
    unnamed x26, local copies, waits for them, and re-layouts  22.2 us
    all_gather x2, waiting for transfers between devices, row_gather(): return lax.all_gather(block, 'row', axis=0, tiled=True)  22 us
    ppermute x6, waiting for transfers between devices, row_sums_paired(): lax.ppermute(piece, 'row', [(i, (i + 2 * hop) % parts) for i in range(par...  13.9 us
    all_to_all x2, starting transfers between devices, group_gather(): pieces = lax.all_to_all(copies, ('col', 'depth'), 0, 0)  13.2 us
    all_to_all x2, starting transfers between devices, group_sums(): lax.all_to_all(full.reshape((parts, rows) + full.shape[1:]), ('col', 'dep...  11.9 us
    all_to_all x2, waiting for transfers between devices, group_sums(): lax.all_to_all(full.reshape((parts, rows) + full.shape[1:]), ('col', 'dep...  9.34 us
    dot_general x1, matrix products, input_term(): lax.dot_general(grads_all, w_both, outer, preferred_element_type=jnp.floa...  8.59 us
  transfers between devices with their start and end apart: 15, of which 9 were waited for; matrix products, arithmetic and copies ran while one was open for 37% of the time, Pallas kernels for 0%

profile of v10, /device:TPU:1, one launch (start us, length us, event | category | flops | bytes accessed | tf_op | source)
XLA Modules:
  0.0 257.9 jit_solution(15267397066652089685)
XLA Ops:
  7.2 2.5 broadcast_in_dim.78
  9.7 8.6 %all-to-all-start = ((bf16[16,64,1024]{2,1,0:T(8,128)(2,1)}), bf16[16,64,1024]{2,1,0:T(8,128)(2,1)}, u32[]{:S(2)}, u32[]{:S(2)}) async-start(bf16[16,64,1024]{2,1,0:T(8,128)(2,1)} %broadcast_in_dim.78), calls=%async_computation | async-start | bytes 4194304 | tf_op jit(solution)/shard_map/all_to_all | solution.py:87
  18.4 2.9 %copy.20 = bf16[1024,896]{0,1:T(8,128)(2,1)S(1)} copy(bf16[1024,896]{1,0:T(8,128)(2,1)} %param.15) | data formatting | bytes 3670016 | tf_op args[1]
  21.5 1.4 bitcast_select_fusion.3
  22.9 26.4 %all-to-all-done = bf16[16,64,1024]{2,1,0:T(8,128)(2,1)} async-done(((bf16[16,64,1024]{2,1,0:T(8,128)(2,1)}), bf16[16,64,1024]{2,1,0:T(8,128)(2,1)}, u32[]{:S(2)}, u32[]{:S(2)}) %all-to-all-start) | async-done | bytes 2097184 | tf_op jit(solution)/shard_map/all_to_all | solution.py:87
  49.3 6.1 %convolution_bitcast_fusion.2 = f32[1024,896]{0,1:T(8,128)} fusion(bf16[1024,896]{0,1:T(8,128)(2,1)} %bitcast_select_fusion.3, bf16[1024,1024]{1,0:T(8,128)(2,1)} %bitcast.1), kind=kOutput, calls=%fused_computation.14 | convolution fusion | flops 1879048192 | bytes 7602176 | tf_op jit(solution)/shard_map/dot_general | solution.py:108
  55.5 2.9 %copy.22 = bf16[1024,896]{0,1:T(8,128)(2,1)S(1)} copy(bf16[1024,896]{1,0:T(8,128)(2,1)} %param.16) | data formatting | bytes 3670016 | tf_op args[2]
  58.6 1.4 bitcast_select_fusion.1
  60.0 6.1 %convolution_bitcast_fusion.1 = f32[1024,896]{0,1:T(8,128)} fusion(bf16[1024,896]{0,1:T(8,128)(2,1)} %bitcast_select_fusion.1, bf16[1024,1024]{1,0:T(8,128)(2,1)} %bitcast.1), kind=kOutput, calls=%fused_computation.13 | convolution fusion | flops 1879048192 | bytes 7602176 | tf_op jit(solution)/shard_map/dot_general | solution.py:109
  66.1 5.0 %copy.23 = f32[1024,896]{1,0:T(8,128)} copy(f32[1024,896]{0,1:T(8,128)} %convolution_bitcast_fusion.1) | data formatting | bytes 7340032 | tf_op jit(solution)/shard_map/dot_general | solution.py:109
  71.2 4.2 %constant_dynamic-slice_fusion.3 = (f32[4,1,128,896]{3,2,1,0:T(8,128)}, f32[4,1,128,896]{3,2,1,0:T(8,128)}) fusion(f32[4,2,128,896]{3,2,1,0:T(8,128)} %bitcast.88, s32[]{:T(128)S(6)} %select_n.117, s32[]{:T(128)S(6)} %select_n.119), kind=kLoop, calls=%fused_computation.49 | loop fusion | bytes 7340040 | tf_op jit(solution)/shard_map/jit(_take) | solution.py:59
  75.4 1.8 copy.31
  77.2 1.4 select_bitcast_fusion.1
  78.5 1.8 collective-permute-start
  80.3 1.6 broadcast_in_dim.81
  81.9 4.6 %all-to-all-start.1 = ((bf16[16,64,1024]{2,1,0:T(8,128)(2,1)}), bf16[16,64,1024]{2,1,0:T(8,128)(2,1)}, u32[]{:S(2)}, u32[]{:S(2)}) async-start(bf16[16,64,1024]{2,1,0:T(8,128)(2,1)} %broadcast_in_dim.81), calls=%async_computation.2 | async-start | bytes 4194304 | tf_op jit(solution)/shard_map/all_to_all | solution.py:87
  86.7 1.8 copy.30
  88.5 3.0 %fusion.20 = (bf16[4,128,896]{1,2,0:T(8,128)(2,1)S(1)}, f32[4,128,896]{1,2,0:T(8,128)}) fusion(f32[4,128,896]{1,2,0:T(8,128)} %collective-permute-done, f32[4,1,128,896]{2,3,0,1:T(8,128)S(1)} %copy.30, pred[]{:T(512)S(6)} %and.63), kind=kLoop, calls=%fused_computation.57 | loop fusion | flops 1376256 | bytes 6422529 | tf_op jit(solution)/shard_map/convert_element_type | solution.py:61
  91.6 2.6 %collective-permute-start.3 = (bf16[128,896]{0,1:T(8,128)(2,1)S(1)}, bf16[128,896]{0,1:T(8,128)(2,1)S(1)}, u32[]{:S(2)}, u32[]{:S(2)}) collective-permute-start(bf16[128,896]{0,1:T(8,128)(2,1)S(1)} %get-tuple-element.77), channel_id=1, source_target_pairs={{0,96},{16,112},{32,0},{48,16},{64,32},{80,48},{96,64},{112,80},{1... | collective-permute-start | bytes 688136 | tf_op jit(solution)/shard_map/ppermute | solution.py:65
  95.3 25.0 %all-to-all-done.1 = bf16[16,64,1024]{2,1,0:T(8,128)(2,1)} async-done(((bf16[16,64,1024]{2,1,0:T(8,128)(2,1)}), bf16[16,64,1024]{2,1,0:T(8,128)(2,1)}, u32[]{:S(2)}, u32[]{:S(2)}) %all-to-all-start.1) | async-done | bytes 2097184 | tf_op jit(solution)/shard_map/all_to_all | solution.py:87
  120.3 2.8 %broadcast_in_dim.83 = pred[896,8,128]{2,1,0:T(8,128)(4,1)S(1)} broadcast(pred[896,8]{1,0:T(8,128)(4,1)S(1)} %bitcast.95), dimensions={0,1} | broadcast | bytes 924672 | tf_op jit(solution)/shard_map/broadcast_in_dim | solution.py:10
  123.1 6.7 %fusion.9 = f32[1024,896]{1,0:T(8,128)} fusion(bf16[1024,1024]{1,0:T(8,128)(2,1)} %bitcast.12, bf16[896,1024]{1,0:T(8,128)(2,1)} %param.17, pred[112,8,8,128]{3,2,1,0:T(8,128)(4,1)S(1)} %bitcast.92), kind=kOutput, calls=%fused_computation.21 | convolution fusion | flops 1879965696 | bytes 8519680 | tf_op jit(solution)/shard_map/dot_general | solution.py:114
  129.8 1.1 fusion.15
  130.9 1.1 pad_maximum_fusion
  133.1 4.2 %constant_dynamic-slice_fusion.1 = (f32[4,1,128,896]{3,2,1,0:T(8,128)}, f32[4,1,128,896]{3,2,1,0:T(8,128)}) fusion(f32[4,2,128,896]{3,2,1,0:T(8,128)} %bitcast.89, s32[]{:T(128)S(6)} %select_n.117, s32[]{:T(128)S(6)} %select_n.119), kind=kLoop, calls=%fused_computation.47 | loop fusion | bytes 7340040 | tf_op jit(solution)/shard_map/jit(_take) | solution.py:59
  137.3 1.8 copy.33
  139.1 1.4 select_bitcast_fusion
  141.3 1.8 copy.32
  143.1 2.1 collective-permute-done.4
  145.2 1.7 fusion.19
  147.1 2.7 %collective-permute-start.7 = (bf16[128,896]{0,1:T(8,128)(2,1)S(1)}, bf16[128,896]{0,1:T(8,128)(2,1)S(1)}, u32[]{:S(2)}, u32[]{:S(2)}) collective-permute-start(bf16[128,896]{0,1:T(8,128)(2,1)S(1)} %get-tuple-element.74), channel_id=1, source_target_pairs={{0,96},{16,112},{32,0},{48,16},{64,32},{80,48},{96,64},{112,80},{1... | collective-permute-start | bytes 688136 | tf_op jit(solution)/shard_map/ppermute | solution.py:65
  150.8 6.7 %collective-permute-done.7 = bf16[128,896]{0,1:T(8,128)(2,1)S(1)} collective-permute-done((bf16[128,896]{0,1:T(8,128)(2,1)S(1)}, bf16[128,896]{0,1:T(8,128)(2,1)S(1)}, u32[]{:S(2)}, u32[]{:S(2)}) %collective-permute-start.7) | collective-permute-done | bytes 229408 | tf_op jit(solution)/shard_map/ppermute | solution.py:65
  157.5 1.8 collective-permute-done.6
  159.3 5.4 %collective-permute-done.5 = bf16[128,896]{0,1:T(8,128)(2,1)S(1)} collective-permute-done((bf16[128,896]{0,1:T(8,128)(2,1)S(1)}, bf16[128,896]{0,1:T(8,128)(2,1)S(1)}, u32[]{:S(2)}, u32[]{:S(2)}) %collective-permute-start.5) | collective-permute-done | bytes 229408 | tf_op jit(solution)/shard_map/ppermute | solution.py:65
  166.0 5.8 %convolution_convert_fusion = bf16[1024,1024]{1,0:T(8,128)(2,1)} fusion(bf16[1024,896]{0,1:T(8,128)(2,1)} %all-gather.3.cloned.1.call-done, bf16[896,1024]{1,0:T(8,128)(2,1)} %param.17, pred[112,8,8,128]{3,2,1,0:T(8,128)(4,1)S(1)} %bitcast.93), kind=kOutput, calls=%fused_computation.16 | convolution fusion | flops 1881014272 | bytes 6684672 | tf_op jit(solution)/shard_map/dot_general | solution.py:119
  171.8 7.2 %all-to-all-start.2 = ((bf16[16,64,1024]{2,1,0:T(8,128)(2,1)}), bf16[16,64,1024]{2,1,0:T(8,128)(2,1)S(1)}, u32[]{:S(2)}, u32[]{:S(2)}) async-start(bf16[16,64,1024]{2,1,0:T(8,128)(2,1)} %bitcast.91), calls=%async_computation.3 | async-start | bytes 4194304 | tf_op jit(solution)/shard_map/all_to_all | solution.py:80
  179.1 22.0 %all-gather.5.cloned.1.call-done = bf16[1024,1792]{0,1:T(8,128)(2,1)} async-done(((bf16[128,1792]{0,1:T(8,128)(2,1)}), bf16[1024,1792]{0,1:T(8,128)(2,1)}) %all-gather.5.cloned.1.call-update) | async-done | bytes 3670032 | tf_op jit(solution)/shard_map/all_gather | solution.py:38
  201.1 8.6 %fusion.6 = bf16[1024,1024]{1,0:T(8,128)(2,1)} fusion(bf16[1024,1792]{0,1:T(8,128)(2,1)} %all-gather.5.cloned.1.call-done, bf16[1024,896]{0,1:T(8,128)(2,1)} %bitcast_select_fusion.1, bf16[1024,896]{0,1:T(8,128)(2,1)} %bitcast_select_fusion.3), kind=kOutput, calls=%fused_computation.15 | convolution fusion | flops 3766484992 | bytes 9437184 | tf_op jit(solution)/shard_map/dot_general | solution.py:136
  209.6 2.1 all-to-all-done.2
  211.7 1.3 copy-done
  213.0 4.7 %all-to-all-start.3 = ((bf16[16,64,1024]{2,1,0:T(8,128)(2,1)}), bf16[16,64,1024]{2,1,0:T(8,128)(2,1)S(1)}, u32[]{:S(2)}, u32[]{:S(2)}) async-start(bf16[16,64,1024]{2,1,0:T(8,128)(2,1)} %bitcast.90), calls=%async_computation.4 | async-start | bytes 4194304 | tf_op jit(solution)/shard_map/all_to_all | solution.py:80
  217.7 5.5 %select_convert_fusion = bf16[896,1024]{1,0:T(8,128)(2,1)} fusion(pred[112,8,8,128]{3,2,1,0:T(8,128)(4,1)S(1)} %bitcast.94, bf16[1024,896]{0,1:T(8,128)(2,1)} %all-gather.3.cloned.1.call-done, bf16[1024,1024]{1,0:T(8,128)(2,1)} %bitcast.12), kind=kOutput, calls=%fused_computation.11 | convolution fusion | flops 1880883200 | bytes 6684672 | tf_op jit(solution)/shard_map/dot_general | solution.py:122
  223.1 2.7 %reduce_sum.24 = bf16[64,1024]{1,0:T(8,128)(2,1)} reduce(bf16[16,64,1024]{2,1,0:T(8,128)(2,1)} %copy-done, bf16[]{:T(256)} %constant.93.clone.1), dimensions={0}, to_apply=%region_1.5 | reduce | flops 983040 | bytes 2228226 | tf_op jit(solution)/shard_map/reduce_sum | solution.py:81
  225.8 6.7 %convolution_bitcast_fusion = bf16[1024,1792]{0,1:T(8,128)(2,1)S(1)} fusion(bf16[1024,1792]{0,1:T(8,128)(2,1)} %all-gather.5.cloned.1.call-done, bf16[1024,1024]{1,0:T(8,128)(2,1)} %bitcast.1), kind=kOutput, calls=%fused_computation.4 | convolution fusion | flops 3758096384 | bytes 9437184 | tf_op jit(solution)/shard_map/dot_general | solution.py:128
  232.5 2.9 %fusion.1 = (bf16[1024,896]{0,1:T(8,128)(2,1)}, bf16[1024,896]{0,1:T(8,128)(2,1)}) fusion(bf16[1024,1792]{0,1:T(8,128)(2,1)S(1)} %convolution_bitcast_fusion, pred[1024,7]{0,1:T(8,128)(4,1)S(1)} %bitcast.99, pred[1024,7]{0,1:T(8,128)(4,1)S(1)} %bitcast.97), kind=kLoop, calls=%fused_computation.6 | loop fusion | flops 1835008 | bytes 7354368 | tf_op jit(solution)/shard_map/convert_element_type | solution.py:133
  235.4 3.8 %copy.28 = bf16[1024,896]{1,0:T(8,128)(2,1)} copy(bf16[1024,896]{0,1:T(8,128)(2,1)} %get-tuple-element.66) | data formatting | bytes 3670016
  239.2 3.8 %copy.29 = bf16[1024,896]{1,0:T(8,128)(2,1)} copy(bf16[1024,896]{0,1:T(8,128)(2,1)} %get-tuple-element.65) | data formatting | bytes 3670016
  243.0 7.3 %all-to-all-done.3 = bf16[16,64,1024]{2,1,0:T(8,128)(2,1)S(1)} async-done(((bf16[16,64,1024]{2,1,0:T(8,128)(2,1)}), bf16[16,64,1024]{2,1,0:T(8,128)(2,1)S(1)}, u32[]{:S(2)}, u32[]{:S(2)}) %all-to-all-start.3) | async-done | bytes 2097184 | tf_op jit(solution)/shard_map/all_to_all | solution.py:80
  (46 shorter events, 7.1 us)
Async XLA Ops:
  9.7 39.7 %all-to-all-start = ((bf16[16,64,1024]{2,1,0:T(8,128)(2,1)}), bf16[16,64,1024]{2,1,0:T(8,128)(2,1)}, u32[]{:S(2)}, u32[]{:S(2)}) async-start(bf16[16,64,1024]{2,1,0:T(8,128)(2,1)} %broadcast_in_dim.78), calls=%async_computation | async-start | bytes 4194304 | tf_op jit(solution)/shard_map/all_to_all | solution.py:87
  18.3 3.0 %copy-start.5 = (s32[8,7]{1,0:T(8,128)S(1)}, s32[8,7]{1,0:T(8,128)}, u32[]{:S(2)}) copy-start(s32[8,7]{1,0:T(8,128)} %param.19) | copy-start | bytes 676
  18.3 3.0 %copy-start.6 = (s32[8,7]{1,0:T(8,128)S(1)}, s32[8,7]{1,0:T(8,128)}, u32[]{:S(2)}) copy-start(s32[8,7]{1,0:T(8,128)} %param.18) | copy-start | bytes 676
  18.4 112.6 %reduce-scatter.2.cloned.1.call-start = ((), (), s32[]{:S(2)}) async-start(), calls=%async_computation.5 | async-start | bytes 4128768 | tf_op jit(solution)/shard_map/reduce_scatter | solution.py:32
  77.2 3.2 %copy-start.3 = (bf16[64,1024]{1,0:T(8,128)(2,1)S(1)}, bf16[64,1024]{1,0:T(8,128)(2,1)}, u32[]{:S(2)}) copy-start(bf16[64,1024]{1,0:T(8,128)(2,1)} %param.21) | copy-start | bytes 393220
  78.5 10.0 %collective-permute-start = (f32[4,128,896]{1,2,0:T(8,128)}, f32[4,128,896]{1,2,0:T(8,128)}, u32[]{:S(2)}, u32[]{:S(2)}) collective-permute-start(f32[4,128,896]{1,2,0:T(8,128)} %select_bitcast_fusion.1), channel_id=1, source_target_pairs={{0,16},{16,0},{32,48},{48,32},{64,80},{80,64},{96,112},{112,96},{1... | collective-permute-start | bytes 5505032 | tf_op jit(solution)/shard_map/ppermute | solution.py:60
  81.9 4.8 %copy-start.4 = (s32[7,8]{1,0:T(8,128)S(1)}, s32[7,8]{1,0:T(8,128)}, u32[]{:S(2)}) copy-start(s32[7,8]{1,0:T(8,128)} %param.20) | copy-start | bytes 676
  81.9 38.3 %all-to-all-start.1 = ((bf16[16,64,1024]{2,1,0:T(8,128)(2,1)}), bf16[16,64,1024]{2,1,0:T(8,128)(2,1)}, u32[]{:S(2)}, u32[]{:S(2)}) async-start(bf16[16,64,1024]{2,1,0:T(8,128)(2,1)} %broadcast_in_dim.81), calls=%async_computation.2 | async-start | bytes 4194304 | tf_op jit(solution)/shard_map/all_to_all | solution.py:87
  86.5 78.4 %all-gather.3.cloned.1.call-start = ((), (), s32[]{:S(2)}) async-start(), calls=%async_computation.6 | async-start | bytes 2064384 | tf_op jit(solution)/shard_map/all_gather | solution.py:38
  91.6 38.2 %collective-permute-start.3 = (bf16[128,896]{0,1:T(8,128)(2,1)S(1)}, bf16[128,896]{0,1:T(8,128)(2,1)S(1)}, u32[]{:S(2)}, u32[]{:S(2)}) collective-permute-start(bf16[128,896]{0,1:T(8,128)(2,1)S(1)} %get-tuple-element.77), channel_id=1, source_target_pairs={{0,96},{16,112},{32,0},{48,16},{64,32},{80,48},{96,64},{112,80},{1... | collective-permute-start | bytes 688136 | tf_op jit(solution)/shard_map/ppermute | solution.py:65
  94.2 35.6 %collective-permute-start.2 = (bf16[128,896]{0,1:T(8,128)(2,1)S(1)}, bf16[128,896]{0,1:T(8,128)(2,1)S(1)}, u32[]{:S(2)}, u32[]{:S(2)}) collective-permute-start(bf16[128,896]{0,1:T(8,128)(2,1)S(1)} %get-tuple-element.78), channel_id=1, source_target_pairs={{0,64},{16,80},{32,96},{48,112},{64,0},{80,16},{96,32},{112,48},{1... | collective-permute-start | bytes 688136 | tf_op jit(solution)/shard_map/ppermute | solution.py:65
  94.7 35.1 %collective-permute-start.1 = (bf16[128,896]{0,1:T(8,128)(2,1)S(1)}, bf16[128,896]{0,1:T(8,128)(2,1)S(1)}, u32[]{:S(2)}, u32[]{:S(2)}) collective-permute-start(bf16[128,896]{0,1:T(8,128)(2,1)S(1)} %get-tuple-element.76), channel_id=1, source_target_pairs={{0,32},{16,48},{32,64},{48,80},{64,96},{80,112},{96,0},{112,16},{1... | collective-permute-start | bytes 688136 | tf_op jit(solution)/shard_map/ppermute | solution.py:65
  123.1 6.7 %copy-start.1 = (pred[896,8,128]{2,1,0:T(8,128)(4,1)}, pred[896,8,128]{2,1,0:T(8,128)(4,1)S(1)}, u32[]{:S(2)}) copy-start(pred[896,8,128]{2,1,0:T(8,128)(4,1)S(1)} %broadcast_in_dim.83) | copy-start | bytes 2752516
  132.9 68.2 %all-gather.5.cloned.1.call-start = ((), (), s32[]{:S(2)}) async-start(), calls=%async_computation.7 | async-start | bytes 4128768 | tf_op jit(solution)/shard_map/all_gather | solution.py:38
  140.4 4.8 %collective-permute-start.4 = (f32[4,128,896]{1,2,0:T(8,128)}, f32[4,128,896]{1,2,0:T(8,128)}, u32[]{:S(2)}, u32[]{:S(2)}) collective-permute-start(f32[4,128,896]{1,2,0:T(8,128)} %select_bitcast_fusion), channel_id=1, source_target_pairs={{0,16},{16,0},{32,48},{48,32},{64,80},{80,64},{96,112},{112,96},{1... | collective-permute-start | bytes 5505032 | tf_op jit(solution)/shard_map/ppermute | solution.py:60
  147.1 10.5 %collective-permute-start.7 = (bf16[128,896]{0,1:T(8,128)(2,1)S(1)}, bf16[128,896]{0,1:T(8,128)(2,1)S(1)}, u32[]{:S(2)}, u32[]{:S(2)}) collective-permute-start(bf16[128,896]{0,1:T(8,128)(2,1)S(1)} %get-tuple-element.74), channel_id=1, source_target_pairs={{0,96},{16,112},{32,0},{48,16},{64,32},{80,48},{96,64},{112,80},{1... | collective-permute-start | bytes 688136 | tf_op jit(solution)/shard_map/ppermute | solution.py:65
  149.8 9.5 %collective-permute-start.6 = (bf16[128,896]{0,1:T(8,128)(2,1)S(1)}, bf16[128,896]{0,1:T(8,128)(2,1)S(1)}, u32[]{:S(2)}, u32[]{:S(2)}) collective-permute-start(bf16[128,896]{0,1:T(8,128)(2,1)S(1)} %get-tuple-element.75), channel_id=1, source_target_pairs={{0,64},{16,80},{32,96},{48,112},{64,0},{80,16},{96,32},{112,48},{1... | collective-permute-start | bytes 688136 | tf_op jit(solution)/shard_map/ppermute | solution.py:65
  150.2 14.5 %collective-permute-start.5 = (bf16[128,896]{0,1:T(8,128)(2,1)S(1)}, bf16[128,896]{0,1:T(8,128)(2,1)S(1)}, u32[]{:S(2)}, u32[]{:S(2)}) collective-permute-start(bf16[128,896]{0,1:T(8,128)(2,1)S(1)} %get-tuple-element.73), channel_id=1, source_target_pairs={{0,32},{16,48},{32,64},{48,80},{64,96},{80,112},{96,0},{112,16},{1... | collective-permute-start | bytes 688136 | tf_op jit(solution)/shard_map/ppermute | solution.py:65
  164.8 1.2 copy-start.2
  171.8 39.9 %all-to-all-start.2 = ((bf16[16,64,1024]{2,1,0:T(8,128)(2,1)}), bf16[16,64,1024]{2,1,0:T(8,128)(2,1)S(1)}, u32[]{:S(2)}, u32[]{:S(2)}) async-start(bf16[16,64,1024]{2,1,0:T(8,128)(2,1)} %bitcast.91), calls=%async_computation.3 | async-start | bytes 4194304 | tf_op jit(solution)/shard_map/all_to_all | solution.py:80
  211.7 1.3 copy-start
  213.0 37.3 %all-to-all-start.3 = ((bf16[16,64,1024]{2,1,0:T(8,128)(2,1)}), bf16[16,64,1024]{2,1,0:T(8,128)(2,1)S(1)}, u32[]{:S(2)}, u32[]{:S(2)}) async-start(bf16[16,64,1024]{2,1,0:T(8,128)(2,1)} %bitcast.90), calls=%async_computation.4 | async-start | bytes 4194304 | tf_op jit(solution)/shard_map/all_to_all | solution.py:80
Sparse Core Ops, SparseCore 0:
  55.6 32.7 reduce-scatter.1
  133.0 31.1 all-gather.2
  166.4 34.5 all-gather.4

commit v11 on v9

--- a/solution.py
+++ b/solution.py
@@ -52,12 +52,12 @@
     chips = parts // 2
     rows = full.shape[0] // parts
     member = lax.axis_index("row")
-    core = member % 2
     chip = member // 2
     blocks = full.reshape((chips, 2, rows) + full.shape[1:])
-    give = jnp.take(blocks, 1 - core, axis=1)
-    keep = jnp.take(blocks, core, axis=1)
-    pair = keep + lax.ppermute(give, "row", [(i, i ^ 1) for i in range(parts)])
+    even, odd = blocks[:, 0], blocks[:, 1]
+    from_even = lax.ppermute(odd, "row", [(2 * i, 2 * i + 1) for i in range(chips)])
+    from_odd = lax.ppermute(even, "row", [(2 * i + 1, 2 * i) for i in range(chips)])
+    pair = jnp.where(member % 2 == 0, even + from_odd, odd + from_even)
     sent = pair.astype(jnp.bfloat16)
     total = jnp.take(pair, chip, axis=0)
     for hop in range(1, chips):

time: 236 us -> 238 us (level)
  starting transfers between devices: 31.2 us -> 36.8 us
  waiting for transfers between devices: 97 us -> 93.3 us
    ppermute x1 -> x2, starting transfers between devices: 1.18 us -> 6.87 us  [the longest x1 5.59 us: row_sums_paired(): lax.ppermute(even, 'row', [(2 * i + 1, 2 * i) for i in range(chips)])]
    another operation x1 -> x0, local copies, waits for them, and re-layouts: 4.21 us -> none  [row_sums_paired(): keep = jnp.take(blocks, core, axis=1)]
    slice x0 -> x1, local copies, waits for them, and re-layouts: none -> 4.2 us  [row_sums_paired(): even, odd = (blocks[:, 0], blocks[:, 1])]
    ppermute x3, waiting for transfers between devices: 12.4 us -> 9.75 us  [row_sums_paired(): lax.ppermute(piece, 'row', [(i, (i + 2 * hop) % parts) for i in range(par...]
  transfers between devices with their start and end apart: 11 -> 12, of which waited for: 9 -> 8; matrix products, arithmetic and copies ran while one was open for 32% -> 32% of each run, Pallas kernels for 0% -> 0%
where the time goes in v11:
time: 238 us; the launch traced here: 237 us
  waiting for transfers between devices  93.3 us (39%)
  matrix products  42 us (18%)
  starting transfers between devices  36.8 us (15%)
  local copies, waits for them, and re-layouts  32.6 us (14%)
  other arithmetic  18.7 us (8%)
  between operations  13.9 us (6%)
    all_to_all x2, waiting for transfers between devices, group_gather(): pieces = lax.all_to_all(copies, ('col', 'depth'), 0, 0)  48.8 us
    all_gather x2, waiting for transfers between devices, row_gather(): return lax.all_gather(block, 'row', axis=0, tiled=True)  22.7 us
    unnamed x24, local copies, waits for them, and re-layouts  21.2 us
    all_to_all x2, starting transfers between devices, group_sums(): lax.all_to_all(full.reshape((parts, rows) + full.shape[1:]), ('col', 'dep...  13 us
    all_to_all x2, starting transfers between devices, group_gather(): pieces = lax.all_to_all(copies, ('col', 'depth'), 0, 0)  12.7 us
    ppermute x3, waiting for transfers between devices, row_sums_paired(): lax.ppermute(piece, 'row', [(i, (i + 2 * hop) % parts) for i in range(par...  9.75 us
    dot_general x1, matrix products, local(): hidden = jnp.dot(x_all, w_both, preferred_element_type=jnp.float32)  9.66 us
    dot_general x1, matrix products, input_term(): lax.dot_general(grads_all, w_both, outer, preferred_element_type=jnp.floa...  8.53 us
  transfers between devices with their start and end apart: 12, of which 8 were waited for; matrix products, arithmetic and copies ran while one was open for 32% of the time, Pallas kernels for 0%

profile of v11, /device:TPU:1, one launch (start us, length us, event | category | flops | bytes accessed | tf_op | source)
XLA Modules:
  0.0 237.3 jit_solution(3872171325009791896)
XLA Ops:
  7.2 2.5 %broadcast_in_dim.74 = bf16[16,64,1024]{2,1,0:T(8,128)(2,1)} broadcast(bf16[64,1024]{1,0:T(8,128)(2,1)} %param.10), dimensions={1,2} | broadcast | bytes 2228224 | tf_op jit(solution)/shard_map/broadcast_in_dim | solution.py:86
  9.7 8.8 %all-to-all-start = ((bf16[16,64,1024]{2,1,0:T(8,128)(2,1)}), bf16[16,64,1024]{2,1,0:T(8,128)(2,1)}, u32[]{:S(2)}, u32[]{:S(2)}) async-start(bf16[16,64,1024]{2,1,0:T(8,128)(2,1)} %broadcast_in_dim.74), calls=%async_computation | async-start | bytes 4194304 | tf_op jit(solution)/shard_map/all_to_all | solution.py:87
  18.5 0.1 copy.19
  18.6 0.1 copy.21
  18.7 0.1 broadcast_bitcast_fusion
  18.8 0.1 broadcast_bitcast_fusion.1
  18.9 2.9 %copy.20 = bf16[1024,896]{0,1:T(8,128)(2,1)S(1)} copy(bf16[1024,896]{1,0:T(8,128)(2,1)} %param.11) | data formatting | bytes 3670016 | tf_op args[1]
  21.8 3.8 %copy.22 = bf16[1024,896]{0,1:T(8,128)(2,1)} copy(bf16[1024,896]{1,0:T(8,128)(2,1)} %param.12) | data formatting | bytes 3670016 | tf_op args[2]
  25.6 3.6 %bitcast_select_fusion.1 = (bf16[1024,896]{0,1:T(8,128)(2,1)}, bf16[1024,896]{0,1:T(8,128)(2,1)}) fusion(bf16[1024,896]{0,1:T(8,128)(2,1)} %copy.22, pred[1024,7]{0,1:T(8,128)(4,1)S(1)} %bitcast.77, bf16[1024,896]{0,1:T(8,128)(2,1)S(1)} %copy.20, pred[1024,7]{0,1:T(8,128)(4,1)S(1)} %bitcast.79), kind=kLoop, calls=%fused_computation.1 | loop fusion | flops 1835008 | bytes 7354368 | tf_op jit(solution)/shard_map/jit(_where)/select_n | solution.py:97
  29.2 20.2 %all-to-all-done = bf16[16,64,1024]{2,1,0:T(8,128)(2,1)} async-done(((bf16[16,64,1024]{2,1,0:T(8,128)(2,1)}), bf16[16,64,1024]{2,1,0:T(8,128)(2,1)}, u32[]{:S(2)}, u32[]{:S(2)}) %all-to-all-start) | async-done | bytes 2097184 | tf_op jit(solution)/shard_map/all_to_all | solution.py:87
  49.5 9.7 %convolution_bitcast_fusion.1 = f32[1024,1792]{0,1:T(8,128)} fusion(bf16[1024,1024]{1,0:T(8,128)(2,1)} %bitcast.2, bf16[1024,896]{0,1:T(8,128)(2,1)} %get-tuple-element.59, bf16[1024,896]{0,1:T(8,128)(2,1)} %get-tuple-element.60), kind=kOutput, calls=%fused_computation.5 | convolution fusion | flops 3765436416 | bytes 13107200 | tf_op jit(solution)/shard_map/dot_general | solution.py:107
  59.1 0.9 copy-done.3
  60.0 1.7 broadcast_in_dim.75
  61.7 3.9 %all-to-all-start.1 = ((bf16[16,64,1024]{2,1,0:T(8,128)(2,1)}), bf16[16,64,1024]{2,1,0:T(8,128)(2,1)S(1)}, u32[]{:S(2)}, u32[]{:S(2)}) async-start(bf16[16,64,1024]{2,1,0:T(8,128)(2,1)} %broadcast_in_dim.75), calls=%async_computation.2 | async-start | bytes 4194304 | tf_op jit(solution)/shard_map/all_to_all | solution.py:87
  65.7 28.5 %all-to-all-done.1 = bf16[16,64,1024]{2,1,0:T(8,128)(2,1)S(1)} async-done(((bf16[16,64,1024]{2,1,0:T(8,128)(2,1)}), bf16[16,64,1024]{2,1,0:T(8,128)(2,1)S(1)}, u32[]{:S(2)}, u32[]{:S(2)}) %all-to-all-start.1) | async-done | bytes 2097184 | tf_op jit(solution)/shard_map/all_to_all | solution.py:87
  94.3 2.8 %broadcast_in_dim.77 = pred[896,8,128]{2,1,0:T(8,128)(4,1)S(1)} broadcast(pred[896,8]{1,0:T(8,128)(4,1)S(1)} %bitcast.76), dimensions={0,1} | broadcast | bytes 924672 | tf_op jit(solution)/shard_map/broadcast_in_dim | solution.py:10
  97.1 5.9 %fusion.4 = f32[1024,896]{1,0:T(8,128)} fusion(bf16[1024,1024]{1,0:T(8,128)(2,1)S(1)} %bitcast.69, bf16[896,1024]{1,0:T(8,128)(2,1)} %param.13, pred[112,8,8,128]{3,2,1,0:T(8,128)(4,1)S(1)} %bitcast.73), kind=kOutput, calls=%fused_computation.15 | convolution fusion | flops 1879965696 | bytes 8519680 | tf_op jit(solution)/shard_map/dot_general | solution.py:111
  103.0 2.1 reduce-scatter.2.cloned.1.call-done
  105.1 2.0 multiply_convert_fusion.2
  107.2 4.2 %fusion.14 = (f32[4,1,128,896]{3,2,1,0:T(8,128)}, f32[4,1,128,896]{3,2,1,0:T(8,128)}) fusion(f32[4,2,128,896]{3,2,1,0:T(8,128)} %bitcast.68), kind=kLoop, calls=%fused_computation.41 | loop fusion | bytes 7340032 | tf_op jit(solution)/shard_map/slice | solution.py:57
  111.4 1.8 copy.27
  113.2 2.7 %copy.28 = f32[4,1,128,896]{2,3,0,1:T(8,128)} copy(f32[4,1,128,896]{3,2,1,0:T(8,128)} %get-tuple-element.53) | data formatting | bytes 3670016
  115.9 1.3 collective-permute-start.1
  117.2 5.6 %collective-permute-start = (f32[4,128,896]{1,2,0:T(8,128)S(1)}, f32[4,128,896]{1,2,0:T(8,128)}, u32[]{:S(2)}, u32[]{:S(2)}) collective-permute-start(f32[4,128,896]{1,2,0:T(8,128)S(1)} %bitcast.66), channel_id=1, source_target_pairs={{16,0},{48,32},{80,64},{112,96},{17,1},{49,33},{81,65},{113,97},{1... | collective-permute-start | bytes 5505032 | tf_op jit(solution)/shard_map/ppermute | solution.py:59
  122.8 2.6 %collective-permute-done = f32[4,128,896]{1,2,0:T(8,128)} collective-permute-done((f32[4,128,896]{1,2,0:T(8,128)S(1)}, f32[4,128,896]{1,2,0:T(8,128)}, u32[]{:S(2)}, u32[]{:S(2)}) %collective-permute-start) | collective-permute-done | bytes 1835040 | tf_op jit(solution)/shard_map/ppermute | solution.py:59
  125.4 4.2 %fusion.13 = (bf16[4,128,896]{1,2,0:T(8,128)(2,1)S(1)}, f32[4,128,896]{1,2,0:T(8,128)}) fusion(f32[4,128,896]{1,2,0:T(8,128)} %collective-permute-done.1, f32[4,1,128,896]{2,3,0,1:T(8,128)} %copy.28, f32[4,128,896]{1,2,0:T(8,128)} %collective-permute-done, f32[4,1,128,896]{2,3,0,1:T(8,128)S(1)} %copy.27, pred[]{:T(512)S(6)} %eq.8), kind=kLoop, calls=%fused_computation.40 | loop fusion | flops 1835008 | bytes 10092545 | tf_op jit(solution)/shard_map/convert_element_type | solution.py:61
  129.6 1.0 collective-permute-start.2
  130.6 1.8 collective-permute-start.4
  132.4 1.4 collective-permute-start.3
  133.8 3.9 %collective-permute-done.2 = bf16[128,896]{0,1:T(8,128)(2,1)S(1)} collective-permute-done((bf16[128,896]{0,1:T(8,128)(2,1)S(1)}, bf16[128,896]{0,1:T(8,128)(2,1)S(1)}, u32[]{:S(2)}, u32[]{:S(2)}) %collective-permute-start.2) | collective-permute-done | bytes 229408 | tf_op jit(solution)/shard_map/ppermute | solution.py:65
  137.7 5.8 %collective-permute-done.3 = bf16[128,896]{0,1:T(8,128)(2,1)S(1)} collective-permute-done((bf16[128,896]{0,1:T(8,128)(2,1)S(1)}, bf16[128,896]{0,1:T(8,128)(2,1)S(1)}, u32[]{:S(2)}, u32[]{:S(2)}) %collective-permute-start.3) | collective-permute-done | bytes 229408 | tf_op jit(solution)/shard_map/ppermute | solution.py:65
  143.5 1.1 fusion.8
  144.7 0.2 multiply_convert_fusion.1
  144.9 0.8 pad_maximum_fusion.5
  145.8 5.8 %convolution_convert_fusion = bf16[1024,1024]{1,0:T(8,128)(2,1)} fusion(bf16[1024,896]{0,1:T(8,128)(2,1)} %all-gather.3.cloned.1.call-done, bf16[896,1024]{1,0:T(8,128)(2,1)} %param.13, pred[112,8,8,128]{3,2,1,0:T(8,128)(4,1)S(1)} %bitcast.74), kind=kOutput, calls=%fused_computation.13 | convolution fusion | flops 1881014272 | bytes 6684672 | tf_op jit(solution)/shard_map/dot_general | solution.py:116
  151.6 6.3 %all-to-all-start.2 = ((bf16[16,64,1024]{2,1,0:T(8,128)(2,1)}), bf16[16,64,1024]{2,1,0:T(8,128)(2,1)S(1)}, u32[]{:S(2)}, u32[]{:S(2)}) async-start(bf16[16,64,1024]{2,1,0:T(8,128)(2,1)} %bitcast.72), calls=%async_computation.3 | async-start | bytes 4194304 | tf_op jit(solution)/shard_map/all_to_all | solution.py:80
  157.8 22.7 %all-gather.5.cloned.1.call-done = bf16[1024,1792]{0,1:T(8,128)(2,1)} async-done(((bf16[128,1792]{0,1:T(8,128)(2,1)}), bf16[1024,1792]{0,1:T(8,128)(2,1)}) %all-gather.5.cloned.1.call-update) | async-done | bytes 3670032 | tf_op jit(solution)/shard_map/all_gather | solution.py:38
  180.5 8.5 %fusion.3 = bf16[1024,1024]{1,0:T(8,128)(2,1)} fusion(bf16[1024,1792]{0,1:T(8,128)(2,1)} %all-gather.5.cloned.1.call-done, bf16[1024,896]{0,1:T(8,128)(2,1)} %get-tuple-element.59, bf16[1024,896]{0,1:T(8,128)(2,1)} %get-tuple-element.60), kind=kOutput, calls=%fused_computation.12 | convolution fusion | flops 3766484992 | bytes 9437184 | tf_op jit(solution)/shard_map/dot_general | solution.py:133
  189.1 1.3 copy-done
  190.4 6.7 %all-to-all-start.3 = ((bf16[16,64,1024]{2,1,0:T(8,128)(2,1)}), bf16[16,64,1024]{2,1,0:T(8,128)(2,1)S(1)}, u32[]{:S(2)}, u32[]{:S(2)}) async-start(bf16[16,64,1024]{2,1,0:T(8,128)(2,1)} %bitcast.71), calls=%async_computation.4 | async-start | bytes 4194304 | tf_op jit(solution)/shard_map/all_to_all | solution.py:80
  197.1 5.5 %select_convert_fusion = bf16[896,1024]{1,0:T(8,128)(2,1)} fusion(pred[112,8,8,128]{3,2,1,0:T(8,128)(4,1)S(1)} %bitcast.75, bf16[1024,896]{0,1:T(8,128)(2,1)} %all-gather.3.cloned.1.call-done, bf16[1024,1024]{1,0:T(8,128)(2,1)} %bitcast.70), kind=kOutput, calls=%fused_computation.9 | convolution fusion | flops 1880883200 | bytes 6684672 | tf_op jit(solution)/shard_map/dot_general | solution.py:119
  202.6 2.7 %reduce_sum.24 = bf16[64,1024]{1,0:T(8,128)(2,1)} reduce(bf16[16,64,1024]{2,1,0:T(8,128)(2,1)} %copy-done, bf16[]{:T(256)} %constant.74.clone.1), dimensions={0}, to_apply=%region_1.2 | reduce | flops 983040 | bytes 2228226 | tf_op jit(solution)/shard_map/reduce_sum | solution.py:81
  205.2 6.7 %convolution_bitcast_fusion = bf16[1024,1792]{0,1:T(8,128)(2,1)S(1)} fusion(bf16[1024,1792]{0,1:T(8,128)(2,1)} %all-gather.5.cloned.1.call-done, bf16[1024,1024]{1,0:T(8,128)(2,1)} %bitcast.2), kind=kOutput, calls=%fused_computation.4 | convolution fusion | flops 3758096384 | bytes 9437184 | tf_op jit(solution)/shard_map/dot_general | solution.py:125
  211.9 3.0 %fusion.1 = (bf16[1024,896]{0,1:T(8,128)(2,1)}, bf16[1024,896]{0,1:T(8,128)(2,1)}) fusion(bf16[1024,1792]{0,1:T(8,128)(2,1)S(1)} %convolution_bitcast_fusion, pred[1024,7]{0,1:T(8,128)(4,1)S(1)} %bitcast.78, pred[1024,7]{0,1:T(8,128)(4,1)S(1)} %bitcast.80), kind=kLoop, calls=%fused_computation.7 | loop fusion | flops 1835008 | bytes 7354368 | tf_op jit(solution)/shard_map/convert_element_type | solution.py:130
  214.9 3.8 %copy.26 = bf16[1024,896]{1,0:T(8,128)(2,1)} copy(bf16[1024,896]{0,1:T(8,128)(2,1)} %get-tuple-element.50) | data formatting | bytes 3670016
  218.7 3.8 %copy.25 = bf16[1024,896]{1,0:T(8,128)(2,1)} copy(bf16[1024,896]{0,1:T(8,128)(2,1)} %get-tuple-element.51) | data formatting | bytes 3670016
  222.5 7.2 %all-to-all-done.3 = bf16[16,64,1024]{2,1,0:T(8,128)(2,1)S(1)} async-done(((bf16[16,64,1024]{2,1,0:T(8,128)(2,1)}), bf16[16,64,1024]{2,1,0:T(8,128)(2,1)S(1)}, u32[]{:S(2)}, u32[]{:S(2)}) %all-to-all-start.3) | async-done | bytes 2097184 | tf_op jit(solution)/shard_map/all_to_all | solution.py:80
  229.7 1.1 reduce_sum.25
  (29 shorter events, 0.4 us)
Async XLA Ops:
  9.7 8.8 %copy-start.4 = (s32[8,7]{1,0:T(8,128)S(1)}, s32[8,7]{1,0:T(8,128)}, u32[]{:S(2)}) copy-start(s32[8,7]{1,0:T(8,128)} %param.14) | copy-start | bytes 676
  9.7 8.9 %copy-start.5 = (s32[8,7]{1,0:T(8,128)S(1)}, s32[8,7]{1,0:T(8,128)}, u32[]{:S(2)}) copy-start(s32[8,7]{1,0:T(8,128)} %param.15) | copy-start | bytes 676
  9.7 39.8 %all-to-all-start = ((bf16[16,64,1024]{2,1,0:T(8,128)(2,1)}), bf16[16,64,1024]{2,1,0:T(8,128)(2,1)}, u32[]{:S(2)}, u32[]{:S(2)}) async-start(bf16[16,64,1024]{2,1,0:T(8,128)(2,1)} %broadcast_in_dim.74), calls=%async_computation | async-start | bytes 4194304 | tf_op jit(solution)/shard_map/all_to_all | solution.py:87
  18.4 86.7 %reduce-scatter.2.cloned.1.call-start = ((), (), s32[]{:S(2)}) async-start(), calls=%async_computation.5 | async-start | bytes 8257536 | tf_op jit(solution)/shard_map/reduce_scatter | solution.py:32
  59.1 0.9 copy-start.3
  61.7 4.0 %copy-start.6 = (s32[7,8]{1,0:T(8,128)S(1)}, s32[7,8]{1,0:T(8,128)}, u32[]{:S(2)}) copy-start(s32[7,8]{1,0:T(8,128)} %param.16) | copy-start | bytes 676
  61.7 32.6 %all-to-all-start.1 = ((bf16[16,64,1024]{2,1,0:T(8,128)(2,1)}), bf16[16,64,1024]{2,1,0:T(8,128)(2,1)S(1)}, u32[]{:S(2)}, u32[]{:S(2)}) async-start(bf16[16,64,1024]{2,1,0:T(8,128)(2,1)} %broadcast_in_dim.75), calls=%async_computation.2 | async-start | bytes 4194304 | tf_op jit(solution)/shard_map/all_to_all | solution.py:87
  65.7 79.0 %all-gather.3.cloned.1.call-start = ((), (), s32[]{:S(2)}) async-start(), calls=%async_computation.6 | async-start | bytes 2064384 | tf_op jit(solution)/shard_map/all_gather | solution.py:38
  94.3 8.7 %copy-start.2 = (bf16[16,64,1024]{2,1,0:T(8,128)(2,1)}, bf16[16,64,1024]{2,1,0:T(8,128)(2,1)S(1)}, u32[]{:S(2)}) copy-start(bf16[16,64,1024]{2,1,0:T(8,128)(2,1)S(1)} %all-to-all-done.1) | copy-start | bytes 6291460
  107.1 73.4 %all-gather.5.cloned.1.call-start = ((), (), s32[]{:S(2)}) async-start(), calls=%async_computation.7 | async-start | bytes 4128768 | tf_op jit(solution)/shard_map/all_gather | solution.py:38
  115.9 6.9 %collective-permute-start.1 = (f32[4,128,896]{1,2,0:T(8,128)}, f32[4,128,896]{1,2,0:T(8,128)}, u32[]{:S(2)}, u32[]{:S(2)}) collective-permute-start(f32[4,128,896]{1,2,0:T(8,128)} %bitcast.67), channel_id=1, source_target_pairs={{0,16},{32,48},{64,80},{96,112},{1,17},{33,49},{65,81},{97,113},{2... | collective-permute-start | bytes 5505032 | tf_op jit(solution)/shard_map/ppermute | solution.py:58
  117.2 8.2 %collective-permute-start = (f32[4,128,896]{1,2,0:T(8,128)S(1)}, f32[4,128,896]{1,2,0:T(8,128)}, u32[]{:S(2)}, u32[]{:S(2)}) collective-permute-start(f32[4,128,896]{1,2,0:T(8,128)S(1)} %bitcast.66), channel_id=1, source_target_pairs={{16,0},{48,32},{80,64},{112,96},{17,1},{49,33},{81,65},{113,97},{1... | collective-permute-start | bytes 5505032 | tf_op jit(solution)/shard_map/ppermute | solution.py:59
  129.6 15.1 %copy-start.1 = (f32[128,1792]{0,1:T(8,128)S(1)}, f32[128,1792]{0,1:T(8,128)}, u32[]{:S(2)}) copy-start(f32[128,1792]{0,1:T(8,128)} %reduce-scatter.2.cloned.1.call-done) | copy-start | bytes 2752516
  129.6 8.1 %collective-permute-start.2 = (bf16[128,896]{0,1:T(8,128)(2,1)S(1)}, bf16[128,896]{0,1:T(8,128)(2,1)S(1)}, u32[]{:S(2)}, u32[]{:S(2)}) collective-permute-start(bf16[128,896]{0,1:T(8,128)(2,1)S(1)} %get-tuple-element.56), channel_id=1, source_target_pairs={{0,32},{16,48},{32,64},{48,80},{64,96},{80,112},{96,0},{112,16},{1... | collective-permute-start | bytes 688136 | tf_op jit(solution)/shard_map/ppermute | solution.py:65
  130.6 7.1 %collective-permute-start.4 = (bf16[128,896]{0,1:T(8,128)(2,1)S(1)}, bf16[128,896]{0,1:T(8,128)(2,1)S(1)}, u32[]{:S(2)}, u32[]{:S(2)}) collective-permute-start(bf16[128,896]{0,1:T(8,128)(2,1)S(1)} %get-tuple-element.57), channel_id=1, source_target_pairs={{0,96},{16,112},{32,0},{48,16},{64,32},{80,48},{96,64},{112,80},{1... | collective-permute-start | bytes 688136 | tf_op jit(solution)/shard_map/ppermute | solution.py:65
  132.4 11.1 %collective-permute-start.3 = (bf16[128,896]{0,1:T(8,128)(2,1)S(1)}, bf16[128,896]{0,1:T(8,128)(2,1)S(1)}, u32[]{:S(2)}, u32[]{:S(2)}) collective-permute-start(bf16[128,896]{0,1:T(8,128)(2,1)S(1)} %get-tuple-element.58), channel_id=1, source_target_pairs={{0,64},{16,80},{32,96},{48,112},{64,0},{80,16},{96,32},{112,48},{1... | collective-permute-start | bytes 688136 | tf_op jit(solution)/shard_map/ppermute | solution.py:65
  151.6 37.5 %all-to-all-start.2 = ((bf16[16,64,1024]{2,1,0:T(8,128)(2,1)}), bf16[16,64,1024]{2,1,0:T(8,128)(2,1)S(1)}, u32[]{:S(2)}, u32[]{:S(2)}) async-start(bf16[16,64,1024]{2,1,0:T(8,128)(2,1)} %bitcast.72), calls=%async_computation.3 | async-start | bytes 4194304 | tf_op jit(solution)/shard_map/all_to_all | solution.py:80
  189.1 1.3 copy-start
  190.4 39.3 %all-to-all-start.3 = ((bf16[16,64,1024]{2,1,0:T(8,128)(2,1)}), bf16[16,64,1024]{2,1,0:T(8,128)(2,1)S(1)}, u32[]{:S(2)}, u32[]{:S(2)}) async-start(bf16[16,64,1024]{2,1,0:T(8,128)(2,1)} %bitcast.71), calls=%async_computation.4 | async-start | bytes 4194304 | tf_op jit(solution)/shard_map/all_to_all | solution.py:80
Sparse Core Ops, SparseCore 0:
  59.3 45.7 reduce-scatter.1
  107.2 26.3 all-gather.2
  145.9 34.5 all-gather.4

commit v12 on v9

--- a/solution.py
+++ b/solution.py
@@ -57,7 +57,8 @@
     blocks = full.reshape((chips, 2, rows) + full.shape[1:])
     give = jnp.take(blocks, 1 - core, axis=1)
     keep = jnp.take(blocks, core, axis=1)
-    pair = keep + lax.ppermute(give, "row", [(i, i ^ 1) for i in range(parts)])
+    moved_in = lax.ppermute(give.astype(jnp.bfloat16), "row", [(i, i ^ 1) for i in range(parts)])
+    pair = keep + moved_in.astype(jnp.float32)
     sent = pair.astype(jnp.bfloat16)
     total = jnp.take(pair, chip, axis=0)
     for hop in range(1, chips):

time: 236 us -> 235 us (level)
    ppermute x3, waiting for transfers between devices: 12.4 us -> 15 us  [row_sums_paired(): lax.ppermute(piece, 'row', [(i, (i + 2 * hop) % parts) for i in range(par...]
  transfers between devices with their start and end apart: 11 -> 11, of which waited for: 9 -> 8; matrix products, arithmetic and copies ran while one was open for 32% -> 31% of each run, Pallas kernels for 0% -> 0%
where the time goes in v12:
time: 235 us; the launch traced here: 234 us
  waiting for transfers between devices  97.3 us (41%)
  matrix products  42 us (18%)
  starting transfers between devices  31.8 us (14%)
  local copies, waits for them, and re-layouts  30.7 us (13%)
  other arithmetic  18.4 us (8%)
  between operations  13.9 us (6%)
    all_to_all x2, waiting for transfers between devices, group_gather(): pieces = lax.all_to_all(copies, ('col', 'depth'), 0, 0)  48.8 us
    all_gather x2, waiting for transfers between devices, row_gather(): return lax.all_gather(block, 'row', axis=0, tiled=True)  23.3 us
    unnamed x24, local copies, waits for them, and re-layouts  19.1 us
    ppermute x3, waiting for transfers between devices, row_sums_paired(): lax.ppermute(piece, 'row', [(i, (i + 2 * hop) % parts) for i in range(par...  15 us
    all_to_all x2, starting transfers between devices, group_sums(): lax.all_to_all(full.reshape((parts, rows) + full.shape[1:]), ('col', 'dep...  13.7 us
    all_to_all x2, starting transfers between devices, group_gather(): pieces = lax.all_to_all(copies, ('col', 'depth'), 0, 0)  12.7 us
    dot_general x1, matrix products, local(): hidden = jnp.dot(x_all, w_both, preferred_element_type=jnp.float32)  9.65 us
    dot_general x1, matrix products, input_term(): lax.dot_general(grads_all, w_both, outer, preferred_element_type=jnp.floa...  8.52 us
  transfers between devices with their start and end apart: 11, of which 8 were waited for; matrix products, arithmetic and copies ran while one was open for 31% of the time, Pallas kernels for 0%

profile of v12, /device:TPU:1, one launch (start us, length us, event | category | flops | bytes accessed | tf_op | source)
XLA Modules:
  0.0 234.1 jit_solution(18047022158019151847)
XLA Ops:
  7.2 2.5 %broadcast_in_dim.83 = bf16[16,64,1024]{2,1,0:T(8,128)(2,1)} broadcast(bf16[64,1024]{1,0:T(8,128)(2,1)} %param.12), dimensions={1,2} | broadcast | bytes 2228224 | tf_op jit(solution)/shard_map/broadcast_in_dim | solution.py:87
  9.7 8.8 %all-to-all-start = ((bf16[16,64,1024]{2,1,0:T(8,128)(2,1)}), bf16[16,64,1024]{2,1,0:T(8,128)(2,1)}, u32[]{:S(2)}, u32[]{:S(2)}) async-start(bf16[16,64,1024]{2,1,0:T(8,128)(2,1)} %broadcast_in_dim.83), calls=%async_computation | async-start | bytes 4194304 | tf_op jit(solution)/shard_map/all_to_all | solution.py:88
  18.5 0.1 copy.19
  18.6 0.1 copy.21
  18.7 0.1 broadcast_bitcast_fusion
  18.9 2.9 %copy.20 = bf16[1024,896]{0,1:T(8,128)(2,1)S(1)} copy(bf16[1024,896]{1,0:T(8,128)(2,1)} %param.13) | data formatting | bytes 3670016 | tf_op args[1]
  21.8 3.8 %copy.22 = bf16[1024,896]{0,1:T(8,128)(2,1)} copy(bf16[1024,896]{1,0:T(8,128)(2,1)} %param.14) | data formatting | bytes 3670016 | tf_op args[2]
  25.6 3.6 %bitcast_select_fusion.1 = (bf16[1024,896]{0,1:T(8,128)(2,1)}, bf16[1024,896]{0,1:T(8,128)(2,1)}) fusion(bf16[1024,896]{0,1:T(8,128)(2,1)} %copy.22, pred[1024,7]{0,1:T(8,128)(4,1)S(1)} %bitcast.75, bf16[1024,896]{0,1:T(8,128)(2,1)S(1)} %copy.20, pred[1024,7]{0,1:T(8,128)(4,1)S(1)} %bitcast.77), kind=kLoop, calls=%fused_computation.1 | loop fusion | flops 1835008 | bytes 7354368 | tf_op jit(solution)/shard_map/jit(_where)/select_n | solution.py:98
  29.2 20.2 %all-to-all-done = bf16[16,64,1024]{2,1,0:T(8,128)(2,1)} async-done(((bf16[16,64,1024]{2,1,0:T(8,128)(2,1)}), bf16[16,64,1024]{2,1,0:T(8,128)(2,1)}, u32[]{:S(2)}, u32[]{:S(2)}) %all-to-all-start) | async-done | bytes 2097184 | tf_op jit(solution)/shard_map/all_to_all | solution.py:88
  49.5 9.7 %convolution_bitcast_fusion.1 = f32[1024,1792]{0,1:T(8,128)} fusion(bf16[1024,1024]{1,0:T(8,128)(2,1)} %bitcast.2, bf16[1024,896]{0,1:T(8,128)(2,1)} %get-tuple-element.69, bf16[1024,896]{0,1:T(8,128)(2,1)} %get-tuple-element.70), kind=kOutput, calls=%fused_computation.5 | convolution fusion | flops 3765436416 | bytes 13107200 | tf_op jit(solution)/shard_map/dot_general | solution.py:108
  59.1 0.9 copy-done.3
  60.0 1.7 broadcast_in_dim.84
  61.7 3.9 %all-to-all-start.1 = ((bf16[16,64,1024]{2,1,0:T(8,128)(2,1)}), bf16[16,64,1024]{2,1,0:T(8,128)(2,1)S(1)}, u32[]{:S(2)}, u32[]{:S(2)}) async-start(bf16[16,64,1024]{2,1,0:T(8,128)(2,1)} %broadcast_in_dim.84), calls=%async_computation.2 | async-start | bytes 4194304 | tf_op jit(solution)/shard_map/all_to_all | solution.py:88
  65.7 28.5 %all-to-all-done.1 = bf16[16,64,1024]{2,1,0:T(8,128)(2,1)S(1)} async-done(((bf16[16,64,1024]{2,1,0:T(8,128)(2,1)}), bf16[16,64,1024]{2,1,0:T(8,128)(2,1)S(1)}, u32[]{:S(2)}, u32[]{:S(2)}) %all-to-all-start.1) | async-done | bytes 2097184 | tf_op jit(solution)/shard_map/all_to_all | solution.py:88
  94.3 2.8 %broadcast_in_dim.86 = pred[896,8,128]{2,1,0:T(8,128)(4,1)S(1)} broadcast(pred[896,8]{1,0:T(8,128)(4,1)S(1)} %bitcast.74), dimensions={0,1} | broadcast | bytes 924672 | tf_op jit(solution)/shard_map/broadcast_in_dim | solution.py:10
  97.1 5.9 %fusion.4 = f32[1024,896]{1,0:T(8,128)} fusion(bf16[1024,1024]{1,0:T(8,128)(2,1)S(1)} %bitcast.65, bf16[896,1024]{1,0:T(8,128)(2,1)} %param.15, pred[112,8,8,128]{3,2,1,0:T(8,128)(4,1)S(1)} %bitcast.71), kind=kOutput, calls=%fused_computation.16 | convolution fusion | flops 1879965696 | bytes 8519680 | tf_op jit(solution)/shard_map/dot_general | solution.py:112
  103.0 2.1 reduce-scatter.2.cloned.1.call-done
  105.1 2.0 multiply_convert_fusion.2
  107.2 1.6 constant_dynamic-slice_fusion
  108.8 0.6 copy.28
  109.4 1.1 bitcast_convert_fusion
  110.6 1.2 collective-permute-start
  111.8 2.8 %constant_dynamic-slice_fusion.1 = f32[4,1,128,896]{3,2,1,0:T(8,128)} fusion(f32[4,2,128,896]{3,2,1,0:T(8,128)} %bitcast.70, s32[]{:T(128)S(6)} %select_n.92), kind=kLoop, calls=%fused_computation.38 | loop fusion | bytes 3670020 | tf_op jit(solution)/shard_map/jit(_take) | solution.py:59
  114.6 1.8 copy.27
  116.4 2.7 %fusion.13 = (bf16[4,128,896]{1,2,0:T(8,128)(2,1)S(1)}, f32[4,128,896]{1,2,0:T(8,128)}) fusion(bf16[4,128,896]{1,2,0:T(8,128)(2,1)} %collective-permute-done, f32[4,1,128,896]{2,3,0,1:T(8,128)S(1)} %copy.27, pred[]{:T(512)S(6)} %and.48), kind=kLoop, calls=%fused_computation.43 | loop fusion | flops 1835008 | bytes 5505025 | tf_op jit(solution)/shard_map/convert_element_type | solution.py:62
  119.2 1.1 collective-permute-start.1
  120.3 1.7 collective-permute-start.3
  121.9 1.3 collective-permute-start.2
  123.3 7.4 %collective-permute-done.1 = bf16[128,896]{0,1:T(8,128)(2,1)S(1)} collective-permute-done((bf16[128,896]{0,1:T(8,128)(2,1)S(1)}, bf16[128,896]{0,1:T(8,128)(2,1)S(1)}, u32[]{:S(2)}, u32[]{:S(2)}) %collective-permute-start.1) | collective-permute-done | bytes 229408 | tf_op jit(solution)/shard_map/ppermute | solution.py:66
  130.7 7.5 %collective-permute-done.2 = bf16[128,896]{0,1:T(8,128)(2,1)S(1)} collective-permute-done((bf16[128,896]{0,1:T(8,128)(2,1)S(1)}, bf16[128,896]{0,1:T(8,128)(2,1)S(1)}, u32[]{:S(2)}, u32[]{:S(2)}) %collective-permute-start.2) | collective-permute-done | bytes 229408 | tf_op jit(solution)/shard_map/ppermute | solution.py:66
  138.3 1.1 fusion.8
  139.4 0.2 multiply_convert_fusion.1
  139.7 0.8 pad_maximum_fusion.5
  140.5 5.8 %convolution_convert_fusion = bf16[1024,1024]{1,0:T(8,128)(2,1)} fusion(bf16[1024,896]{0,1:T(8,128)(2,1)} %all-gather.3.cloned.1.call-done, bf16[896,1024]{1,0:T(8,128)(2,1)} %param.15, pred[112,8,8,128]{3,2,1,0:T(8,128)(4,1)S(1)} %bitcast.72), kind=kOutput, calls=%fused_computation.13 | convolution fusion | flops 1881014272 | bytes 6684672 | tf_op jit(solution)/shard_map/dot_general | solution.py:117
  146.3 7.7 %all-to-all-start.2 = ((bf16[16,64,1024]{2,1,0:T(8,128)(2,1)}), bf16[16,64,1024]{2,1,0:T(8,128)(2,1)S(1)}, u32[]{:S(2)}, u32[]{:S(2)}) async-start(bf16[16,64,1024]{2,1,0:T(8,128)(2,1)} %bitcast.68), calls=%async_computation.3 | async-start | bytes 4194304 | tf_op jit(solution)/shard_map/all_to_all | solution.py:81
  154.1 23.3 %all-gather.5.cloned.1.call-done = bf16[1024,1792]{0,1:T(8,128)(2,1)} async-done(((bf16[128,1792]{0,1:T(8,128)(2,1)}), bf16[1024,1792]{0,1:T(8,128)(2,1)}) %all-gather.5.cloned.1.call-update) | async-done | bytes 3670032 | tf_op jit(solution)/shard_map/all_gather | solution.py:38
  177.4 8.5 %fusion.3 = bf16[1024,1024]{1,0:T(8,128)(2,1)} fusion(bf16[1024,1792]{0,1:T(8,128)(2,1)} %all-gather.5.cloned.1.call-done, bf16[1024,896]{0,1:T(8,128)(2,1)} %get-tuple-element.69, bf16[1024,896]{0,1:T(8,128)(2,1)} %get-tuple-element.70), kind=kOutput, calls=%fused_computation.12 | convolution fusion | flops 3766484992 | bytes 9437184 | tf_op jit(solution)/shard_map/dot_general | solution.py:134
  185.9 0.8 all-to-all-done.2
  186.7 1.3 copy-done
  188.0 5.9 %all-to-all-start.3 = ((bf16[16,64,1024]{2,1,0:T(8,128)(2,1)}), bf16[16,64,1024]{2,1,0:T(8,128)(2,1)S(1)}, u32[]{:S(2)}, u32[]{:S(2)}) async-start(bf16[16,64,1024]{2,1,0:T(8,128)(2,1)} %bitcast.67), calls=%async_computation.4 | async-start | bytes 4194304 | tf_op jit(solution)/shard_map/all_to_all | solution.py:81
  193.9 5.5 %select_convert_fusion = bf16[896,1024]{1,0:T(8,128)(2,1)} fusion(pred[112,8,8,128]{3,2,1,0:T(8,128)(4,1)S(1)} %bitcast.73, bf16[1024,896]{0,1:T(8,128)(2,1)} %all-gather.3.cloned.1.call-done, bf16[1024,1024]{1,0:T(8,128)(2,1)} %bitcast.66), kind=kOutput, calls=%fused_computation.9 | convolution fusion | flops 1880883200 | bytes 6684672 | tf_op jit(solution)/shard_map/dot_general | solution.py:120
  199.4 2.7 %reduce_sum.24 = bf16[64,1024]{1,0:T(8,128)(2,1)} reduce(bf16[16,64,1024]{2,1,0:T(8,128)(2,1)} %copy-done, bf16[]{:T(256)} %constant.84.clone.1), dimensions={0}, to_apply=%region_1.2 | reduce | flops 983040 | bytes 2228226 | tf_op jit(solution)/shard_map/reduce_sum | solution.py:82
  202.1 6.7 %convolution_bitcast_fusion = bf16[1024,1792]{0,1:T(8,128)(2,1)S(1)} fusion(bf16[1024,1792]{0,1:T(8,128)(2,1)} %all-gather.5.cloned.1.call-done, bf16[1024,1024]{1,0:T(8,128)(2,1)} %bitcast.2), kind=kOutput, calls=%fused_computation.4 | convolution fusion | flops 3758096384 | bytes 9437184 | tf_op jit(solution)/shard_map/dot_general | solution.py:126
  208.7 3.0 %fusion.1 = (bf16[1024,896]{0,1:T(8,128)(2,1)}, bf16[1024,896]{0,1:T(8,128)(2,1)}) fusion(bf16[1024,1792]{0,1:T(8,128)(2,1)S(1)} %convolution_bitcast_fusion, pred[1024,7]{0,1:T(8,128)(4,1)S(1)} %bitcast.76, pred[1024,7]{0,1:T(8,128)(4,1)S(1)} %bitcast.78), kind=kLoop, calls=%fused_computation.7 | loop fusion | flops 1835008 | bytes 7354368 | tf_op jit(solution)/shard_map/convert_element_type | solution.py:131
  211.7 3.8 %copy.26 = bf16[1024,896]{1,0:T(8,128)(2,1)} copy(bf16[1024,896]{0,1:T(8,128)(2,1)} %get-tuple-element.62) | data formatting | bytes 3670016
  215.5 3.8 %copy.25 = bf16[1024,896]{1,0:T(8,128)(2,1)} copy(bf16[1024,896]{0,1:T(8,128)(2,1)} %get-tuple-element.63) | data formatting | bytes 3670016
  219.3 7.2 %all-to-all-done.3 = bf16[16,64,1024]{2,1,0:T(8,128)(2,1)S(1)} async-done(((bf16[16,64,1024]{2,1,0:T(8,128)(2,1)}), bf16[16,64,1024]{2,1,0:T(8,128)(2,1)S(1)}, u32[]{:S(2)}, u32[]{:S(2)}) %all-to-all-start.3) | async-done | bytes 2097184 | tf_op jit(solution)/shard_map/all_to_all | solution.py:81
  226.5 1.1 reduce_sum.25
  (29 shorter events, 0.4 us)
Async XLA Ops:
  9.7 8.8 %copy-start.4 = (s32[8,7]{1,0:T(8,128)S(1)}, s32[8,7]{1,0:T(8,128)}, u32[]{:S(2)}) copy-start(s32[8,7]{1,0:T(8,128)} %param.16) | copy-start | bytes 676
  9.7 8.9 %copy-start.5 = (s32[8,7]{1,0:T(8,128)S(1)}, s32[8,7]{1,0:T(8,128)}, u32[]{:S(2)}) copy-start(s32[8,7]{1,0:T(8,128)} %param.17) | copy-start | bytes 676
  9.7 39.8 %all-to-all-start = ((bf16[16,64,1024]{2,1,0:T(8,128)(2,1)}), bf16[16,64,1024]{2,1,0:T(8,128)(2,1)}, u32[]{:S(2)}, u32[]{:S(2)}) async-start(bf16[16,64,1024]{2,1,0:T(8,128)(2,1)} %broadcast_in_dim.83), calls=%async_computation | async-start | bytes 4194304 | tf_op jit(solution)/shard_map/all_to_all | solution.py:88
  18.5 86.7 %reduce-scatter.2.cloned.1.call-start = ((), (), s32[]{:S(2)}) async-start(), calls=%async_computation.5 | async-start | bytes 8257536 | tf_op jit(solution)/shard_map/reduce_scatter | solution.py:32
  59.1 0.9 copy-start.3
  61.7 4.0 %copy-start.6 = (s32[7,8]{1,0:T(8,128)S(1)}, s32[7,8]{1,0:T(8,128)}, u32[]{:S(2)}) copy-start(s32[7,8]{1,0:T(8,128)} %param.18) | copy-start | bytes 676
  61.7 32.6 %all-to-all-start.1 = ((bf16[16,64,1024]{2,1,0:T(8,128)(2,1)}), bf16[16,64,1024]{2,1,0:T(8,128)(2,1)S(1)}, u32[]{:S(2)}, u32[]{:S(2)}) async-start(bf16[16,64,1024]{2,1,0:T(8,128)(2,1)} %broadcast_in_dim.84), calls=%async_computation.2 | async-start | bytes 4194304 | tf_op jit(solution)/shard_map/all_to_all | solution.py:88
  65.6 73.8 %all-gather.3.cloned.1.call-start = ((), (), s32[]{:S(2)}) async-start(), calls=%async_computation.6 | async-start | bytes 2064384 | tf_op jit(solution)/shard_map/all_gather | solution.py:38
  94.2 8.7 %copy-start.2 = (bf16[16,64,1024]{2,1,0:T(8,128)(2,1)}, bf16[16,64,1024]{2,1,0:T(8,128)(2,1)S(1)}, u32[]{:S(2)}) copy-start(bf16[16,64,1024]{2,1,0:T(8,128)(2,1)S(1)} %all-to-all-done.1) | copy-start | bytes 6291460
  107.1 70.3 %all-gather.5.cloned.1.call-start = ((), (), s32[]{:S(2)}) async-start(), calls=%async_computation.7 | async-start | bytes 4128768 | tf_op jit(solution)/shard_map/all_gather | solution.py:38
  110.6 5.9 %collective-permute-start = (bf16[4,128,896]{1,2,0:T(8,128)(2,1)}, bf16[4,128,896]{1,2,0:T(8,128)(2,1)}, u32[]{:S(2)}, u32[]{:S(2)}) collective-permute-start(bf16[4,128,896]{1,2,0:T(8,128)(2,1)} %bitcast_convert_fusion), channel_id=1, source_target_pairs={{0,16},{16,0},{32,48},{48,32},{64,80},{80,64},{96,112},{112,96},{1... | collective-permute-start | bytes 2752520 | tf_op jit(solution)/shard_map/ppermute | solution.py:60
  119.1 20.3 %copy-start.1 = (f32[128,1792]{0,1:T(8,128)S(1)}, f32[128,1792]{0,1:T(8,128)}, u32[]{:S(2)}) copy-start(f32[128,1792]{0,1:T(8,128)} %reduce-scatter.2.cloned.1.call-done) | copy-start | bytes 2752516
  119.2 11.5 %collective-permute-start.1 = (bf16[128,896]{0,1:T(8,128)(2,1)S(1)}, bf16[128,896]{0,1:T(8,128)(2,1)S(1)}, u32[]{:S(2)}, u32[]{:S(2)}) collective-permute-start(bf16[128,896]{0,1:T(8,128)(2,1)S(1)} %get-tuple-element.66), channel_id=1, source_target_pairs={{0,32},{16,48},{32,64},{48,80},{64,96},{80,112},{96,0},{112,16},{1... | collective-permute-start | bytes 688136 | tf_op jit(solution)/shard_map/ppermute | solution.py:66
  120.3 10.4 %collective-permute-start.3 = (bf16[128,896]{0,1:T(8,128)(2,1)S(1)}, bf16[128,896]{0,1:T(8,128)(2,1)S(1)}, u32[]{:S(2)}, u32[]{:S(2)}) collective-permute-start(bf16[128,896]{0,1:T(8,128)(2,1)S(1)} %get-tuple-element.67), channel_id=1, source_target_pairs={{0,96},{16,112},{32,0},{48,16},{64,32},{80,48},{96,64},{112,80},{1... | collective-permute-start | bytes 688136 | tf_op jit(solution)/shard_map/ppermute | solution.py:66
  121.9 16.3 %collective-permute-start.2 = (bf16[128,896]{0,1:T(8,128)(2,1)S(1)}, bf16[128,896]{0,1:T(8,128)(2,1)S(1)}, u32[]{:S(2)}, u32[]{:S(2)}) collective-permute-start(bf16[128,896]{0,1:T(8,128)(2,1)S(1)} %get-tuple-element.68), channel_id=1, source_target_pairs={{0,64},{16,80},{32,96},{48,112},{64,0},{80,16},{96,32},{112,48},{1... | collective-permute-start | bytes 688136 | tf_op jit(solution)/shard_map/ppermute | solution.py:66
  146.3 40.4 %all-to-all-start.2 = ((bf16[16,64,1024]{2,1,0:T(8,128)(2,1)}), bf16[16,64,1024]{2,1,0:T(8,128)(2,1)S(1)}, u32[]{:S(2)}, u32[]{:S(2)}) async-start(bf16[16,64,1024]{2,1,0:T(8,128)(2,1)} %bitcast.68), calls=%async_computation.3 | async-start | bytes 4194304 | tf_op jit(solution)/shard_map/all_to_all | solution.py:81
  186.7 1.3 copy-start
  188.0 38.5 %all-to-all-start.3 = ((bf16[16,64,1024]{2,1,0:T(8,128)(2,1)}), bf16[16,64,1024]{2,1,0:T(8,128)(2,1)S(1)}, u32[]{:S(2)}, u32[]{:S(2)}) async-start(bf16[16,64,1024]{2,1,0:T(8,128)(2,1)} %bitcast.67), calls=%async_computation.4 | async-start | bytes 4194304 | tf_op jit(solution)/shard_map/all_to_all | solution.py:81
Sparse Core Ops, SparseCore 0:
  59.3 45.7 reduce-scatter.1
  107.2 32.0 all-gather.2
  141.6 35.6 all-gather.4
